TPU v7x, 128 devices: a whole 4x4x4 slice. The times are simulated.
128 devices in a mesh: dp: 32 (over x_lo, z, y), mp: 4 (over x_hi, core).
Axes of the slice: x: 4 (x_hi: 2, x_lo: 2; x = x_hi * 2 + x_lo), y: 4, z: 4, core: 2. Of those that a mesh axis runs over, the one named last changes fastest.
Arguments:
- samples: bfloat16 [24576, 8192], P('dp', 'mp'), may hold values from -6 to 6
- gain: float32 [8192], P('mp'), may hold values from 0.1 to 1.9
- left_blocks: bfloat16 [64, 128, 128], P('mp'), may hold values from -0.5 to 0.5
- gate_blocks: bfloat16 [64, 128, 128], P('mp'), may hold values from -0.5 to 0.5
- right_blocks: bfloat16 [64, 128, 128], P('mp'), may hold values from -0.5 to 0.5
- cotangent: bfloat16 [24576, 8192], P('dp', 'mp'), may hold values from -6 to 6
Outputs:
- grad_input: bfloat16 [24576, 8192], P('dp', 'mp')
- grad_left: float32 [64, 128, 128], P('mp')
- grad_gate: float32 [64, 128, 128], P('mp')
- grad_right: float32 [64, 128, 128], P('mp')
All inputs are finite; a program needn't handle non-finite values.
Results may differ from a plain program's by a relative error of at most 0.007.
Values may be sent and summed in bfloat16 or wider, within the bound.
No kernel may reach another device: no remote copies, remote signals or barrier semaphores. Data moves between devices by JAX's collectives and lax.ppermute only.
A program may use at most 128 MiB of HBM per device.

v0:
```python
import jax
import jax.numpy as jnp
from jax import lax
from jax.sharding import PartitionSpec as P

W = 8192
BLOCK = 128
NBLK = 64


def dp_reduce_scatter(parts):
    ndp = lax.axis_size("dp")
    flat = jnp.concatenate([p.reshape(-1, BLOCK) for p in parts]).reshape(ndp, -1, BLOCK)
    got = lax.all_to_all(flat, "dp", 0, 0, tiled=True)
    return jnp.sum(got, axis=0)


def dp_all_gather(mine, shapes):
    ndp = lax.axis_size("dp")
    copies = jnp.broadcast_to(mine.astype(jnp.bfloat16)[None], (ndp,) + mine.shape)
    whole = lax.all_to_all(copies, "dp", 0, 0, tiled=True).reshape(-1, BLOCK, BLOCK)
    out, at = [], 0
    for shape in shapes:
        out.append(whole[at:at + shape[0]].astype(jnp.float32))
        at += shape[0]
    return tuple(out)


def pair_major(blocks):
    n, c, _ = blocks.shape
    return blocks.reshape(n, c, NBLK, 2).transpose(0, 1, 3, 2).reshape(n, c, 2 * NBLK)


def pair_minor(blocks):
    n, c, _ = blocks.shape
    return blocks.reshape(n, c, 2, NBLK).transpose(0, 1, 3, 2).reshape(n, c, 2 * NBLK)


def body(samples, gain, left_blocks, gate_blocks, right_blocks, cotangent):
    rows, width_local = samples.shape
    nlocal = left_blocks.shape[0]
    xf = samples.astype(jnp.float32)
    cot_blocks = cotangent.reshape(rows, nlocal, BLOCK)
    grad_perm = jnp.einsum(
        "tkm,kcm->tkc", cot_blocks, right_blocks, preferred_element_type=jnp.float32
    ).astype(jnp.bfloat16)
    squares = lax.psum(jnp.sum(xf * xf, axis=1), "mp")
    grad_perm, squares = lax.optimization_barrier((grad_perm, squares))
    rstd = lax.rsqrt(squares / W + 1e-05)[:, None]
    xn = (xf * rstd * gain).astype(jnp.bfloat16).reshape(rows, nlocal, BLOCK)
    left_p = pair_major(left_blocks)
    gate_p = pair_major(gate_blocks)
    act_a = jnp.einsum("tic,icj->tij", xn, left_p, preferred_element_type=jnp.float32)
    act_g = jnp.einsum("tic,icj->tij", xn, gate_p, preferred_element_type=jnp.float32)
    gated = (act_a * jax.nn.silu(act_g)).astype(jnp.bfloat16)
    outgoing = (
        gated.reshape(rows, nlocal, 2, NBLK).transpose(0, 3, 1, 2).reshape(rows, NBLK, 2 * nlocal)
    )
    returned = lax.all_to_all(grad_perm, "mp", split_axis=2, concat_axis=1, tiled=True)
    outgoing, xn_b = lax.optimization_barrier((outgoing, xn))
    permuted = lax.all_to_all(outgoing, "mp", split_axis=1, concat_axis=2, tiled=True)
    right_local = jnp.einsum(
        "tkc,tkm->kcm", permuted, cot_blocks, preferred_element_type=jnp.float32
    )
    act_a = jnp.einsum("tic,icj->tij", xn_b, left_p, preferred_element_type=jnp.float32)
    act_g = jnp.einsum("tic,icj->tij", xn_b, gate_p, preferred_element_type=jnp.float32)
    silu_g = jax.nn.silu(act_g)
    grad_gated = (
        returned.reshape(rows, NBLK, nlocal, 2)
        .transpose(0, 2, 3, 1)
        .reshape(rows, nlocal, BLOCK)
        .astype(jnp.float32)
    )
    sigma = jax.nn.sigmoid(act_g)
    grad_a = (grad_gated * silu_g).astype(jnp.bfloat16)
    grad_g = (grad_gated * act_a * sigma * (1.0 + act_g * (1.0 - sigma))).astype(jnp.bfloat16)
    left_local = pair_minor(jnp.einsum("tic,tij->icj", xn_b, grad_a, preferred_element_type=jnp.float32))
    gate_local = pair_minor(jnp.einsum("tic,tij->icj", xn_b, grad_g, preferred_element_type=jnp.float32))
    grad_norm = jnp.einsum("tij,icj->tic", grad_a, left_p, preferred_element_type=jnp.float32)
    grad_norm = grad_norm + jnp.einsum(
        "tij,icj->tic", grad_g, gate_p, preferred_element_type=jnp.float32
    )
    partials = (left_local, gate_local, right_local)
    mine = dp_reduce_scatter(partials)
    scaled = grad_norm.reshape(rows, width_local) * gain
    mine, scaled = lax.optimization_barrier((mine, scaled))
    inner = lax.psum(jnp.sum(scaled * xf, axis=1), "mp")
    mean_inner = (inner / W)[:, None]
    grad_input = (
        cotangent.astype(jnp.float32) + rstd * (scaled - xf * rstd * rstd * mean_inner)
    ).astype(jnp.bfloat16)
    left_total, gate_total, right_total = dp_all_gather(mine, [p.shape for p in partials])
    return (grad_input, left_total, gate_total, right_total)


def solution(mesh):
    placed = (
        P("dp", "mp"),
        P("mp"),
        P("mp", None, None),
        P("mp", None, None),
        P("mp", None, None),
        P("dp", "mp"),
    )
    return jax.shard_map(
        body,
        mesh=mesh,
        in_specs=placed,
        out_specs=(P("dp", "mp"), P("mp", None, None), P("mp", None, None), P("mp", None, None)),
        check_vma=False,
    )
```

profile of v0, /device:TPU:6, one launch (start us, length us, event | category | flops | bytes accessed | tf_op | source)
XLA Modules:
  0.0 228.0 jit_solution(13866291150214589768)
XLA Ops:
  3.3 8.3 %psum.14 = f32[768]{0:T(1024)S(1)} all-reduce(f32[768]{0:T(1024)S(1)} %fusion.8), channel_id=1, replica_groups=mesh['dp'=32,'mp'=4] {'mp'}, use_global_device_ids=true, to_apply=%region_1.0 | all-reduce | flops 768 | bytes 6144 | tf_op jit(solution)/shard_map/psum | solution.py:47
  11.6 2.9 %convert_bitcast_fusion.1 = bf16[768,16,128]{0,2,1:T(8,128)(2,1)S(1)} fusion(bf16[16,128,128]{2,1,0:T(8,128)(2,1)S(1)} %copy-done, bf16[768,2048]{1,0:T(8,128)(2,1)} %param.11), kind=kOutput, calls=%fused_computation.44 | convolution fusion | flops 404226048 | bytes 6815744 | tf_op jit(solution)/shard_map/tkm,kcm->tkc/dot_general | solution.py:44
  14.5 3.4 %copy.118 = bf16[768,16,128]{0,1,2:T(8,128)(2,1)} copy(bf16[768,16,128]{0,2,1:T(8,128)(2,1)S(1)} %convert_bitcast_fusion.1) | data formatting | bytes 6291456 | tf_op jit(solution)/shard_map/optimization_barrier | solution.py:48
  17.9 6.9 %all-to-all-start = ((bf16[768,16,128]{0,1,2:T(8,128)(2,1)}), bf16[768,16,128]{0,1,2:T(8,128)(2,1)}, u32[]{:S(2)}, u32[]{:S(2)}) async-start(bf16[768,16,128]{0,1,2:T(8,128)(2,1)} %copy.118), calls=%async_computation | async-start | bytes 6291456 | tf_op jit(solution)/shard_map/all_to_all | solution.py:59
  26.1 2.8 %fusion.48 = (bf16[96,8,16,128]{3,1,2,0:T(8,128)(2,1)S(1)}, bf16[96,16,8,128]{3,2,1,0:T(8,128)(2,1)S(1)}) fusion(f32[2048]{0:T(1024)S(1)} %copy-done.10, f32[768]{0:T(1024)S(1)} %add_rsqrt_fusion, bf16[768,2048]{1,0:T(8,128)(2,1)} %param.6), kind=kLoop, calls=%fused_computation.60 | loop fusion | flops 6291456 | bytes 9448448
  34.8 3.4 %copy.148 = bf16[768,64,32]{0,2,1:T(8,128)(2,1)} copy(bf16[768,64,32]{0,1,2:T(8,128)(2,1)S(1)} %bitcast.154) | data formatting | bytes 6291456 | tf_op jit(solution)/shard_map/reshape | solution.py:57
  38.2 21.9 %all-to-all-done = bf16[768,16,128]{0,1,2:T(8,128)(2,1)} async-done(((bf16[768,16,128]{0,1,2:T(8,128)(2,1)}), bf16[768,16,128]{0,1,2:T(8,128)(2,1)}, u32[]{:S(2)}, u32[]{:S(2)}) %all-to-all-start) | async-done | bytes 3145760 | tf_op jit(solution)/shard_map/all_to_all | solution.py:59
  60.1 7.8 %all-to-all-start.1 = ((bf16[768,64,32]{0,2,1:T(8,128)(2,1)}), bf16[768,64,32]{0,2,1:T(8,128)(2,1)}, u32[]{:S(2)}, u32[]{:S(2)}) async-start(bf16[768,64,32]{0,2,1:T(8,128)(2,1)} %copy.148), calls=%async_computation.1 | async-start | bytes 6291456 | tf_op jit(solution)/shard_map/all_to_all | solution.py:61
  67.9 2.9 %copy.119 = bf16[768,16,128]{0,2,1:T(8,128)(2,1)S(1)} copy(bf16[768,16,128]{0,1,2:T(8,128)(2,1)} %all-to-all-done) | data formatting | bytes 6291456 | tf_op jit(solution)/shard_map/all_to_all | solution.py:59
  71.7 6.3 %copy.120 = f32[768,4,16,32]{0,2,1,3:T(8,128)} copy(f32[768,4,16,32]{0,3,1,2:T(8,128)S(1)} %convert_bitcast_fusion) | data formatting | bytes 12582912 | tf_op jit(solution)/shard_map/convert_element_type | solution.py:72
  78.0 25.3 %all-to-all-done.1 = bf16[768,64,32]{0,2,1:T(8,128)(2,1)} async-done(((bf16[768,64,32]{0,2,1:T(8,128)(2,1)}), bf16[768,64,32]{0,2,1:T(8,128)(2,1)}, u32[]{:S(2)}, u32[]{:S(2)}) %all-to-all-start.1) | async-done | bytes 3145760 | tf_op jit(solution)/shard_map/all_to_all | solution.py:61
  110.8 9.2 %fusion.17 = (bf16[768,16,128]{0,2,1:T(8,128)(2,1)S(1)}, f32[16,768,128]{1,2,0:T(8,128)}) fusion(f32[768,16,128]{0,2,1:T(8,128)} %bitcast.140, bf16[16,128,128]{1,2,0:T(8,128)(2,1)S(1)} %bitcast.146, bf16[768,16,128]{2,1,0:T(8,128)(2,1)} %bitcast.150), kind=kOutput, calls=%fused_computation.25 | convolution fusion | flops 412090368 | bytes 19398656 | tf_op jit(solution)/shard_map/tic,icj->tij/dot_general | solution.py:66
  120.0 6.9 %fusion.12 = bf16[768,16,128]{0,2,1:T(8,128)(2,1)S(1)} fusion(f32[768,16,128]{0,2,1:T(8,128)S(1)} %bitcast.143, f32[16,768,128]{1,2,0:T(8,128)} %get-tuple-element.22, bf16[16,128,128]{1,2,0:T(8,128)(2,1)S(1)} %bitcast.157, bf16[768,16,128]{2,1,0:T(8,128)(2,1)S(1)} %bitcast.151), kind=kOutput, calls=%fused_computation.17 | convolution fusion | flops 418381824 | bytes 19398656 | tf_op jit(solution)/shard_map/tic,icj->tij/dot_general | solution.py:65
  134.9 3.5 %copy.134 = f32[6144,128]{1,0:T(8,128)} copy(f32[6144,128]{0,1:T(8,128)} %pad_maximum_fusion) | data formatting | bytes 6291456 | tf_op jit(solution)/shard_map/concatenate | solution.py:13
  138.5 9.6 %all-to-all-start.2 = ((f32[32,192,128]{2,1,0:T(8,128)}), f32[32,192,128]{2,1,0:T(8,128)}, u32[]{:S(2)}, u32[]{:S(2)}) async-start(f32[32,192,128]{2,1,0:T(8,128)} %bitcast.138), calls=%async_computation.2 | async-start | bytes 6291456 | tf_op jit(solution)/shard_map/all_to_all | solution.py:14
  148.1 3.1 %fusion.49 = f32[16,768,128]{1,2,0:T(8,128)S(1)} fusion(bf16[768,16,128]{0,2,1:T(8,128)(2,1)} %copy-done.4, bf16[16,128,128]{1,2,0:T(8,128)(2,1)S(1)} %bitcast.158), kind=kOutput, calls=%fused_computation.66 | convolution fusion | flops 402653184 | bytes 9961472 | tf_op jit(solution)/shard_map/tij,icj->tic/dot_general | solution.py:79
  151.2 3.7 %convolution_add_fusion = f32[16,768,128]{1,2,0:T(8,128)} fusion(f32[16,768,128]{1,2,0:T(8,128)S(1)} %fusion.49, bf16[768,16,128]{0,2,1:T(8,128)(2,1)S(1)} %copy-done.7, bf16[16,128,128]{1,2,0:T(8,128)(2,1)S(1)} %bitcast.147), kind=kOutput, calls=%fused_computation.49 | convolution fusion | flops 404226048 | bytes 16252928 | tf_op jit(solution)/shard_map/tij,icj->tic/dot_general | solution.py:80
  154.9 6.6 %copy.139 = f32[768,2048]{1,0:T(8,128)} copy(f32[768,2048]{0,1:T(8,128)} %bitcast.137) | data formatting | bytes 12582912 | tf_op jit(solution)/shard_map/reshape | solution.py:85
  161.5 6.6 %broadcast_multiply_fusion = f32[768,2048]{1,0:T(8,128)} fusion(f32[768,2048]{1,0:T(8,128)} %copy.139, f32[2048]{0:T(1024)S(1)} %copy-done.10), kind=kLoop, calls=%fused_computation.43 | loop fusion | flops 1572864 | bytes 12591104 | tf_op jit(solution)/shard_map/mul | solution.py:85
  168.1 20.9 %all-to-all-done.2 = f32[32,192,128]{2,1,0:T(8,128)} async-done(((f32[32,192,128]{2,1,0:T(8,128)}), f32[32,192,128]{2,1,0:T(8,128)}, u32[]{:S(2)}, u32[]{:S(2)}) %all-to-all-start.2) | async-done | bytes 3145760 | tf_op jit(solution)/shard_map/all_to_all | solution.py:14
  192.5 5.4 %all-to-all-start.3 = ((bf16[32,192,128]{2,1,0:T(8,128)(2,1)}), bf16[32,192,128]{2,1,0:T(8,128)(2,1)S(1)}, u32[]{:S(2)}, u32[]{:S(2)}) async-start(bf16[32,192,128]{2,1,0:T(8,128)(2,1)} %broadcast_in_dim.2), calls=%async_computation.3 | async-start | bytes 3145728 | tf_op jit(solution)/shard_map/all_to_all | solution.py:21
  197.9 4.4 %fusion.9 = f32[768]{0:T(1024)S(1)} fusion(f32[768,2048]{1,0:T(8,128)} %broadcast_multiply_fusion, bf16[768,2048]{1,0:T(8,128)(2,1)} %param.6), kind=kLoop, calls=%fused_computation.12 | loop fusion | flops 4717824 | bytes 9440256 | tf_op jit(solution)/shard_map/reduce_sum | solution.py:87
  202.3 17.1 %psum.15 = f32[768]{0:T(1024)S(1)} all-reduce(f32[768]{0:T(1024)S(1)} %fusion.9), channel_id=1, replica_groups=mesh['dp'=32,'mp'=4] {'mp'}, use_global_device_ids=true, to_apply=%region_4.5 | all-reduce | flops 768 | bytes 6144 | tf_op jit(solution)/shard_map/psum | solution.py:87
  219.4 6.8 %fusion.7 = bf16[768,2048]{1,0:T(8,128)(2,1)} fusion(f32[768,2048]{1,0:T(8,128)} %broadcast_multiply_fusion, bf16[768,2048]{1,0:T(8,128)(2,1)} %param.6, bf16[768,2048]{1,0:T(8,128)(2,1)} %param.11, f32[768]{0:T(1024)S(1)} %broadcast_multiply_fusion.1, f32[768]{0:T(1024)S(1)} %add_rsqrt_fusion), kind=kLoop, calls=%fused_computation.10 | loop fusion | flops 14155776 | bytes 15734784 | tf_op jit(solution)/shard_map/convert_element_type | solution.py:91
  (51 shorter events, 31.4 us)
Async XLA Ops:
  0.6 11.0 %copy-start = (bf16[16,128,128]{2,1,0:T(8,128)(2,1)S(1)}, bf16[16,128,128]{2,1,0:T(8,128)(2,1)}, u32[]{:S(2)}) copy-start(bf16[16,128,128]{2,1,0:T(8,128)(2,1)} %param.10) | copy-start | bytes 1572868
  17.9 6.9 %copy-start.8 = (bf16[16,128,128]{2,1,0:T(8,128)(2,1)S(1)}, bf16[16,128,128]{2,1,0:T(8,128)(2,1)}, u32[]{:S(2)}) copy-start(bf16[16,128,128]{2,1,0:T(8,128)(2,1)} %param.8) | copy-start | bytes 1572868
  17.9 7.5 %copy-start.9 = (bf16[16,128,128]{2,1,0:T(8,128)(2,1)S(1)}, bf16[16,128,128]{2,1,0:T(8,128)(2,1)}, u32[]{:S(2)}) copy-start(bf16[16,128,128]{2,1,0:T(8,128)(2,1)} %param.9) | copy-start | bytes 1572868
  17.9 42.2 %all-to-all-start = ((bf16[768,16,128]{0,1,2:T(8,128)(2,1)}), bf16[768,16,128]{0,1,2:T(8,128)(2,1)}, u32[]{:S(2)}, u32[]{:S(2)}) async-start(bf16[768,16,128]{0,1,2:T(8,128)(2,1)} %copy.118), calls=%async_computation | async-start | bytes 6291456 | tf_op jit(solution)/shard_map/all_to_all | solution.py:59
  24.8 1.3 copy-start.10
  60.1 43.2 %all-to-all-start.1 = ((bf16[768,64,32]{0,2,1:T(8,128)(2,1)}), bf16[768,64,32]{0,2,1:T(8,128)(2,1)}, u32[]{:S(2)}, u32[]{:S(2)}) async-start(bf16[768,64,32]{0,2,1:T(8,128)(2,1)} %copy.148), calls=%async_computation.1 | async-start | bytes 6291456 | tf_op jit(solution)/shard_map/all_to_all | solution.py:61
  103.3 2.8 %copy-start.2 = (bf16[768,2048]{1,0:T(8,128)(2,1)S(1)}, bf16[768,2048]{1,0:T(8,128)(2,1)}, u32[]{:S(2)}) copy-start(bf16[768,2048]{1,0:T(8,128)(2,1)} %param.11) | copy-start | bytes 9437188
  108.1 11.9 %slice-start = ((s8[6291456]{0:T(1024)(128)(4,1)}), s8[2097152]{0:T(1024)(128)(4,1)S(1)}, s32[]{:S(2)}) async-start(s8[6291456]{0:T(1024)(128)(4,1)} %bitcast.141), calls=%async_computation.4 | async-start | bytes 4194304
  110.8 9.2 %slice-start.1 = ((s8[6291456]{0:T(1024)(128)(4,1)}), s8[4194304]{0:T(1024)(128)(4,1)S(1)}, s32[]{:S(2)}) async-start(s8[6291456]{0:T(1024)(128)(4,1)} %bitcast.141), calls=%async_computation.5 | async-start | bytes 8388608
  110.8 9.2 %copy-start.5 = (bf16[96,8,16,128]{3,2,1,0:T(8,128)(2,1)S(1)}, bf16[96,8,16,128]{3,2,1,0:T(8,128)(2,1)}, u32[]{:S(2)}) copy-start(bf16[96,8,16,128]{3,2,1,0:T(8,128)(2,1)} %copy.151) | copy-start | bytes 9437188
  120.0 9.0 %copy-start.4 = (bf16[768,16,128]{0,2,1:T(8,128)(2,1)}, bf16[768,16,128]{0,2,1:T(8,128)(2,1)S(1)}, u32[]{:S(2)}) copy-start(bf16[768,16,128]{0,2,1:T(8,128)(2,1)S(1)} %get-tuple-element.21) | copy-start | bytes 9437188
  127.0 2.0 copy-start.6
  131.4 1.5 copy-start.3
  138.5 50.5 %all-to-all-start.2 = ((f32[32,192,128]{2,1,0:T(8,128)}), f32[32,192,128]{2,1,0:T(8,128)}, u32[]{:S(2)}, u32[]{:S(2)}) async-start(f32[32,192,128]{2,1,0:T(8,128)} %bitcast.138), calls=%async_computation.2 | async-start | bytes 6291456 | tf_op jit(solution)/shard_map/all_to_all | solution.py:14
  148.1 3.1 %copy-start.7 = (bf16[768,16,128]{0,2,1:T(8,128)(2,1)S(1)}, bf16[768,16,128]{0,2,1:T(8,128)(2,1)}, u32[]{:S(2)}) copy-start(bf16[768,16,128]{0,2,1:T(8,128)(2,1)} %copy-done.6) | copy-start | bytes 9437188
  192.5 33.7 %all-to-all-start.3 = ((bf16[32,192,128]{2,1,0:T(8,128)(2,1)}), bf16[32,192,128]{2,1,0:T(8,128)(2,1)S(1)}, u32[]{:S(2)}, u32[]{:S(2)}) async-start(bf16[32,192,128]{2,1,0:T(8,128)(2,1)} %broadcast_in_dim.2), calls=%async_computation.3 | async-start | bytes 3145728 | tf_op jit(solution)/shard_map/all_to_all | solution.py:21
  219.4 8.6 %copy-start.1 = (bf16[16,128,128]{2,1,0:T(8,128)(2,1)S(1)}, bf16[16,128,128]{2,1,0:T(8,128)(2,1)}, u32[]{:S(2)}) copy-start(bf16[16,128,128]{2,1,0:T(8,128)(2,1)} %param.10) | copy-start | bytes 1572868
where the time goes:
time: 230 us; the launch traced here: 228 us
  waiting for transfers between devices  68.1 us (30%)
  local copies, waits for them, and re-layouts  39.3 us (17%)
  matrix products  34.7 us (15%)
  other arithmetic  29.8 us (13%)
  starting transfers between devices  29.7 us (13%)
  blocking collectives  25.4 us (11%)
    all_to_all x1, waiting for transfers between devices, body(): lax.all_to_all(outgoing, 'mp', split_axis=1, concat_axis=2, tiled=True)  25.3 us
    all_to_all x1, waiting for transfers between devices, body(): lax.all_to_all(grad_perm, 'mp', split_axis=2, concat_axis=1, tiled=True)  21.9 us
    all_to_all x1, waiting for transfers between devices, dp_reduce_scatter(): got = lax.all_to_all(flat, 'dp', 0, 0, tiled=True)  20.9 us
    psum x1, blocking collectives, body(): inner = lax.psum(jnp.sum(scaled * xf, axis=1), 'mp')  17.1 us
    all_to_all x1, starting transfers between devices, dp_reduce_scatter(): got = lax.all_to_all(flat, 'dp', 0, 0, tiled=True)  9.62 us
    dot_general x1, matrix products, body(): jnp.einsum('tic,icj->tij', xn_b, gate_p, preferred_element_type=jnp.float32)  9.2 us
    psum x1, blocking collectives, body(): squares = lax.psum(jnp.sum(xf * xf, axis=1), 'mp')  8.31 us
    all_to_all x1, starting transfers between devices, body(): lax.all_to_all(outgoing, 'mp', split_axis=1, concat_axis=2, tiled=True)  7.79 us
  transfers between devices with their start and end apart: 4, of which 3 were waited for; matrix products, arithmetic and copies ran while one was open for 24% of the time, Pallas kernels for 0%

commit v1 on v0

--- a/solution.py
+++ b/solution.py
@@ -59,9 +59,6 @@
     returned = lax.all_to_all(grad_perm, "mp", split_axis=2, concat_axis=1, tiled=True)
     outgoing, xn_b = lax.optimization_barrier((outgoing, xn))
     permuted = lax.all_to_all(outgoing, "mp", split_axis=1, concat_axis=2, tiled=True)
-    right_local = jnp.einsum(
-        "tkc,tkm->kcm", permuted, cot_blocks, preferred_element_type=jnp.float32
-    )
     act_a = jnp.einsum("tic,icj->tij", xn_b, left_p, preferred_element_type=jnp.float32)
     act_g = jnp.einsum("tic,icj->tij", xn_b, gate_p, preferred_element_type=jnp.float32)
     silu_g = jax.nn.silu(act_g)
@@ -80,15 +77,21 @@
     grad_norm = grad_norm + jnp.einsum(
         "tij,icj->tic", grad_g, gate_p, preferred_element_type=jnp.float32
     )
+    permuted, left_local, gate_local, grad_norm = lax.optimization_barrier(
+        (permuted, left_local, gate_local, grad_norm)
+    )
+    right_local = jnp.einsum(
+        "tkc,tkm->kcm", permuted, cot_blocks, preferred_element_type=jnp.float32
+    )
     partials = (left_local, gate_local, right_local)
     mine = dp_reduce_scatter(partials)
     scaled = grad_norm.reshape(rows, width_local) * gain
-    mine, scaled = lax.optimization_barrier((mine, scaled))
     inner = lax.psum(jnp.sum(scaled * xf, axis=1), "mp")
     mean_inner = (inner / W)[:, None]
     grad_input = (
         cotangent.astype(jnp.float32) + rstd * (scaled - xf * rstd * rstd * mean_inner)
     ).astype(jnp.bfloat16)
+    mine, grad_input = lax.optimization_barrier((mine, grad_input))
     left_total, gate_total, right_total = dp_all_gather(mine, [p.shape for p in partials])
     return (grad_input, left_total, gate_total, right_total)
 

time: 230 us -> 212 us (0.922)
  matrix products: 34.7 us -> 22.2 us
  waiting for transfers between devices: 68.1 us -> 55.6 us
  other arithmetic: 29.8 us -> 23.2 us
  blocking collectives: 25.4 us -> 32 us
  local copies, waits for them, and re-layouts: 39.3 us -> 44.3 us
  starting transfers between devices: 29.7 us -> 32.4 us
    all_to_all x1, waiting for transfers between devices: 20.9 us -> 0.01 us  [dp_reduce_scatter(): got = lax.all_to_all(flat, 'dp', 0, 0, tiled=True)]
    all_to_all x1, waiting for transfers between devices: 0.01 us -> 17 us  [dp_all_gather(): lax.all_to_all(copies, 'dp', 0, 0, tiled=True).reshape(-1, BLOCK, BLOCK)]
    unnamed x29 -> x21, local copies, waits for them, and re-layouts: 4.1 us -> 15.6 us
    all_to_all x1, waiting for transfers between devices: 25.3 us -> 14.3 us  [body(): lax.all_to_all(outgoing, 'mp', split_axis=1, concat_axis=2, tiled=True)]
    dot_general x1, matrix products: 9.2 us -> 2.41 us  [body(): jnp.einsum('tic,icj->tij', xn_b, gate_p, preferred_element_type=jnp.float32)]
    psum x1, blocking collectives: 17.1 us -> 23.7 us  [body(): inner = lax.psum(jnp.sum(scaled * xf, axis=1), 'mp')]
    reshape x1 -> x0, local copies, waits for them, and re-layouts: 6.65 us -> none  [body(): scaled = grad_norm.reshape(rows, width_local) * gain]
    mul x1 -> x0, other arithmetic: 6.58 us -> none  [body(): scaled = grad_norm.reshape(rows, width_local) * gain]
  transfers between devices with their start and end apart: 4 -> 4, of which waited for: 3 -> 3; matrix products, arithmetic and copies ran while one was open for 24% -> 28% of each run, Pallas kernels for 0% -> 0%
where the time goes in v1:
time: 212 us; the launch traced here: 211 us
  waiting for transfers between devices  55.6 us (26%)
  local copies, waits for them, and re-layouts  44.3 us (21%)
  starting transfers between devices  32.4 us (15%)
  blocking collectives  32 us (15%)
  other arithmetic  23.2 us (11%)
  matrix products  22.2 us (10%)
    all_to_all x1, waiting for transfers between devices, body(): lax.all_to_all(grad_perm, 'mp', split_axis=2, concat_axis=1, tiled=True)  24.3 us
    psum x1, blocking collectives, body(): inner = lax.psum(jnp.sum(scaled * xf, axis=1), 'mp')  23.7 us
    all_to_all x1, waiting for transfers between devices, dp_all_gather(): lax.all_to_all(copies, 'dp', 0, 0, tiled=True).reshape(-1, BLOCK, BLOCK)  17 us
    unnamed x21, local copies, waits for them, and re-layouts  15.6 us
    all_to_all x1, waiting for transfers between devices, body(): lax.all_to_all(outgoing, 'mp', split_axis=1, concat_axis=2, tiled=True)  14.3 us
    all_to_all x1, starting transfers between devices, dp_reduce_scatter(): got = lax.all_to_all(flat, 'dp', 0, 0, tiled=True)  9.62 us
    psum x1, blocking collectives, body(): squares = lax.psum(jnp.sum(xf * xf, axis=1), 'mp')  8.3 us
    all_to_all x1, starting transfers between devices, dp_all_gather(): lax.all_to_all(copies, 'dp', 0, 0, tiled=True).reshape(-1, BLOCK, BLOCK)  8.11 us
  transfers between devices with their start and end apart: 4, of which 3 were waited for; matrix products, arithmetic and copies ran while one was open for 28% of the time, Pallas kernels for 0%

profile of v1, /device:TPU:6, one launch (start us, length us, event | category | flops | bytes accessed | tf_op | source)
XLA Modules:
  0.0 210.6 jit_solution(8252090274251396414)
XLA Ops:
  0.6 4.7 %copy.118 = bf16[768,2048]{0,1:T(8,128)(2,1)} copy(bf16[768,2048]{1,0:T(8,128)(2,1)} %param.6) | data formatting | bytes 6291456 | tf_op args[0]
  7.9 8.3 %psum.14 = f32[768]{0:T(1024)S(1)} all-reduce(f32[768]{0:T(1024)S(1)} %fusion.8), channel_id=1, replica_groups=mesh['dp'=32,'mp'=4] {'mp'}, use_global_device_ids=true, to_apply=%region_1.0 | all-reduce | flops 768 | bytes 6144 | tf_op jit(solution)/shard_map/psum | solution.py:47
  16.2 2.9 %convert_bitcast_fusion.1 = bf16[768,16,128]{0,2,1:T(8,128)(2,1)S(1)} fusion(bf16[16,128,128]{2,1,0:T(8,128)(2,1)S(1)} %copy-done, bf16[768,2048]{1,0:T(8,128)(2,1)} %param.11), kind=kOutput, calls=%fused_computation.41 | convolution fusion | flops 404226048 | bytes 6815744 | tf_op jit(solution)/shard_map/tkm,kcm->tkc/dot_general | solution.py:44
  19.1 3.4 %copy.128 = bf16[768,16,128]{0,1,2:T(8,128)(2,1)} copy(bf16[768,16,128]{0,2,1:T(8,128)(2,1)S(1)} %convert_bitcast_fusion.1) | data formatting | bytes 6291456 | tf_op jit(solution)/shard_map/optimization_barrier | solution.py:48
  22.6 6.9 %all-to-all-start.1 = ((bf16[768,16,128]{0,1,2:T(8,128)(2,1)}), bf16[768,16,128]{0,1,2:T(8,128)(2,1)}, u32[]{:S(2)}, u32[]{:S(2)}) async-start(bf16[768,16,128]{0,1,2:T(8,128)(2,1)} %copy.128), calls=%async_computation.1 | async-start | bytes 6291456 | tf_op jit(solution)/shard_map/all_to_all | solution.py:59
  37.1 3.4 %copy.165 = bf16[768,64,32]{0,2,1:T(8,128)(2,1)} copy(bf16[768,64,32]{0,1,2:T(8,128)(2,1)S(1)} %bitcast.152) | data formatting | bytes 6291456 | tf_op jit(solution)/shard_map/reshape | solution.py:57
  40.5 24.3 %all-to-all-done.1 = bf16[768,16,128]{0,1,2:T(8,128)(2,1)} async-done(((bf16[768,16,128]{0,1,2:T(8,128)(2,1)}), bf16[768,16,128]{0,1,2:T(8,128)(2,1)}, u32[]{:S(2)}, u32[]{:S(2)}) %all-to-all-start.1) | async-done | bytes 3145760 | tf_op jit(solution)/shard_map/all_to_all | solution.py:59
  64.8 7.8 %all-to-all-start = ((bf16[768,64,32]{0,2,1:T(8,128)(2,1)}), bf16[768,64,32]{0,2,1:T(8,128)(2,1)}, u32[]{:S(2)}, u32[]{:S(2)}) async-start(bf16[768,64,32]{0,2,1:T(8,128)(2,1)} %copy.165), calls=%async_computation | async-start | bytes 6291456 | tf_op jit(solution)/shard_map/all_to_all | solution.py:61
  72.6 2.9 %copy.129 = bf16[768,16,128]{0,2,1:T(8,128)(2,1)S(1)} copy(bf16[768,16,128]{0,1,2:T(8,128)(2,1)} %all-to-all-done.1) | data formatting | bytes 6291456 | tf_op jit(solution)/shard_map/all_to_all | solution.py:59
  76.3 3.6 %copy.130 = f32[768,4,16,32]{0,2,1,3:T(8,128)S(1)} copy(f32[768,4,16,32]{0,3,1,2:T(8,128)S(1)} %convert_bitcast_fusion) | data formatting | bytes 12582912 | tf_op jit(solution)/shard_map/convert_element_type | solution.py:69
  82.4 3.2 %fusion.12 = bf16[768,16,128]{0,2,1:T(8,128)(2,1)S(1)} fusion(f32[768,16,128]{0,2,1:T(8,128)S(1)} %bitcast.140, f32[16,768,128]{1,2,0:T(8,128)S(1)} %get-tuple-element.44, bf16[16,128,128]{1,2,0:T(8,128)(2,1)S(1)} %bitcast.154, bf16[768,16,128]{0,2,1:T(8,128)(2,1)S(1)} %bitcast.134), kind=kOutput, calls=%fused_computation.18 | convolution fusion | flops 418381824 | bytes 19398656 | tf_op jit(solution)/shard_map/tic,icj->tij/dot_general | solution.py:62
  89.9 3.8 %add_bitcast_fusion = f32[768,16,128]{2,0,1:T(8,128)} fusion(f32[16,768,128]{2,1,0:T(8,128)S(1)} %fusion.34, bf16[768,16,128]{0,2,1:T(8,128)(2,1)S(1)} %fusion.12, bf16[16,128,128]{1,2,0:T(8,128)(2,1)S(1)} %bitcast.144), kind=kOutput, calls=%fused_computation.34 | convolution fusion | flops 404226048 | bytes 16252928 | tf_op jit(solution)/shard_map/tij,icj->tic/dot_general | solution.py:77
  93.7 14.3 %all-to-all-done = bf16[768,64,32]{0,2,1:T(8,128)(2,1)} async-done(((bf16[768,64,32]{0,2,1:T(8,128)(2,1)}), bf16[768,64,32]{0,2,1:T(8,128)(2,1)}, u32[]{:S(2)}, u32[]{:S(2)}) %all-to-all-start) | async-done | bytes 3145760 | tf_op jit(solution)/shard_map/all_to_all | solution.py:61
  108.0 3.8 %copy.127 = bf16[768,16,4,32]{0,3,2,1:T(8,128)(2,1)} copy(bf16[768,16,4,32]{0,3,1,2:T(8,128)(2,1)} %bitcast.14) | data formatting | bytes 6291456 | tf_op jit(solution)/shard_map/all_to_all | solution.py:61
  113.6 3.9 %fusion.24 = f32[16,128,128]{2,1,0:T(8,128)S(1)} fusion(bf16[768,16,128]{0,2,1:T(8,128)(2,1)} %bitcast.151, bf16[768,2048]{1,0:T(8,128)(2,1)} %param.11), kind=kOutput, calls=%fused_computation.36 | convolution fusion | flops 402653184 | bytes 7340032 | tf_op jit(solution)/shard_map/tkc,tkm->kcm/dot_general | solution.py:83
  119.4 9.6 %all-to-all-start.2 = ((f32[32,192,128]{2,1,0:T(8,128)}), f32[32,192,128]{2,1,0:T(8,128)}, u32[]{:S(2)}, u32[]{:S(2)}) async-start(f32[32,192,128]{2,1,0:T(8,128)} %bitcast.137), calls=%async_computation.2 | async-start | bytes 6291456 | tf_op jit(solution)/shard_map/all_to_all | solution.py:14
  129.0 4.7 %copy.148 = bf16[768,2048]{0,1:T(8,128)(2,1)} copy(bf16[768,2048]{1,0:T(8,128)(2,1)} %param.11) | data formatting | bytes 6291456 | tf_op args[5]
  133.7 6.5 %copy.149 = f32[768,16,128]{0,2,1:T(8,128)} copy(f32[768,16,128]{2,0,1:T(8,128)} %add_bitcast_fusion) | data formatting | bytes 12582912 | tf_op jit(solution)/shard_map/optimization_barrier | solution.py:80
  140.2 4.6 %fusion.9 = f32[768]{0:T(1024)S(1)} fusion(bf16[768,2048]{0,1:T(8,128)(2,1)} %copy.118, f32[768,16,128]{0,2,1:T(8,128)} %copy.149, f32[2048]{0:T(1024)S(1)} %copy-done.7), kind=kLoop, calls=%fused_computation.12 | loop fusion | flops 6290688 | bytes 9448448 | tf_op jit(solution)/shard_map/reduce_sum | solution.py:89
  144.9 23.7 %psum.15 = f32[768]{0:T(1024)S(1)} all-reduce(f32[768]{0:T(1024)S(1)} %fusion.9), channel_id=1, replica_groups=mesh['dp'=32,'mp'=4] {'mp'}, use_global_device_ids=true, to_apply=%region_4.5 | all-reduce | flops 768 | bytes 6144 | tf_op jit(solution)/shard_map/psum | solution.py:89
  168.6 6.8 %fusion.7 = bf16[768,2048]{0,1:T(8,128)(2,1)} fusion(bf16[768,2048]{0,1:T(8,128)(2,1)} %copy.118, bf16[768,2048]{0,1:T(8,128)(2,1)} %copy.148, f32[768,16,128]{0,2,1:T(8,128)} %copy.149, f32[768]{0:T(1024)S(1)} %broadcast_multiply_fusion, f32[2048]{0:T(1024)S(1)} %copy-done.7, f32[768]{0:T(1024)S(1)} %add_rsqrt_fusion), kind=kLoop, calls=%fused_computation.10 | loop fusion | flops 15728640 | bytes 15742976 | tf_op jit(solution)/shard_map/convert_element_type | solution.py:93
  179.0 8.1 %all-to-all-start.3 = ((bf16[32,192,128]{2,1,0:T(8,128)(2,1)}), bf16[32,192,128]{2,1,0:T(8,128)(2,1)S(1)}, u32[]{:S(2)}, u32[]{:S(2)}) async-start(bf16[32,192,128]{2,1,0:T(8,128)(2,1)} %broadcast_in_dim.2), calls=%async_computation.3 | async-start | bytes 3145728 | tf_op jit(solution)/shard_map/all_to_all | solution.py:21
  187.1 4.7 %copy.150 = bf16[768,2048]{1,0:T(8,128)(2,1)} copy(bf16[768,2048]{0,1:T(8,128)(2,1)} %fusion.7) | data formatting | bytes 6291456
  191.8 17.0 %all-to-all-done.3 = bf16[32,192,128]{2,1,0:T(8,128)(2,1)S(1)} async-done(((bf16[32,192,128]{2,1,0:T(8,128)(2,1)}), bf16[32,192,128]{2,1,0:T(8,128)(2,1)S(1)}, u32[]{:S(2)}, u32[]{:S(2)}) %all-to-all-start.3) | async-done | bytes 1572896 | tf_op jit(solution)/shard_map/all_to_all | solution.py:21
  (40 shorter events, 26.7 us)
Async XLA Ops:
  0.6 15.6 %copy-start = (bf16[16,128,128]{2,1,0:T(8,128)(2,1)S(1)}, bf16[16,128,128]{2,1,0:T(8,128)(2,1)}, u32[]{:S(2)}) copy-start(bf16[16,128,128]{2,1,0:T(8,128)(2,1)} %param.10) | copy-start | bytes 1572868
  22.6 6.9 %copy-start.5 = (bf16[16,128,128]{2,1,0:T(8,128)(2,1)S(1)}, bf16[16,128,128]{2,1,0:T(8,128)(2,1)}, u32[]{:S(2)}) copy-start(bf16[16,128,128]{2,1,0:T(8,128)(2,1)} %param.9) | copy-start | bytes 1572868
  22.6 7.5 %copy-start.6 = (bf16[16,128,128]{2,1,0:T(8,128)(2,1)S(1)}, bf16[16,128,128]{2,1,0:T(8,128)(2,1)}, u32[]{:S(2)}) copy-start(bf16[16,128,128]{2,1,0:T(8,128)(2,1)} %param.8) | copy-start | bytes 1572868
  22.6 42.2 %all-to-all-start.1 = ((bf16[768,16,128]{0,1,2:T(8,128)(2,1)}), bf16[768,16,128]{0,1,2:T(8,128)(2,1)}, u32[]{:S(2)}, u32[]{:S(2)}) async-start(bf16[768,16,128]{0,1,2:T(8,128)(2,1)} %copy.128), calls=%async_computation.1 | async-start | bytes 6291456 | tf_op jit(solution)/shard_map/all_to_all | solution.py:59
  29.4 1.3 copy-start.7
  33.4 1.7 copy-start.2
  64.8 43.1 %all-to-all-start = ((bf16[768,64,32]{0,2,1:T(8,128)(2,1)}), bf16[768,64,32]{0,2,1:T(8,128)(2,1)}, u32[]{:S(2)}, u32[]{:S(2)}) async-start(bf16[768,64,32]{0,2,1:T(8,128)(2,1)} %copy.165), calls=%async_computation | async-start | bytes 6291456 | tf_op jit(solution)/shard_map/all_to_all | solution.py:61
  76.3 3.7 %copy-start.3 = (bf16[768,2048]{0,1:T(8,128)(2,1)S(1)}, bf16[768,2048]{0,1:T(8,128)(2,1)}, u32[]{:S(2)}) copy-start(bf16[768,2048]{0,1:T(8,128)(2,1)} %copy-done.2) | copy-start | bytes 9437188
  113.6 3.9 %copy-start.4 = (f32[16,128,128]{2,1,0:T(8,128)S(1)}, f32[16,128,128]{2,1,0:T(8,128)}, u32[]{:S(2)}) copy-start(f32[16,128,128]{2,1,0:T(8,128)} %copy.166) | copy-start | bytes 3145732
  119.4 56.0 %all-to-all-start.2 = ((f32[32,192,128]{2,1,0:T(8,128)}), f32[32,192,128]{2,1,0:T(8,128)}, u32[]{:S(2)}, u32[]{:S(2)}) async-start(f32[32,192,128]{2,1,0:T(8,128)} %bitcast.137), calls=%async_computation.2 | async-start | bytes 6291456 | tf_op jit(solution)/shard_map/all_to_all | solution.py:14
  179.0 29.9 %all-to-all-start.3 = ((bf16[32,192,128]{2,1,0:T(8,128)(2,1)}), bf16[32,192,128]{2,1,0:T(8,128)(2,1)S(1)}, u32[]{:S(2)}, u32[]{:S(2)}) async-start(bf16[32,192,128]{2,1,0:T(8,128)(2,1)} %broadcast_in_dim.2), calls=%async_computation.3 | async-start | bytes 3145728 | tf_op jit(solution)/shard_map/all_to_all | solution.py:21
  187.1 23.5 %copy-start.1 = (bf16[16,128,128]{2,1,0:T(8,128)(2,1)S(1)}, bf16[16,128,128]{2,1,0:T(8,128)(2,1)}, u32[]{:S(2)}) copy-start(bf16[16,128,128]{2,1,0:T(8,128)(2,1)} %param.10) | copy-start | bytes 1572868

commit v2 on v1

--- a/solution.py
+++ b/solution.py
@@ -26,6 +26,12 @@
     return tuple(out)
 
 
+def mp_sum(v):
+    n = lax.axis_size("mp")
+    v = v + lax.ppermute(v, "mp", [(i, i ^ 1) for i in range(n)])
+    return v + lax.ppermute(v, "mp", [(i, i ^ 2) for i in range(n)])
+
+
 def pair_major(blocks):
     n, c, _ = blocks.shape
     return blocks.reshape(n, c, NBLK, 2).transpose(0, 1, 3, 2).reshape(n, c, 2 * NBLK)
@@ -44,7 +50,7 @@
     grad_perm = jnp.einsum(
         "tkm,kcm->tkc", cot_blocks, right_blocks, preferred_element_type=jnp.float32
     ).astype(jnp.bfloat16)
-    squares = lax.psum(jnp.sum(xf * xf, axis=1), "mp")
+    squares = mp_sum(jnp.sum(xf * xf, axis=1))
     grad_perm, squares = lax.optimization_barrier((grad_perm, squares))
     rstd = lax.rsqrt(squares / W + 1e-05)[:, None]
     xn = (xf * rstd * gain).astype(jnp.bfloat16).reshape(rows, nlocal, BLOCK)
@@ -86,12 +92,12 @@
     partials = (left_local, gate_local, right_local)
     mine = dp_reduce_scatter(partials)
     scaled = grad_norm.reshape(rows, width_local) * gain
-    inner = lax.psum(jnp.sum(scaled * xf, axis=1), "mp")
+    inner = mp_sum(jnp.sum(scaled * xf, axis=1))
+    mine, inner = lax.optimization_barrier((mine, inner))
     mean_inner = (inner / W)[:, None]
     grad_input = (
         cotangent.astype(jnp.float32) + rstd * (scaled - xf * rstd * rstd * mean_inner)
     ).astype(jnp.bfloat16)
-    mine, grad_input = lax.optimization_barrier((mine, grad_input))
     left_total, gate_total, right_total = dp_all_gather(mine, [p.shape for p in partials])
     return (grad_input, left_total, gate_total, right_total)
 

time: 212 us -> 216 us (1.019)
  blocking collectives: 32 us -> 0 us
  waiting for transfers between devices: 55.6 us -> 77.1 us
  matrix products: 22.2 us -> 29.9 us
  local copies, waits for them, and re-layouts: 44.3 us -> 46.7 us
  starting transfers between devices: 32.4 us -> 34.7 us
    psum x2 -> x0, blocking collectives: 32 us -> none  [the longest x1 23.7 us: body(): inner = lax.psum(jnp.sum(scaled * xf, axis=1), 'mp')]
    ppermute x0 -> x4, waiting for transfers between devices: none -> 24.5 us  [the longest x2 22.2 us: mp_sum(): return v + lax.ppermute(v, 'mp', [(i, i ^ 2) for i in range(n)])]
    all_to_all x1, waiting for transfers between devices: 17 us -> 5.39 us  [dp_all_gather(): lax.all_to_all(copies, 'dp', 0, 0, tiled=True).reshape(-1, BLOCK, BLOCK)]
    ppermute x0 -> x4, starting transfers between devices: none -> 4.81 us  [the longest x2 4.64 us: mp_sum(): return v + lax.ppermute(v, 'mp', [(i, i ^ 2) for i in range(n)])]
    all_to_all x1, waiting for transfers between devices: 14.3 us -> 18.7 us  [body(): lax.all_to_all(outgoing, 'mp', split_axis=1, concat_axis=2, tiled=True)]
    dot_general x1, matrix products: 3.2 us -> 6.5 us  [body(): jnp.einsum('tic,icj->tij', xn_b, left_p, preferred_element_type=jnp.float32)]
    all_to_all x1, waiting for transfers between devices: 0.01 us -> 2.97 us  [dp_reduce_scatter(): got = lax.all_to_all(flat, 'dp', 0, 0, tiled=True)]
    dot_general x1, matrix products: 1.06 us -> 3.68 us  [body(): jnp.einsum('tij,icj->tic', grad_a, left_p, preferred_element_type=jnp.flo...]
  transfers between devices with their start and end apart: 4 -> 8, of which waited for: 3 -> 7; matrix products, arithmetic and copies ran while one was open for 28% -> 27% of each run, Pallas kernels for 0% -> 0%
where the time goes in v2:
time: 216 us; the launch traced here: 213 us
  waiting for transfers between devices  77.1 us (36%)
  local copies, waits for them, and re-layouts  46.7 us (22%)
  starting transfers between devices  34.7 us (16%)
  matrix products  29.9 us (14%)
  other arithmetic  23.5 us (11%)
    all_to_all x1, waiting for transfers between devices, body(): lax.all_to_all(grad_perm, 'mp', split_axis=2, concat_axis=1, tiled=True)  25.5 us
    ppermute x2, waiting for transfers between devices, mp_sum(): return v + lax.ppermute(v, 'mp', [(i, i ^ 2) for i in range(n)])  22.2 us
    all_to_all x1, waiting for transfers between devices, body(): lax.all_to_all(outgoing, 'mp', split_axis=1, concat_axis=2, tiled=True)  18.7 us
    unnamed x31, local copies, waits for them, and re-layouts  15.9 us
    all_to_all x1, starting transfers between devices, dp_reduce_scatter(): got = lax.all_to_all(flat, 'dp', 0, 0, tiled=True)  9.62 us
    all_to_all x1, starting transfers between devices, body(): lax.all_to_all(outgoing, 'mp', split_axis=1, concat_axis=2, tiled=True)  7.8 us
    convert_element_type x1, other arithmetic, body(): grad_input = (cotangent.astype(jnp.float32) + rstd * (scaled - xf * rstd...  6.91 us
    all_to_all x1, starting transfers between devices, body(): lax.all_to_all(grad_perm, 'mp', split_axis=2, concat_axis=1, tiled=True)  6.86 us
  transfers between devices with their start and end apart: 8, of which 7 were waited for; matrix products, arithmetic and copies ran while one was open for 27% of the time, Pallas kernels for 0%

profile of v2, /device:TPU:6, one launch (start us, length us, event | category | flops | bytes accessed | tf_op | source)
XLA Modules:
  0.0 212.9 jit_solution(7343709104582799012)
XLA Ops:
  0.6 4.7 %copy.120 = bf16[768,2048]{0,1:T(8,128)(2,1)} copy(bf16[768,2048]{1,0:T(8,128)(2,1)} %param.6) | data formatting | bytes 6291456 | tf_op args[0]
  14.8 5.3 %copy.129 = bf16[768,16,128]{0,1,2:T(8,128)(2,1)} copy(bf16[768,16,128]{0,2,1:T(8,128)(2,1)} %convert_bitcast_fusion.1) | data formatting | bytes 6291456 | tf_op jit(solution)/shard_map/optimization_barrier | solution.py:54
  20.1 6.9 %all-to-all-start.1 = ((bf16[768,16,128]{0,1,2:T(8,128)(2,1)}), bf16[768,16,128]{0,1,2:T(8,128)(2,1)}, u32[]{:S(2)}, u32[]{:S(2)}) async-start(bf16[768,16,128]{0,1,2:T(8,128)(2,1)} %copy.129), calls=%async_computation.1 | async-start | bytes 6291456 | tf_op jit(solution)/shard_map/all_to_all | solution.py:65
  33.4 3.5 %copy.165 = bf16[768,64,32]{0,2,1:T(8,128)(2,1)} copy(bf16[768,64,32]{0,1,2:T(8,128)(2,1)S(1)} %bitcast.154) | data formatting | bytes 6291456 | tf_op jit(solution)/shard_map/reshape | solution.py:63
  36.8 25.5 %all-to-all-done.1 = bf16[768,16,128]{0,1,2:T(8,128)(2,1)} async-done(((bf16[768,16,128]{0,1,2:T(8,128)(2,1)}), bf16[768,16,128]{0,1,2:T(8,128)(2,1)}, u32[]{:S(2)}, u32[]{:S(2)}) %all-to-all-start.1) | async-done | bytes 3145760 | tf_op jit(solution)/shard_map/all_to_all | solution.py:65
  62.3 7.8 %all-to-all-start = ((bf16[768,64,32]{0,2,1:T(8,128)(2,1)}), bf16[768,64,32]{0,2,1:T(8,128)(2,1)}, u32[]{:S(2)}, u32[]{:S(2)}) async-start(bf16[768,64,32]{0,2,1:T(8,128)(2,1)} %copy.165), calls=%async_computation | async-start | bytes 6291456 | tf_op jit(solution)/shard_map/all_to_all | solution.py:67
  73.9 3.6 %copy.131 = f32[768,4,16,32]{0,2,1,3:T(8,128)S(1)} copy(f32[768,4,16,32]{0,3,1,2:T(8,128)S(1)} %convert_bitcast_fusion) | data formatting | bytes 12582912 | tf_op jit(solution)/shard_map/convert_element_type | solution.py:75
  77.6 4.4 %fusion.17 = (bf16[768,16,128]{0,2,1:T(8,128)(2,1)S(1)}, f32[16,768,128]{1,2,0:T(8,128)}) fusion(f32[768,16,128]{0,2,1:T(8,128)S(1)} %bitcast.141, bf16[16,128,128]{1,2,0:T(8,128)(2,1)S(1)} %bitcast.145, bf16[768,16,128]{0,2,1:T(8,128)(2,1)S(1)} %bitcast.133), kind=kOutput, calls=%fused_computation.26 | convolution fusion | flops 412090368 | bytes 19398656 | tf_op jit(solution)/shard_map/tic,icj->tij/dot_general | solution.py:69
  83.1 3.7 %fusion.34 = f32[16,768,128]{2,1,0:T(8,128)} fusion(bf16[768,16,128]{0,2,1:T(8,128)(2,1)S(1)} %get-tuple-element.43, bf16[16,128,128]{1,2,0:T(8,128)(2,1)S(1)} %bitcast.156), kind=kOutput, calls=%fused_computation.51 | convolution fusion | flops 402653184 | bytes 9961472 | tf_op jit(solution)/shard_map/tij,icj->tic/dot_general | solution.py:82
  86.8 18.7 %all-to-all-done = bf16[768,64,32]{0,2,1:T(8,128)(2,1)} async-done(((bf16[768,64,32]{0,2,1:T(8,128)(2,1)}), bf16[768,64,32]{0,2,1:T(8,128)(2,1)}, u32[]{:S(2)}, u32[]{:S(2)}) %all-to-all-start) | async-done | bytes 3145760 | tf_op jit(solution)/shard_map/all_to_all | solution.py:67
  105.5 4.0 %copy.128 = bf16[768,16,4,32]{0,3,2,1:T(8,128)(2,1)} copy(bf16[768,16,4,32]{0,3,1,2:T(8,128)(2,1)} %bitcast.14) | data formatting | bytes 6291456 | tf_op jit(solution)/shard_map/all_to_all | solution.py:67
  109.5 6.5 %fusion.12 = bf16[768,16,128]{0,2,1:T(8,128)(2,1)S(1)} fusion(f32[768,16,128]{0,2,1:T(8,128)} %bitcast.142, f32[16,768,128]{1,2,0:T(8,128)} %get-tuple-element.44, bf16[16,128,128]{1,2,0:T(8,128)(2,1)S(1)} %bitcast.157, bf16[768,16,128]{0,2,1:T(8,128)(2,1)S(1)} %bitcast.135), kind=kOutput, calls=%fused_computation.18 | convolution fusion | flops 418381824 | bytes 19398656 | tf_op jit(solution)/shard_map/tic,icj->tij/dot_general | solution.py:68
  118.3 3.8 %add_bitcast_fusion = f32[768,16,128]{2,0,1:T(8,128)} fusion(f32[16,768,128]{2,1,0:T(8,128)S(1)} %bitcast.138, bf16[768,16,128]{0,2,1:T(8,128)(2,1)S(1)} %fusion.12, bf16[16,128,128]{1,2,0:T(8,128)(2,1)S(1)} %bitcast.146), kind=kOutput, calls=%fused_computation.34 | convolution fusion | flops 404226048 | bytes 16252928 | tf_op jit(solution)/shard_map/tij,icj->tic/dot_general | solution.py:83
  123.9 3.9 %fusion.24 = f32[16,128,128]{2,1,0:T(8,128)S(1)} fusion(bf16[768,16,128]{0,2,1:T(8,128)(2,1)} %bitcast.153, bf16[768,2048]{1,0:T(8,128)(2,1)} %param.11), kind=kOutput, calls=%fused_computation.36 | convolution fusion | flops 402653184 | bytes 7340032 | tf_op jit(solution)/shard_map/tkc,tkm->kcm/dot_general | solution.py:89
  129.7 9.6 %all-to-all-start.2 = ((f32[32,192,128]{2,1,0:T(8,128)}), f32[32,192,128]{2,1,0:T(8,128)}, u32[]{:S(2)}, u32[]{:S(2)}) async-start(f32[32,192,128]{2,1,0:T(8,128)} %bitcast.139), calls=%async_computation.2 | async-start | bytes 6291456 | tf_op jit(solution)/shard_map/all_to_all | solution.py:14
  139.3 6.6 %copy.146 = f32[768,16,128]{0,2,1:T(8,128)} copy(f32[768,16,128]{2,0,1:T(8,128)} %add_bitcast_fusion) | data formatting | bytes 12582912 | tf_op jit(solution)/shard_map/optimization_barrier | solution.py:86
  145.9 4.6 %fusion.9 = f32[768]{0:T(1024)S(1)} fusion(bf16[768,2048]{0,1:T(8,128)(2,1)} %copy.120, f32[768,16,128]{0,2,1:T(8,128)} %copy.146, f32[2048]{0:T(1024)S(1)} %copy-done.10), kind=kLoop, calls=%fused_computation.12 | loop fusion | flops 6290688 | bytes 9448448 | tf_op jit(solution)/shard_map/reduce_sum | solution.py:95
  151.8 3.2 %collective-permute-start.3 = (f32[768]{0:T(1024)S(1)}, f32[768]{0:T(1024)S(1)}, u32[]{:S(2)}, u32[]{:S(2)}) collective-permute-start(f32[768]{0:T(1024)S(1)} %add.47), channel_id=1, source_target_pairs={{0,2},{1,3},{2,0},{3,1},{4,6},{5,7},{6,4},{7,5},{8,10},{9,11},{10,... | collective-permute-start | bytes 9224 | tf_op jit(solution)/shard_map/ppermute | solution.py:32
  155.0 22.2 %collective-permute-done.3 = f32[768]{0:T(1024)S(1)} collective-permute-done((f32[768]{0:T(1024)S(1)}, f32[768]{0:T(1024)S(1)}, u32[]{:S(2)}, u32[]{:S(2)}) %collective-permute-start.3) | collective-permute-done | bytes 3104 | tf_op jit(solution)/shard_map/ppermute | solution.py:32
  183.7 5.7 %all-to-all-start.3 = ((bf16[32,192,128]{2,1,0:T(8,128)(2,1)}), bf16[32,192,128]{2,1,0:T(8,128)(2,1)S(1)}, u32[]{:S(2)}, u32[]{:S(2)}) async-start(bf16[32,192,128]{2,1,0:T(8,128)(2,1)} %broadcast_in_dim.2), calls=%async_computation.3 | async-start | bytes 3145728 | tf_op jit(solution)/shard_map/all_to_all | solution.py:21
  189.4 4.7 %copy.118 = bf16[768,2048]{0,1:T(8,128)(2,1)} copy(bf16[768,2048]{1,0:T(8,128)(2,1)} %param.11) | data formatting | bytes 6291456 | tf_op args[5]
  194.1 6.9 %fusion.7 = bf16[768,2048]{0,1:T(8,128)(2,1)} fusion(bf16[768,2048]{0,1:T(8,128)(2,1)} %copy.120, bf16[768,2048]{0,1:T(8,128)(2,1)} %copy.118, f32[768,16,128]{0,2,1:T(8,128)} %copy.146, f32[768]{0:T(1024)S(1)} %broadcast_multiply_fusion, f32[2048]{0:T(1024)S(1)} %copy-done.10, f32[768]{0:T(1024)S(1)} %add_rsqrt_fusion), kind=kLoop, calls=%fused_computation.10 | loop fusion | flops 15728640 | bytes 15742976 | tf_op jit(solution)/shard_map/convert_element_type | solution.py:100
  201.0 4.7 %copy.150 = bf16[768,2048]{1,0:T(8,128)(2,1)} copy(bf16[768,2048]{0,1:T(8,128)(2,1)} %fusion.7) | data formatting | bytes 6291456
  205.7 5.4 %all-to-all-done.3 = bf16[32,192,128]{2,1,0:T(8,128)(2,1)S(1)} async-done(((bf16[32,192,128]{2,1,0:T(8,128)(2,1)}), bf16[32,192,128]{2,1,0:T(8,128)(2,1)S(1)}, u32[]{:S(2)}, u32[]{:S(2)}) %all-to-all-start.3) | async-done | bytes 1572896 | tf_op jit(solution)/shard_map/all_to_all | solution.py:21
  (61 shorter events, 36.1 us)
Async XLA Ops:
  0.6 10.2 %copy-start = (bf16[16,128,128]{2,1,0:T(8,128)(2,1)S(1)}, bf16[16,128,128]{2,1,0:T(8,128)(2,1)}, u32[]{:S(2)}) copy-start(bf16[16,128,128]{2,1,0:T(8,128)(2,1)} %param.10) | copy-start | bytes 1572868
  5.3 5.5 %copy-start.5 = (bf16[768,2048]{1,0:T(8,128)(2,1)S(1)}, bf16[768,2048]{1,0:T(8,128)(2,1)}, u32[]{:S(2)}) copy-start(bf16[768,2048]{1,0:T(8,128)(2,1)} %param.11) | copy-start | bytes 9437188
  8.1 1.2 collective-permute-start
  9.3 4.1 %copy-start.8 = (bf16[16,128,128]{2,1,0:T(8,128)(2,1)S(1)}, bf16[16,128,128]{2,1,0:T(8,128)(2,1)}, u32[]{:S(2)}) copy-start(bf16[16,128,128]{2,1,0:T(8,128)(2,1)} %param.8) | copy-start | bytes 1572868
  9.3 4.8 %copy-start.9 = (bf16[16,128,128]{2,1,0:T(8,128)(2,1)S(1)}, bf16[16,128,128]{2,1,0:T(8,128)(2,1)}, u32[]{:S(2)}) copy-start(bf16[16,128,128]{2,1,0:T(8,128)(2,1)} %param.9) | copy-start | bytes 1572868
  9.3 5.5 %collective-permute-start.1 = (f32[768]{0:T(1024)S(1)}, f32[768]{0:T(1024)S(1)}, u32[]{:S(2)}, u32[]{:S(2)}) collective-permute-start(f32[768]{0:T(1024)S(1)} %add.38), channel_id=1, source_target_pairs={{0,2},{1,3},{2,0},{3,1},{4,6},{5,7},{6,4},{7,5},{8,10},{9,11},{10,... | collective-permute-start | bytes 9224 | tf_op jit(solution)/shard_map/ppermute | solution.py:32
  20.1 6.9 %copy-start.10 = (f32[2048]{0:T(1024)S(1)}, f32[2048]{0:T(1024)}, u32[]{:S(2)}) copy-start(f32[2048]{0:T(1024)} %param.7) | copy-start | bytes 24580
  20.1 42.2 %all-to-all-start.1 = ((bf16[768,16,128]{0,1,2:T(8,128)(2,1)}), bf16[768,16,128]{0,1,2:T(8,128)(2,1)}, u32[]{:S(2)}, u32[]{:S(2)}) async-start(bf16[768,16,128]{0,1,2:T(8,128)(2,1)} %copy.129), calls=%async_computation.1 | async-start | bytes 6291456 | tf_op jit(solution)/shard_map/all_to_all | solution.py:65
  29.6 1.7 copy-start.2
  62.3 43.2 %all-to-all-start = ((bf16[768,64,32]{0,2,1:T(8,128)(2,1)}), bf16[768,64,32]{0,2,1:T(8,128)(2,1)}, u32[]{:S(2)}, u32[]{:S(2)}) async-start(bf16[768,64,32]{0,2,1:T(8,128)(2,1)} %copy.165), calls=%async_computation | async-start | bytes 6291456 | tf_op jit(solution)/shard_map/all_to_all | solution.py:67
  73.9 3.7 %copy-start.3 = (bf16[768,2048]{0,1:T(8,128)(2,1)S(1)}, bf16[768,2048]{0,1:T(8,128)(2,1)}, u32[]{:S(2)}) copy-start(bf16[768,2048]{0,1:T(8,128)(2,1)} %copy-done.2) | copy-start | bytes 9437188
  77.5 4.6 %copy-start.6 = (f32[768,4,16,32]{0,2,1,3:T(8,128)}, f32[768,4,16,32]{0,2,1,3:T(8,128)S(1)}, u32[]{:S(2)}) copy-start(f32[768,4,16,32]{0,2,1,3:T(8,128)S(1)} %copy.131) | copy-start | bytes 18874372
  105.5 4.0 %copy-start.4 = (bf16[768,2048]{0,1:T(8,128)(2,1)S(1)}, bf16[768,2048]{0,1:T(8,128)(2,1)}, u32[]{:S(2)}) copy-start(bf16[768,2048]{0,1:T(8,128)(2,1)} %copy-done.2) | copy-start | bytes 9437188
  109.5 8.7 %slice-start = ((s8[6291456]{0:T(1024)(128)(4,1)}), s8[4194304]{0:T(1024)(128)(4,1)S(1)}, s32[]{:S(2)}) async-start(s8[6291456]{0:T(1024)(128)(4,1)} %bitcast.137), calls=%async_computation.4 | async-start | bytes 8388608
  109.5 8.7 %slice-start.1 = ((s8[6291456]{0:T(1024)(128)(4,1)}), s8[2097152]{0:T(1024)(128)(4,1)S(1)}, s32[]{:S(2)}) async-start(s8[6291456]{0:T(1024)(128)(4,1)} %bitcast.137), calls=%async_computation.5 | async-start | bytes 4194304
  123.9 3.9 %copy-start.7 = (f32[16,128,128]{2,1,0:T(8,128)S(1)}, f32[16,128,128]{2,1,0:T(8,128)}, u32[]{:S(2)}) copy-start(f32[16,128,128]{2,1,0:T(8,128)} %copy.166) | copy-start | bytes 3145732
  129.7 50.5 %all-to-all-start.2 = ((f32[32,192,128]{2,1,0:T(8,128)}), f32[32,192,128]{2,1,0:T(8,128)}, u32[]{:S(2)}, u32[]{:S(2)}) async-start(f32[32,192,128]{2,1,0:T(8,128)} %bitcast.139), calls=%async_computation.2 | async-start | bytes 6291456 | tf_op jit(solution)/shard_map/all_to_all | solution.py:14
  150.6 1.2 collective-permute-start.2
  151.8 25.4 %collective-permute-start.3 = (f32[768]{0:T(1024)S(1)}, f32[768]{0:T(1024)S(1)}, u32[]{:S(2)}, u32[]{:S(2)}) collective-permute-start(f32[768]{0:T(1024)S(1)} %add.47), channel_id=1, source_target_pairs={{0,2},{1,3},{2,0},{3,1},{4,6},{5,7},{6,4},{7,5},{8,10},{9,11},{10,... | collective-permute-start | bytes 9224 | tf_op jit(solution)/shard_map/ppermute | solution.py:32
  183.7 27.4 %all-to-all-start.3 = ((bf16[32,192,128]{2,1,0:T(8,128)(2,1)}), bf16[32,192,128]{2,1,0:T(8,128)(2,1)S(1)}, u32[]{:S(2)}, u32[]{:S(2)}) async-start(bf16[32,192,128]{2,1,0:T(8,128)(2,1)} %broadcast_in_dim.2), calls=%async_computation.3 | async-start | bytes 3145728 | tf_op jit(solution)/shard_map/all_to_all | solution.py:21
  201.0 11.8 %copy-start.1 = (bf16[16,128,128]{2,1,0:T(8,128)(2,1)S(1)}, bf16[16,128,128]{2,1,0:T(8,128)(2,1)}, u32[]{:S(2)}) copy-start(bf16[16,128,128]{2,1,0:T(8,128)(2,1)} %param.10) | copy-start | bytes 1572868

commit v3 on v1

--- a/solution.py
+++ b/solution.py
@@ -8,6 +8,28 @@
 NBLK = 64
 
 
+HALVING_BITS = (0, 2, 1, 3, 4)
+
+
+def dp_halving_sum(flat):
+    me = lax.axis_index("dp")
+    ndp = lax.axis_size("dp")
+    for b in HALVING_BITS:
+        bit = (me >> b) & 1
+        lo, hi = jnp.split(flat, 2)
+        keep = jnp.where(bit == 0, lo, hi)
+        send = jnp.where(bit == 0, hi, lo)
+        flat = keep + lax.ppermute(send, "dp", [(i, i ^ (1 << b)) for i in range(ndp)])
+    return flat
+
+
+def halving_order(gathered):
+    nb = len(HALVING_BITS)
+    view = gathered.reshape((2,) * nb + gathered.shape[1:])
+    axes = [nb - 1 - b for b in HALVING_BITS]
+    return view.transpose(axes + list(range(nb, view.ndim))).reshape(gathered.shape)
+
+
 def dp_reduce_scatter(parts):
     ndp = lax.axis_size("dp")
     flat = jnp.concatenate([p.reshape(-1, BLOCK) for p in parts]).reshape(ndp, -1, BLOCK)
@@ -15,15 +37,10 @@
     return jnp.sum(got, axis=0)
 
 
-def dp_all_gather(mine, shapes):
+def dp_all_gather(mine):
     ndp = lax.axis_size("dp")
     copies = jnp.broadcast_to(mine.astype(jnp.bfloat16)[None], (ndp,) + mine.shape)
-    whole = lax.all_to_all(copies, "dp", 0, 0, tiled=True).reshape(-1, BLOCK, BLOCK)
-    out, at = [], 0
-    for shape in shapes:
-        out.append(whole[at:at + shape[0]].astype(jnp.float32))
-        at += shape[0]
-    return tuple(out)
+    return lax.all_to_all(copies, "dp", 0, 0, tiled=True)
 
 
 def pair_major(blocks):
@@ -77,14 +94,13 @@
     grad_norm = grad_norm + jnp.einsum(
         "tij,icj->tic", grad_g, gate_p, preferred_element_type=jnp.float32
     )
-    permuted, left_local, gate_local, grad_norm = lax.optimization_barrier(
-        (permuted, left_local, gate_local, grad_norm)
-    )
+    lg_mine = dp_halving_sum(jnp.concatenate([left_local.reshape(-1, BLOCK), gate_local.reshape(-1, BLOCK)]))
+    permuted, grad_norm = lax.optimization_barrier((permuted, grad_norm))
     right_local = jnp.einsum(
         "tkc,tkm->kcm", permuted, cot_blocks, preferred_element_type=jnp.float32
     )
-    partials = (left_local, gate_local, right_local)
-    mine = dp_reduce_scatter(partials)
+    right_mine = dp_reduce_scatter((right_local,))
+    mine = jnp.concatenate([lg_mine, right_mine])
     scaled = grad_norm.reshape(rows, width_local) * gain
     inner = lax.psum(jnp.sum(scaled * xf, axis=1), "mp")
     mean_inner = (inner / W)[:, None]
@@ -92,7 +108,11 @@
         cotangent.astype(jnp.float32) + rstd * (scaled - xf * rstd * rstd * mean_inner)
     ).astype(jnp.bfloat16)
     mine, grad_input = lax.optimization_barrier((mine, grad_input))
-    left_total, gate_total, right_total = dp_all_gather(mine, [p.shape for p in partials])
+    whole = dp_all_gather(mine)
+    nlg = lg_mine.shape[0]
+    lg = halving_order(whole[:, :nlg]).reshape(2, nlocal, BLOCK, BLOCK).astype(jnp.float32)
+    left_total, gate_total = lg[0], lg[1]
+    right_total = whole[:, nlg:].reshape(nlocal, BLOCK, BLOCK).astype(jnp.float32)
     return (grad_input, left_total, gate_total, right_total)
 
 

time: 212 us -> 221 us (1.042)
  blocking collectives: 32 us -> 17.3 us
  waiting for transfers between devices: 55.6 us -> 67 us
  starting transfers between devices: 32.4 us -> 41.2 us
  other arithmetic: 23.2 us -> 20.5 us
  matrix products: 22.2 us -> 24.8 us
  local copies, waits for them, and re-layouts: 44.3 us -> 46.6 us
    psum x1, blocking collectives: 23.7 us -> 9.04 us  [body(): inner = lax.psum(jnp.sum(scaled * xf, axis=1), 'mp')]
    ppermute x0 -> x5, waiting for transfers between devices: none -> 14 us  [dp_halving_sum(): lax.ppermute(send, 'dp', [(i, i ^ 1 << b) for i in range(ndp)])]
    ppermute x0 -> x5, starting transfers between devices: none -> 10.7 us  [dp_halving_sum(): lax.ppermute(send, 'dp', [(i, i ^ 1 << b) for i in range(ndp)])]
    reshape x4 -> x0, local copies, waits for them, and re-layouts: 3.04 us -> none  [the longest x2 1.81 us: dp_reduce_scatter(): p.reshape(-1, BLOCK)]
    unnamed x21 -> x26, local copies, waits for them, and re-layouts: 15.6 us -> 17.6 us
  transfers between devices with their start and end apart: 4 -> 9, of which waited for: 3 -> 6; matrix products, arithmetic and copies ran while one was open for 28% -> 25% of each run, Pallas kernels for 0% -> 0%
where the time goes in v3:
time: 221 us; the launch traced here: 218 us
  waiting for transfers between devices  67 us (30%)
  local copies, waits for them, and re-layouts  46.6 us (21%)
  starting transfers between devices  41.2 us (19%)
  matrix products  24.8 us (11%)
  other arithmetic  20.5 us (9%)
  blocking collectives  17.3 us (8%)
    all_to_all x1, waiting for transfers between devices, body(): lax.all_to_all(grad_perm, 'mp', split_axis=2, concat_axis=1, tiled=True)  24.2 us
    unnamed x26, local copies, waits for them, and re-layouts  17.6 us
    all_to_all x1, waiting for transfers between devices, dp_all_gather(): return lax.all_to_all(copies, 'dp', 0, 0, tiled=True)  16.3 us
    ppermute x5, waiting for transfers between devices, dp_halving_sum(): lax.ppermute(send, 'dp', [(i, i ^ 1 << b) for i in range(ndp)])  14 us
    all_to_all x1, waiting for transfers between devices, body(): lax.all_to_all(outgoing, 'mp', split_axis=1, concat_axis=2, tiled=True)  12.5 us
    ppermute x5, starting transfers between devices, dp_halving_sum(): lax.ppermute(send, 'dp', [(i, i ^ 1 << b) for i in range(ndp)])  10.7 us
    all_to_all x1, starting transfers between devices, dp_reduce_scatter(): got = lax.all_to_all(flat, 'dp', 0, 0, tiled=True)  9.27 us
    psum x1, blocking collectives, body(): inner = lax.psum(jnp.sum(scaled * xf, axis=1), 'mp')  9.04 us
  transfers between devices with their start and end apart: 9, of which 6 were waited for; matrix products, arithmetic and copies ran while one was open for 25% of the time, Pallas kernels for 0%

profile of v3, /device:TPU:6, one launch (start us, length us, event | category | flops | bytes accessed | tf_op | source)
XLA Modules:
  0.0 218.4 jit_solution(2726389123053383827)
XLA Ops:
  0.6 4.7 %copy.120 = bf16[768,2048]{0,1:T(8,128)(2,1)} copy(bf16[768,2048]{1,0:T(8,128)(2,1)} %param.6) | data formatting | bytes 6291456 | tf_op args[0]
  7.9 8.3 %psum.14 = f32[768]{0:T(1024)S(1)} all-reduce(f32[768]{0:T(1024)S(1)} %fusion.8), channel_id=1, replica_groups=mesh['dp'=32,'mp'=4] {'mp'}, use_global_device_ids=true, to_apply=%region_1.0 | all-reduce | flops 768 | bytes 6144 | tf_op jit(solution)/shard_map/psum | solution.py:64
  19.1 3.4 %copy.129 = bf16[768,16,128]{0,1,2:T(8,128)(2,1)} copy(bf16[768,16,128]{0,2,1:T(8,128)(2,1)S(1)} %convert_bitcast_fusion.1) | data formatting | bytes 6291456 | tf_op jit(solution)/shard_map/optimization_barrier | solution.py:65
  22.5 6.9 %all-to-all-start = ((bf16[768,16,128]{0,1,2:T(8,128)(2,1)}), bf16[768,16,128]{0,1,2:T(8,128)(2,1)}, u32[]{:S(2)}, u32[]{:S(2)}) async-start(bf16[768,16,128]{0,1,2:T(8,128)(2,1)} %copy.129), calls=%async_computation | async-start | bytes 6291456 | tf_op jit(solution)/shard_map/all_to_all | solution.py:76
  37.1 3.5 %copy.168 = bf16[768,64,32]{0,2,1:T(8,128)(2,1)} copy(bf16[768,64,32]{0,1,2:T(8,128)(2,1)S(1)} %bitcast.164) | data formatting | bytes 6291456 | tf_op jit(solution)/shard_map/reshape | solution.py:74
  40.6 24.2 %all-to-all-done = bf16[768,16,128]{0,1,2:T(8,128)(2,1)} async-done(((bf16[768,16,128]{0,1,2:T(8,128)(2,1)}), bf16[768,16,128]{0,1,2:T(8,128)(2,1)}, u32[]{:S(2)}, u32[]{:S(2)}) %all-to-all-start) | async-done | bytes 3145760 | tf_op jit(solution)/shard_map/all_to_all | solution.py:76
  68.6 3.9 %copy.131 = f32[768,4,16,32]{0,2,1,3:T(8,128)S(1)} copy(f32[768,4,16,32]{0,3,1,2:T(8,128)S(1)} %convert_bitcast_fusion) | data formatting | bytes 12582912 | tf_op jit(solution)/shard_map/convert_element_type | solution.py:86
  84.1 7.8 %all-to-all-start.1 = ((bf16[768,64,32]{0,2,1:T(8,128)(2,1)}), bf16[768,64,32]{0,2,1:T(8,128)(2,1)}, u32[]{:S(2)}, u32[]{:S(2)}) async-start(bf16[768,64,32]{0,2,1:T(8,128)(2,1)} %copy.168), calls=%async_computation.1 | async-start | bytes 6291456 | tf_op jit(solution)/shard_map/all_to_all | solution.py:78
  91.8 4.7 %copy.149 = bf16[768,2048]{0,1:T(8,128)(2,1)} copy(bf16[768,2048]{1,0:T(8,128)(2,1)} %param.11) | data formatting | bytes 6291456 | tf_op args[5]
  100.1 7.5 %collective-permute-done = f32[2048,128]{0,1:T(8,128)S(1)} collective-permute-done((f32[2048,128]{0,1:T(8,128)}, f32[2048,128]{0,1:T(8,128)S(1)}, u32[]{:S(2)}, u32[]{:S(2)}) %collective-permute-start) | collective-permute-done | bytes 1048608 | tf_op jit(solution)/shard_map/ppermute | solution.py:22
  110.9 3.8 %add_bitcast_fusion = f32[768,16,128]{2,0,1:T(8,128)} fusion(f32[16,768,128]{2,1,0:T(8,128)S(1)} %fusion.34, bf16[768,16,128]{0,2,1:T(8,128)(2,1)S(1)} %copy-done.6, bf16[16,128,128]{1,2,0:T(8,128)(2,1)S(1)} %bitcast.157), kind=kOutput, calls=%fused_computation.34 | convolution fusion | flops 404226048 | bytes 16252928 | tf_op jit(solution)/shard_map/tij,icj->tic/dot_general | solution.py:94
  114.8 12.5 %all-to-all-done.1 = bf16[768,64,32]{0,2,1:T(8,128)(2,1)} async-done(((bf16[768,64,32]{0,2,1:T(8,128)(2,1)}), bf16[768,64,32]{0,2,1:T(8,128)(2,1)}, u32[]{:S(2)}, u32[]{:S(2)}) %all-to-all-start.1) | async-done | bytes 3145760 | tf_op jit(solution)/shard_map/all_to_all | solution.py:78
  127.2 3.8 %copy.142 = bf16[768,16,4,32]{0,3,2,1:T(8,128)(2,1)} copy(bf16[768,16,4,32]{0,3,1,2:T(8,128)(2,1)} %bitcast.27) | data formatting | bytes 6291456 | tf_op jit(solution)/shard_map/all_to_all | solution.py:78
  131.0 6.5 %copy.150 = f32[768,16,128]{0,2,1:T(8,128)} copy(f32[768,16,128]{2,0,1:T(8,128)} %add_bitcast_fusion) | data formatting | bytes 12582912 | tf_op jit(solution)/shard_map/optimization_barrier | solution.py:98
  137.6 4.8 %fusion.24 = f32[16,128,128]{2,1,0:T(8,128)} fusion(bf16[768,16,128]{0,2,1:T(8,128)(2,1)} %bitcast.163, bf16[768,2048]{1,0:T(8,128)(2,1)} %param.11), kind=kOutput, calls=%fused_computation.36 | convolution fusion | flops 402653184 | bytes 7340032 | tf_op jit(solution)/shard_map/tkc,tkm->kcm/dot_general | solution.py:99
  142.4 9.3 %all-to-all-start.2 = ((f32[32,64,128]{2,1,0:T(8,128)}), f32[32,64,128]{2,1,0:T(8,128)S(1)}, u32[]{:S(2)}, u32[]{:S(2)}) async-start(f32[32,64,128]{2,1,0:T(8,128)} %bitcast.171), calls=%async_computation.2 | async-start | bytes 2097152 | tf_op jit(solution)/shard_map/all_to_all | solution.py:36
  151.8 3.3 %collective-permute-start.2 = (f32[512,128]{0,1:T(8,128)S(1)}, f32[512,128]{0,1:T(8,128)S(1)}, u32[]{:S(2)}, u32[]{:S(2)}) collective-permute-start(f32[512,128]{0,1:T(8,128)S(1)} %slice_select_fusion.1), channel_id=1, source_target_pairs={{0,8},{4,12},{8,0},{12,4},{16,24},{20,28},{24,16},{28,20},{32,40},... | collective-permute-start | bytes 786440 | tf_op jit(solution)/shard_map/ppermute | solution.py:22
  155.1 4.6 %fusion.9 = f32[768]{0:T(1024)S(1)} fusion(bf16[768,2048]{0,1:T(8,128)(2,1)} %copy.120, f32[768,16,128]{0,2,1:T(8,128)} %copy.150, f32[2048]{0:T(1024)S(1)} %copy-done.9), kind=kLoop, calls=%fused_computation.12 | loop fusion | flops 6290688 | bytes 9448448 | tf_op jit(solution)/shard_map/reduce_sum | solution.py:105
  159.8 9.0 %psum.15 = f32[768]{0:T(1024)S(1)} all-reduce(f32[768]{0:T(1024)S(1)} %fusion.9), channel_id=1, replica_groups=mesh['dp'=32,'mp'=4] {'mp'}, use_global_device_ids=true, to_apply=%region_4.5 | all-reduce | flops 768 | bytes 6144 | tf_op jit(solution)/shard_map/psum | solution.py:105
  175.0 3.4 %collective-permute-done.3 = f32[256,128]{0,1:T(8,128)S(1)} collective-permute-done((f32[256,128]{0,1:T(8,128)S(1)}, f32[256,128]{0,1:T(8,128)S(1)}, u32[]{:S(2)}, u32[]{:S(2)}) %collective-permute-start.3) | collective-permute-done | bytes 131104 | tf_op jit(solution)/shard_map/ppermute | solution.py:22
  179.2 6.8 %fusion.7 = bf16[768,2048]{0,1:T(8,128)(2,1)} fusion(bf16[768,2048]{0,1:T(8,128)(2,1)} %copy.120, bf16[768,2048]{0,1:T(8,128)(2,1)} %copy.149, f32[768,16,128]{0,2,1:T(8,128)} %copy.150, f32[768]{0:T(1024)S(1)} %broadcast_multiply_fusion, f32[2048]{0:T(1024)S(1)} %copy-done.9, f32[768]{0:T(1024)S(1)} %add_rsqrt_fusion), kind=kLoop, calls=%fused_computation.10 | loop fusion | flops 15728640 | bytes 15742976 | tf_op jit(solution)/shard_map/convert_element_type | solution.py:109
  187.9 6.6 %all-to-all-start.3 = ((bf16[32,192,128]{2,1,0:T(8,128)(2,1)}), bf16[32,192,128]{2,1,0:T(8,128)(2,1)S(1)}, u32[]{:S(2)}, u32[]{:S(2)}) async-start(bf16[32,192,128]{2,1,0:T(8,128)(2,1)} %broadcast_in_dim.2), calls=%async_computation.3 | async-start | bytes 3145728 | tf_op jit(solution)/shard_map/all_to_all | solution.py:43
  194.5 4.6 %copy.153 = bf16[768,2048]{1,0:T(8,128)(2,1)} copy(bf16[768,2048]{0,1:T(8,128)(2,1)} %fusion.7) | data formatting | bytes 6291456
  199.1 16.3 %all-to-all-done.3 = bf16[32,192,128]{2,1,0:T(8,128)(2,1)S(1)} async-done(((bf16[32,192,128]{2,1,0:T(8,128)(2,1)}), bf16[32,192,128]{2,1,0:T(8,128)(2,1)S(1)}, u32[]{:S(2)}, u32[]{:S(2)}) %all-to-all-start.3) | async-done | bytes 1572896 | tf_op jit(solution)/shard_map/all_to_all | solution.py:43
  (68 shorter events, 47.0 us)
Async XLA Ops:
  0.6 15.6 %copy-start = (bf16[16,128,128]{2,1,0:T(8,128)(2,1)S(1)}, bf16[16,128,128]{2,1,0:T(8,128)(2,1)}, u32[]{:S(2)}) copy-start(bf16[16,128,128]{2,1,0:T(8,128)(2,1)} %param.10) | copy-start | bytes 1572868
  22.5 6.9 %copy-start.7 = (bf16[16,128,128]{2,1,0:T(8,128)(2,1)S(1)}, bf16[16,128,128]{2,1,0:T(8,128)(2,1)}, u32[]{:S(2)}) copy-start(bf16[16,128,128]{2,1,0:T(8,128)(2,1)} %param.9) | copy-start | bytes 1572868
  22.5 7.5 %copy-start.8 = (bf16[16,128,128]{2,1,0:T(8,128)(2,1)S(1)}, bf16[16,128,128]{2,1,0:T(8,128)(2,1)}, u32[]{:S(2)}) copy-start(bf16[16,128,128]{2,1,0:T(8,128)(2,1)} %param.8) | copy-start | bytes 1572868
  22.5 42.2 %all-to-all-start = ((bf16[768,16,128]{0,1,2:T(8,128)(2,1)}), bf16[768,16,128]{0,1,2:T(8,128)(2,1)}, u32[]{:S(2)}, u32[]{:S(2)}) async-start(bf16[768,16,128]{0,1,2:T(8,128)(2,1)} %copy.129), calls=%async_computation | async-start | bytes 6291456 | tf_op jit(solution)/shard_map/all_to_all | solution.py:76
  29.4 1.3 copy-start.9
  33.4 1.6 copy-start.2
  68.6 3.9 %copy-start.3 = (bf16[768,2048]{0,1:T(8,128)(2,1)S(1)}, bf16[768,2048]{0,1:T(8,128)(2,1)}, u32[]{:S(2)}) copy-start(bf16[768,2048]{0,1:T(8,128)(2,1)} %copy-done.2) | copy-start | bytes 9437188
  74.9 4.7 %copy-start.4 = (bf16[768,16,128]{0,2,1:T(8,128)(2,1)}, bf16[768,16,128]{0,2,1:T(8,128)(2,1)S(1)}, u32[]{:S(2)}) copy-start(bf16[768,16,128]{0,2,1:T(8,128)(2,1)S(1)} %get-tuple-element.40) | copy-start | bytes 9437188
  77.9 1.7 copy-start.5
  82.5 25.2 %collective-permute-start = (f32[2048,128]{0,1:T(8,128)}, f32[2048,128]{0,1:T(8,128)S(1)}, u32[]{:S(2)}, u32[]{:S(2)}) collective-permute-start(f32[2048,128]{0,1:T(8,128)} %bitcast.144), channel_id=1, source_target_pairs={{0,4},{4,0},{8,12},{12,8},{16,20},{20,16},{24,28},{28,24},{32,36},... | collective-permute-start | bytes 3145736 | tf_op jit(solution)/shard_map/ppermute | solution.py:22
  84.1 43.2 %all-to-all-start.1 = ((bf16[768,64,32]{0,2,1:T(8,128)(2,1)}), bf16[768,64,32]{0,2,1:T(8,128)(2,1)}, u32[]{:S(2)}, u32[]{:S(2)}) async-start(bf16[768,64,32]{0,2,1:T(8,128)(2,1)} %copy.168), calls=%async_computation.1 | async-start | bytes 6291456 | tf_op jit(solution)/shard_map/all_to_all | solution.py:78
  100.1 10.8 %copy-start.6 = (bf16[768,16,128]{0,2,1:T(8,128)(2,1)S(1)}, bf16[768,16,128]{0,2,1:T(8,128)(2,1)}, u32[]{:S(2)}) copy-start(bf16[768,16,128]{0,2,1:T(8,128)(2,1)} %copy-done.5) | copy-start | bytes 9437188
  109.0 42.7 %collective-permute-start.1 = (f32[1024,128]{0,1:T(8,128)}, f32[1024,128]{0,1:T(8,128)S(1)}, u32[]{:S(2)}, u32[]{:S(2)}) collective-permute-start(f32[1024,128]{0,1:T(8,128)} %slice_select_fusion), channel_id=1, source_target_pairs={{0,16},{4,20},{8,24},{12,28},{16,0},{20,4},{24,8},{28,12},{32,48},... | collective-permute-start | bytes 1572872 | tf_op jit(solution)/shard_map/ppermute | solution.py:22
  142.4 43.6 %all-to-all-start.2 = ((f32[32,64,128]{2,1,0:T(8,128)}), f32[32,64,128]{2,1,0:T(8,128)S(1)}, u32[]{:S(2)}, u32[]{:S(2)}) async-start(f32[32,64,128]{2,1,0:T(8,128)} %bitcast.171), calls=%async_computation.2 | async-start | bytes 2097152 | tf_op jit(solution)/shard_map/all_to_all | solution.py:36
  151.8 20.0 %collective-permute-start.2 = (f32[512,128]{0,1:T(8,128)S(1)}, f32[512,128]{0,1:T(8,128)S(1)}, u32[]{:S(2)}, u32[]{:S(2)}) collective-permute-start(f32[512,128]{0,1:T(8,128)S(1)} %slice_select_fusion.1), channel_id=1, source_target_pairs={{0,8},{4,12},{8,0},{12,4},{16,24},{20,28},{24,16},{28,20},{32,40},... | collective-permute-start | bytes 786440 | tf_op jit(solution)/shard_map/ppermute | solution.py:22
  171.9 6.6 %collective-permute-start.3 = (f32[256,128]{0,1:T(8,128)S(1)}, f32[256,128]{0,1:T(8,128)S(1)}, u32[]{:S(2)}, u32[]{:S(2)}) collective-permute-start(f32[256,128]{0,1:T(8,128)S(1)} %slice_select_fusion.2), channel_id=1, source_target_pairs={{0,32},{4,36},{8,40},{12,44},{16,48},{20,52},{24,56},{28,60},{32,0... | collective-permute-start | bytes 393224 | tf_op jit(solution)/shard_map/ppermute | solution.py:22
  178.5 7.7 %collective-permute-start.4 = (f32[128,128]{0,1:T(8,128)S(1)}, f32[128,128]{0,1:T(8,128)S(1)}, u32[]{:S(2)}, u32[]{:S(2)}) collective-permute-start(f32[128,128]{0,1:T(8,128)S(1)} %slice_select_fusion.3), channel_id=1, source_target_pairs={{0,64},{4,68},{8,72},{12,76},{16,80},{20,84},{24,88},{28,92},{32,9... | collective-permute-start | bytes 196616 | tf_op jit(solution)/shard_map/ppermute | solution.py:22
  187.9 27.6 %all-to-all-start.3 = ((bf16[32,192,128]{2,1,0:T(8,128)(2,1)}), bf16[32,192,128]{2,1,0:T(8,128)(2,1)S(1)}, u32[]{:S(2)}, u32[]{:S(2)}) async-start(bf16[32,192,128]{2,1,0:T(8,128)(2,1)} %broadcast_in_dim.2), calls=%async_computation.3 | async-start | bytes 3145728 | tf_op jit(solution)/shard_map/all_to_all | solution.py:43
  215.5 2.8 %copy-start.1 = (bf16[16,128,128]{2,1,0:T(8,128)(2,1)S(1)}, bf16[16,128,128]{2,1,0:T(8,128)(2,1)}, u32[]{:S(2)}) copy-start(bf16[16,128,128]{2,1,0:T(8,128)(2,1)} %param.10) | copy-start | bytes 1572868

commit v4 on v3

--- a/solution.py
+++ b/solution.py
@@ -94,8 +94,10 @@
     grad_norm = grad_norm + jnp.einsum(
         "tij,icj->tic", grad_g, gate_p, preferred_element_type=jnp.float32
     )
+    permuted, left_local, gate_local, grad_norm = lax.optimization_barrier(
+        (permuted, left_local, gate_local, grad_norm)
+    )
     lg_mine = dp_halving_sum(jnp.concatenate([left_local.reshape(-1, BLOCK), gate_local.reshape(-1, BLOCK)]))
-    permuted, grad_norm = lax.optimization_barrier((permuted, grad_norm))
     right_local = jnp.einsum(
         "tkc,tkm->kcm", permuted, cot_blocks, preferred_element_type=jnp.float32
     )

time: 221 us -> 235 us (1.063)
  waiting for transfers between devices: 67 us -> 83 us
    ppermute x5, waiting for transfers between devices: 14 us -> 30.3 us  [dp_halving_sum(): lax.ppermute(send, 'dp', [(i, i ^ 1 << b) for i in range(ndp)])]
    unnamed x26 -> x24, local copies, waits for them, and re-layouts: 17.6 us -> 17.9 us
  transfers between devices with their start and end apart: 9 -> 9, of which waited for: 6 -> 6; matrix products, arithmetic and copies ran while one was open for 25% -> 28% of each run, Pallas kernels for 0% -> 0%
where the time goes in v4:
time: 235 us; the launch traced here: 232 us
  waiting for transfers between devices  83 us (35%)
  local copies, waits for them, and re-layouts  47.7 us (20%)
  starting transfers between devices  40.6 us (17%)
  matrix products  23.1 us (10%)
  other arithmetic  21.1 us (9%)
  blocking collectives  16 us (7%)
    ppermute x5, waiting for transfers between devices, dp_halving_sum(): lax.ppermute(send, 'dp', [(i, i ^ 1 << b) for i in range(ndp)])  30.3 us
    all_to_all x1, waiting for transfers between devices, body(): lax.all_to_all(grad_perm, 'mp', split_axis=2, concat_axis=1, tiled=True)  24.3 us
    unnamed x24, local copies, waits for them, and re-layouts  17.9 us
    all_to_all x1, waiting for transfers between devices, dp_all_gather(): return lax.all_to_all(copies, 'dp', 0, 0, tiled=True)  15.2 us
    all_to_all x1, waiting for transfers between devices, body(): lax.all_to_all(outgoing, 'mp', split_axis=1, concat_axis=2, tiled=True)  13.3 us
    ppermute x5, starting transfers between devices, dp_halving_sum(): lax.ppermute(send, 'dp', [(i, i ^ 1 << b) for i in range(ndp)])  10.9 us
    all_to_all x1, starting transfers between devices, dp_reduce_scatter(): got = lax.all_to_all(flat, 'dp', 0, 0, tiled=True)  9.12 us
    psum x1, blocking collectives, body(): squares = lax.psum(jnp.sum(xf * xf, axis=1), 'mp')  8.3 us
  transfers between devices with their start and end apart: 9, of which 6 were waited for; matrix products, arithmetic and copies ran while one was open for 28% of the time, Pallas kernels for 0%

profile of v4, /device:TPU:6, one launch (start us, length us, event | category | flops | bytes accessed | tf_op | source)
XLA Modules:
  0.0 232.5 jit_solution(5899026876289571379)
XLA Ops:
  0.6 4.7 %copy.120 = bf16[768,2048]{0,1:T(8,128)(2,1)} copy(bf16[768,2048]{1,0:T(8,128)(2,1)} %param.6) | data formatting | bytes 6291456 | tf_op args[0]
  7.9 8.3 %psum.14 = f32[768]{0:T(1024)S(1)} all-reduce(f32[768]{0:T(1024)S(1)} %fusion.8), channel_id=1, replica_groups=mesh['dp'=32,'mp'=4] {'mp'}, use_global_device_ids=true, to_apply=%region_1.0 | all-reduce | flops 768 | bytes 6144 | tf_op jit(solution)/shard_map/psum | solution.py:64
  19.1 3.5 %copy.130 = bf16[768,16,128]{0,1,2:T(8,128)(2,1)} copy(bf16[768,16,128]{0,2,1:T(8,128)(2,1)S(1)} %convert_bitcast_fusion.1) | data formatting | bytes 6291456 | tf_op jit(solution)/shard_map/optimization_barrier | solution.py:65
  22.6 6.9 %all-to-all-start.1 = ((bf16[768,16,128]{0,1,2:T(8,128)(2,1)}), bf16[768,16,128]{0,1,2:T(8,128)(2,1)}, u32[]{:S(2)}, u32[]{:S(2)}) async-start(bf16[768,16,128]{0,1,2:T(8,128)(2,1)} %copy.130), calls=%async_computation.1 | async-start | bytes 6291456 | tf_op jit(solution)/shard_map/all_to_all | solution.py:76
  37.2 3.4 %copy.168 = bf16[768,64,32]{0,2,1:T(8,128)(2,1)} copy(bf16[768,64,32]{0,1,2:T(8,128)(2,1)S(1)} %bitcast.168) | data formatting | bytes 6291456 | tf_op jit(solution)/shard_map/reshape | solution.py:74
  40.6 24.3 %all-to-all-done.1 = bf16[768,16,128]{0,1,2:T(8,128)(2,1)} async-done(((bf16[768,16,128]{0,1,2:T(8,128)(2,1)}), bf16[768,16,128]{0,1,2:T(8,128)(2,1)}, u32[]{:S(2)}, u32[]{:S(2)}) %all-to-all-start.1) | async-done | bytes 3145760 | tf_op jit(solution)/shard_map/all_to_all | solution.py:76
  64.8 7.8 %all-to-all-start = ((bf16[768,64,32]{0,2,1:T(8,128)(2,1)}), bf16[768,64,32]{0,2,1:T(8,128)(2,1)}, u32[]{:S(2)}, u32[]{:S(2)}) async-start(bf16[768,64,32]{0,2,1:T(8,128)(2,1)} %copy.168), calls=%async_computation | async-start | bytes 6291456 | tf_op jit(solution)/shard_map/all_to_all | solution.py:78
  76.4 3.6 %copy.132 = f32[768,4,16,32]{0,2,1,3:T(8,128)S(1)} copy(f32[768,4,16,32]{0,3,1,2:T(8,128)S(1)} %convert_bitcast_fusion) | data formatting | bytes 12582912 | tf_op jit(solution)/shard_map/convert_element_type | solution.py:86
  90.9 3.8 %add_bitcast_fusion = f32[768,16,128]{2,0,1:T(8,128)} fusion(f32[16,768,128]{2,1,0:T(8,128)S(1)} %fusion.35, bf16[768,16,128]{0,2,1:T(8,128)(2,1)S(1)} %fusion.12, bf16[16,128,128]{1,2,0:T(8,128)(2,1)S(1)} %bitcast.159), kind=kOutput, calls=%fused_computation.34 | convolution fusion | flops 404226048 | bytes 16252928 | tf_op jit(solution)/shard_map/tij,icj->tic/dot_general | solution.py:94
  94.7 13.3 %all-to-all-done = bf16[768,64,32]{0,2,1:T(8,128)(2,1)} async-done(((bf16[768,64,32]{0,2,1:T(8,128)(2,1)}), bf16[768,64,32]{0,2,1:T(8,128)(2,1)}, u32[]{:S(2)}, u32[]{:S(2)}) %all-to-all-start) | async-done | bytes 3145760 | tf_op jit(solution)/shard_map/all_to_all | solution.py:78
  108.0 3.9 %copy.129 = bf16[768,16,4,32]{0,3,2,1:T(8,128)(2,1)} copy(bf16[768,16,4,32]{0,3,1,2:T(8,128)(2,1)} %bitcast.14) | data formatting | bytes 6291456 | tf_op jit(solution)/shard_map/all_to_all | solution.py:78
  114.9 23.5 %collective-permute-done = f32[2048,128]{0,1:T(8,128)S(1)} collective-permute-done((f32[2048,128]{0,1:T(8,128)}, f32[2048,128]{0,1:T(8,128)S(1)}, u32[]{:S(2)}, u32[]{:S(2)}) %collective-permute-start) | collective-permute-done | bytes 1048608 | tf_op jit(solution)/shard_map/ppermute | solution.py:22
  143.1 4.7 %copy.149 = bf16[768,2048]{0,1:T(8,128)(2,1)} copy(bf16[768,2048]{1,0:T(8,128)(2,1)} %param.11) | data formatting | bytes 6291456 | tf_op args[5]
  147.8 6.6 %copy.150 = f32[768,16,128]{0,2,1:T(8,128)} copy(f32[768,16,128]{2,0,1:T(8,128)} %add_bitcast_fusion) | data formatting | bytes 12582912 | tf_op jit(solution)/shard_map/optimization_barrier | solution.py:97
  154.4 4.8 %fusion.24 = f32[16,128,128]{2,1,0:T(8,128)} fusion(bf16[768,16,128]{0,2,1:T(8,128)(2,1)} %bitcast.167, bf16[768,2048]{1,0:T(8,128)(2,1)} %param.11), kind=kOutput, calls=%fused_computation.36 | convolution fusion | flops 402653184 | bytes 7340032 | tf_op jit(solution)/shard_map/tkc,tkm->kcm/dot_general | solution.py:101
  159.2 9.1 %all-to-all-start.2 = ((f32[32,64,128]{2,1,0:T(8,128)}), f32[32,64,128]{2,1,0:T(8,128)S(1)}, u32[]{:S(2)}, u32[]{:S(2)}) async-start(f32[32,64,128]{2,1,0:T(8,128)} %bitcast.175), calls=%async_computation.2 | async-start | bytes 2097152 | tf_op jit(solution)/shard_map/all_to_all | solution.py:36
  171.5 4.6 %fusion.9 = f32[768]{0:T(1024)S(1)} fusion(bf16[768,2048]{0,1:T(8,128)(2,1)} %copy.120, f32[768,16,128]{0,2,1:T(8,128)} %copy.150, f32[2048]{0:T(1024)S(1)} %copy-done.8), kind=kLoop, calls=%fused_computation.12 | loop fusion | flops 6290688 | bytes 9448448 | tf_op jit(solution)/shard_map/reduce_sum | solution.py:107
  176.2 7.7 %psum.15 = f32[768]{0:T(1024)S(1)} all-reduce(f32[768]{0:T(1024)S(1)} %fusion.9), channel_id=1, replica_groups=mesh['dp'=32,'mp'=4] {'mp'}, use_global_device_ids=true, to_apply=%region_4.5 | all-reduce | flops 768 | bytes 6144 | tf_op jit(solution)/shard_map/psum | solution.py:107
  183.8 3.3 %collective-permute-done.2 = f32[512,128]{0,1:T(8,128)S(1)} collective-permute-done((f32[512,128]{0,1:T(8,128)S(1)}, f32[512,128]{0,1:T(8,128)S(1)}, u32[]{:S(2)}, u32[]{:S(2)}) %collective-permute-start.2) | collective-permute-done | bytes 262176 | tf_op jit(solution)/shard_map/ppermute | solution.py:22
  190.4 3.4 %collective-permute-done.3 = f32[256,128]{0,1:T(8,128)S(1)} collective-permute-done((f32[256,128]{0,1:T(8,128)S(1)}, f32[256,128]{0,1:T(8,128)S(1)}, u32[]{:S(2)}, u32[]{:S(2)}) %collective-permute-start.3) | collective-permute-done | bytes 131104 | tf_op jit(solution)/shard_map/ppermute | solution.py:22
  195.0 6.8 %fusion.7 = bf16[768,2048]{0,1:T(8,128)(2,1)} fusion(bf16[768,2048]{0,1:T(8,128)(2,1)} %copy.120, bf16[768,2048]{0,1:T(8,128)(2,1)} %copy.149, f32[768,16,128]{0,2,1:T(8,128)} %copy.150, f32[768]{0:T(1024)S(1)} %broadcast_multiply_fusion, f32[2048]{0:T(1024)S(1)} %copy-done.8, f32[768]{0:T(1024)S(1)} %add_rsqrt_fusion), kind=kLoop, calls=%fused_computation.10 | loop fusion | flops 15728640 | bytes 15742976 | tf_op jit(solution)/shard_map/convert_element_type | solution.py:111
  203.7 6.0 %all-to-all-start.3 = ((bf16[32,192,128]{2,1,0:T(8,128)(2,1)}), bf16[32,192,128]{2,1,0:T(8,128)(2,1)S(1)}, u32[]{:S(2)}, u32[]{:S(2)}) async-start(bf16[32,192,128]{2,1,0:T(8,128)(2,1)} %broadcast_in_dim.2), calls=%async_computation.3 | async-start | bytes 3145728 | tf_op jit(solution)/shard_map/all_to_all | solution.py:43
  209.7 4.6 %copy.153 = bf16[768,2048]{1,0:T(8,128)(2,1)} copy(bf16[768,2048]{0,1:T(8,128)(2,1)} %fusion.7) | data formatting | bytes 6291456
  214.3 15.2 %all-to-all-done.3 = bf16[32,192,128]{2,1,0:T(8,128)(2,1)S(1)} async-done(((bf16[32,192,128]{2,1,0:T(8,128)(2,1)}), bf16[32,192,128]{2,1,0:T(8,128)(2,1)S(1)}, u32[]{:S(2)}, u32[]{:S(2)}) %all-to-all-start.3) | async-done | bytes 1572896 | tf_op jit(solution)/shard_map/all_to_all | solution.py:43
  (67 shorter events, 47.7 us)
Async XLA Ops:
  0.6 15.6 %copy-start = (bf16[16,128,128]{2,1,0:T(8,128)(2,1)S(1)}, bf16[16,128,128]{2,1,0:T(8,128)(2,1)}, u32[]{:S(2)}) copy-start(bf16[16,128,128]{2,1,0:T(8,128)(2,1)} %param.10) | copy-start | bytes 1572868
  22.6 6.9 %copy-start.6 = (bf16[16,128,128]{2,1,0:T(8,128)(2,1)S(1)}, bf16[16,128,128]{2,1,0:T(8,128)(2,1)}, u32[]{:S(2)}) copy-start(bf16[16,128,128]{2,1,0:T(8,128)(2,1)} %param.9) | copy-start | bytes 1572868
  22.6 7.5 %copy-start.7 = (bf16[16,128,128]{2,1,0:T(8,128)(2,1)S(1)}, bf16[16,128,128]{2,1,0:T(8,128)(2,1)}, u32[]{:S(2)}) copy-start(bf16[16,128,128]{2,1,0:T(8,128)(2,1)} %param.8) | copy-start | bytes 1572868
  22.6 42.2 %all-to-all-start.1 = ((bf16[768,16,128]{0,1,2:T(8,128)(2,1)}), bf16[768,16,128]{0,1,2:T(8,128)(2,1)}, u32[]{:S(2)}, u32[]{:S(2)}) async-start(bf16[768,16,128]{0,1,2:T(8,128)(2,1)} %copy.130), calls=%async_computation.1 | async-start | bytes 6291456 | tf_op jit(solution)/shard_map/all_to_all | solution.py:76
  29.4 1.3 copy-start.8
  33.4 1.7 copy-start.2
  64.8 43.2 %all-to-all-start = ((bf16[768,64,32]{0,2,1:T(8,128)(2,1)}), bf16[768,64,32]{0,2,1:T(8,128)(2,1)}, u32[]{:S(2)}, u32[]{:S(2)}) async-start(bf16[768,64,32]{0,2,1:T(8,128)(2,1)} %copy.168), calls=%async_computation | async-start | bytes 6291456 | tf_op jit(solution)/shard_map/all_to_all | solution.py:78
  76.4 3.7 %copy-start.3 = (bf16[768,2048]{0,1:T(8,128)(2,1)S(1)}, bf16[768,2048]{0,1:T(8,128)(2,1)}, u32[]{:S(2)}) copy-start(bf16[768,2048]{0,1:T(8,128)(2,1)} %copy-done.2) | copy-start | bytes 9437188
  108.0 3.9 %copy-start.4 = (f32[16,128,2,64]{1,0,2,3:T(8,128)S(1)}, f32[16,128,2,64]{1,0,2,3:T(8,128)}, u32[]{:S(2)}) copy-start(f32[16,128,2,64]{1,0,2,3:T(8,128)} %copy.137) | copy-start | bytes 3145732
  113.3 25.1 %collective-permute-start = (f32[2048,128]{0,1:T(8,128)}, f32[2048,128]{0,1:T(8,128)S(1)}, u32[]{:S(2)}, u32[]{:S(2)}) collective-permute-start(f32[2048,128]{0,1:T(8,128)} %bitcast.146), channel_id=1, source_target_pairs={{0,4},{4,0},{8,12},{12,8},{16,20},{20,16},{24,28},{28,24},{32,36},... | collective-permute-start | bytes 3145736 | tf_op jit(solution)/shard_map/ppermute | solution.py:22
  138.4 1.0 copy-start.5
  141.1 27.2 %collective-permute-start.1 = (f32[1024,128]{0,1:T(8,128)S(1)}, f32[1024,128]{0,1:T(8,128)S(1)}, u32[]{:S(2)}, u32[]{:S(2)}) collective-permute-start(f32[1024,128]{0,1:T(8,128)S(1)} %slice_select_fusion), channel_id=1, source_target_pairs={{0,16},{4,20},{8,24},{12,28},{16,0},{20,4},{24,8},{28,12},{32,48},... | collective-permute-start | bytes 1572872 | tf_op jit(solution)/shard_map/ppermute | solution.py:22
  159.2 42.6 %all-to-all-start.2 = ((f32[32,64,128]{2,1,0:T(8,128)}), f32[32,64,128]{2,1,0:T(8,128)S(1)}, u32[]{:S(2)}, u32[]{:S(2)}) async-start(f32[32,64,128]{2,1,0:T(8,128)} %bitcast.175), calls=%async_computation.2 | async-start | bytes 2097152 | tf_op jit(solution)/shard_map/all_to_all | solution.py:36
  168.5 18.7 %collective-permute-start.2 = (f32[512,128]{0,1:T(8,128)S(1)}, f32[512,128]{0,1:T(8,128)S(1)}, u32[]{:S(2)}, u32[]{:S(2)}) collective-permute-start(f32[512,128]{0,1:T(8,128)S(1)} %slice_select_fusion.1), channel_id=1, source_target_pairs={{0,8},{4,12},{8,0},{12,4},{16,24},{20,28},{24,16},{28,20},{32,40},... | collective-permute-start | bytes 786440 | tf_op jit(solution)/shard_map/ppermute | solution.py:22
  187.3 6.6 %collective-permute-start.3 = (f32[256,128]{0,1:T(8,128)S(1)}, f32[256,128]{0,1:T(8,128)S(1)}, u32[]{:S(2)}, u32[]{:S(2)}) collective-permute-start(f32[256,128]{0,1:T(8,128)S(1)} %slice_select_fusion.2), channel_id=1, source_target_pairs={{0,32},{4,36},{8,40},{12,44},{16,48},{20,52},{24,56},{28,60},{32,0... | collective-permute-start | bytes 393224 | tf_op jit(solution)/shard_map/ppermute | solution.py:22
  193.9 8.2 %collective-permute-start.4 = (f32[128,128]{0,1:T(8,128)S(1)}, f32[128,128]{0,1:T(8,128)S(1)}, u32[]{:S(2)}, u32[]{:S(2)}) collective-permute-start(f32[128,128]{0,1:T(8,128)S(1)} %slice_select_fusion.3), channel_id=1, source_target_pairs={{0,64},{4,68},{8,72},{12,76},{16,80},{20,84},{24,88},{28,92},{32,9... | collective-permute-start | bytes 196616 | tf_op jit(solution)/shard_map/ppermute | solution.py:22
  203.7 25.8 %all-to-all-start.3 = ((bf16[32,192,128]{2,1,0:T(8,128)(2,1)}), bf16[32,192,128]{2,1,0:T(8,128)(2,1)S(1)}, u32[]{:S(2)}, u32[]{:S(2)}) async-start(bf16[32,192,128]{2,1,0:T(8,128)(2,1)} %broadcast_in_dim.2), calls=%async_computation.3 | async-start | bytes 3145728 | tf_op jit(solution)/shard_map/all_to_all | solution.py:43
  229.6 2.8 %copy-start.1 = (bf16[16,128,128]{2,1,0:T(8,128)(2,1)S(1)}, bf16[16,128,128]{2,1,0:T(8,128)(2,1)}, u32[]{:S(2)}) copy-start(bf16[16,128,128]{2,1,0:T(8,128)(2,1)} %param.10) | copy-start | bytes 1572868

commit v5 on v1

--- a/solution.py
+++ b/solution.py
@@ -45,7 +45,6 @@
         "tkm,kcm->tkc", cot_blocks, right_blocks, preferred_element_type=jnp.float32
     ).astype(jnp.bfloat16)
     squares = lax.psum(jnp.sum(xf * xf, axis=1), "mp")
-    grad_perm, squares = lax.optimization_barrier((grad_perm, squares))
     rstd = lax.rsqrt(squares / W + 1e-05)[:, None]
     xn = (xf * rstd * gain).astype(jnp.bfloat16).reshape(rows, nlocal, BLOCK)
     left_p = pair_major(left_blocks)

time: 212 us -> 216 us (1.019)
  blocking collectives: 32 us -> 60.4 us
  waiting for transfers between devices: 55.6 us -> 28.8 us
  local copies, waits for them, and re-layouts: 44.3 us -> 51 us
  other arithmetic: 23.2 us -> 19.5 us
  starting transfers between devices: 32.4 us -> 28.7 us
  matrix products: 22.2 us -> 25.4 us
    psum x1, blocking collectives: 8.3 us -> 35.7 us  [body(): squares = lax.psum(jnp.sum(xf * xf, axis=1), 'mp')]
    all_to_all x1, waiting for transfers between devices: 24.3 us -> 0.01 us  [body(): lax.all_to_all(grad_perm, 'mp', split_axis=2, concat_axis=1, tiled=True)]
    unnamed x21 -> x27, local copies, waits for them, and re-layouts: 15.6 us -> 20.2 us
    optimization_barrier x1 -> x0, local copies, waits for them, and re-layouts: 3.45 us -> none  [body(): grad_perm, squares = lax.optimization_barrier((grad_perm, squares))]
    convert_element_type x0 -> x1, local copies, waits for them, and re-layouts: none -> 3.41 us  [body(): grad_perm = jnp.einsum('tkm,kcm->tkc', cot_blocks, right_blocks, preferre...]
    reshape x2, local copies, waits for them, and re-layouts: 1.81 us -> 5.1 us  [dp_reduce_scatter(): p.reshape(-1, BLOCK)]
    convert_element_type x1, local copies, waits for them, and re-layouts: 3.64 us -> 0.52 us  [body(): grad_gated = returned.reshape(rows, NBLK, nlocal, 2).transpose(0, 2, 3, 1...]
    all_to_all x1 -> x0, local copies, waits for them, and re-layouts: 2.89 us -> none  [body(): lax.all_to_all(grad_perm, 'mp', split_axis=2, concat_axis=1, tiled=True)]
  transfers between devices with their start and end apart: 4 -> 4, of which waited for: 3 -> 2; matrix products, arithmetic and copies ran while one was open for 28% -> 31% of each run, Pallas kernels for 0% -> 0%
where the time goes in v5:
time: 216 us; the launch traced here: 215 us
  blocking collectives  60.4 us (28%)
  local copies, waits for them, and re-layouts  51 us (24%)
  waiting for transfers between devices  28.8 us (13%)
  starting transfers between devices  28.7 us (13%)
  matrix products  25.4 us (12%)
  other arithmetic  19.5 us (9%)
    psum x1, blocking collectives, body(): squares = lax.psum(jnp.sum(xf * xf, axis=1), 'mp')  35.7 us
    psum x1, blocking collectives, body(): inner = lax.psum(jnp.sum(scaled * xf, axis=1), 'mp')  24.7 us
    unnamed x27, local copies, waits for them, and re-layouts  20.2 us
    all_to_all x1, waiting for transfers between devices, dp_all_gather(): lax.all_to_all(copies, 'dp', 0, 0, tiled=True).reshape(-1, BLOCK, BLOCK)  17 us
    all_to_all x1, waiting for transfers between devices, body(): lax.all_to_all(outgoing, 'mp', split_axis=1, concat_axis=2, tiled=True)  11.8 us
    all_to_all x1, starting transfers between devices, dp_reduce_scatter(): got = lax.all_to_all(flat, 'dp', 0, 0, tiled=True)  9.63 us
    all_to_all x1, starting transfers between devices, dp_all_gather(): lax.all_to_all(copies, 'dp', 0, 0, tiled=True).reshape(-1, BLOCK, BLOCK)  8.08 us
    optimization_barrier x1, local copies, waits for them, and re-layouts, body(): lax.optimization_barrier((permuted, left_local, gate_local, grad_norm))  6.55 us
  transfers between devices with their start and end apart: 4, of which 2 were waited for; matrix products, arithmetic and copies ran while one was open for 31% of the time, Pallas kernels for 0%

profile of v5, /device:TPU:6, one launch (start us, length us, event | category | flops | bytes accessed | tf_op | source)
XLA Modules:
  0.0 214.8 jit_solution(11168735633496494769)
XLA Ops:
  1.7 2.9 %convert_bitcast_fusion.1 = bf16[768,16,128]{0,2,1:T(8,128)(2,1)S(1)} fusion(bf16[16,128,128]{2,1,0:T(8,128)(2,1)S(1)} %copy-done, bf16[768,2048]{1,0:T(8,128)(2,1)} %param.11), kind=kOutput, calls=%fused_computation.41 | convolution fusion | flops 404226048 | bytes 6815744 | tf_op jit(solution)/shard_map/tkm,kcm->tkc/dot_general | solution.py:44
  4.6 3.4 %copy.98 = bf16[768,16,128]{0,1,2:T(8,128)(2,1)} copy(bf16[768,16,128]{0,2,1:T(8,128)(2,1)S(1)} %convert_bitcast_fusion.1) | data formatting | bytes 6291456 | tf_op jit(solution)/shard_map/convert_element_type | solution.py:46
  8.0 6.0 %all-to-all-start.1 = ((bf16[768,16,128]{0,1,2:T(8,128)(2,1)}), bf16[768,16,128]{0,1,2:T(8,128)(2,1)}, u32[]{:S(2)}, u32[]{:S(2)}) async-start(bf16[768,16,128]{0,1,2:T(8,128)(2,1)} %copy.98), calls=%async_computation.1 | async-start | bytes 6291456 | tf_op jit(solution)/shard_map/all_to_all | solution.py:58
  14.0 3.2 %copy.88 = bf16[768,2048]{0,1:T(8,128)(2,1)S(1)} copy(bf16[768,2048]{1,0:T(8,128)(2,1)} %param.6) | data formatting | bytes 6291456 | tf_op args[0]
  17.9 35.7 %psum.14 = f32[768]{0:T(1024)S(1)} all-reduce(f32[768]{0:T(1024)S(1)} %fusion.8), channel_id=1, replica_groups=mesh['dp'=32,'mp'=4] {'mp'}, use_global_device_ids=true, to_apply=%region_1.0 | all-reduce | flops 768 | bytes 6144 | tf_op jit(solution)/shard_map/psum | solution.py:47
  65.9 3.4 %copy.134 = bf16[768,64,32]{0,2,1:T(8,128)(2,1)} copy(bf16[768,64,32]{0,1,2:T(8,128)(2,1)S(1)} %bitcast.151) | data formatting | bytes 6291456 | tf_op jit(solution)/shard_map/reshape | solution.py:56
  69.3 5.0 %all-to-all-start = ((bf16[768,64,32]{0,2,1:T(8,128)(2,1)}), bf16[768,64,32]{0,2,1:T(8,128)(2,1)}, u32[]{:S(2)}, u32[]{:S(2)}) async-start(bf16[768,64,32]{0,2,1:T(8,128)(2,1)} %copy.134), calls=%async_computation | async-start | bytes 6291456 | tf_op jit(solution)/shard_map/all_to_all | solution.py:60
  74.3 2.8 %convert_bitcast_fusion = f32[768,4,16,32]{0,2,3,1:T(8,128)S(1)} fusion(bf16[768,16,4,32]{0,1,3,2:T(8,128)(2,1)} %bitcast.43), kind=kLoop, calls=%fused_computation.13 | loop fusion | flops 1572864 | bytes 9437184 | tf_op jit(solution)/shard_map/convert_element_type | solution.py:68
  79.0 3.9 %fusion.17 = (bf16[768,16,128]{0,2,1:T(8,128)(2,1)S(1)}, f32[16,768,128]{1,2,0:T(8,128)}) fusion(f32[768,16,128]{0,2,1:T(8,128)S(1)} %bitcast.138, bf16[16,128,128]{1,2,0:T(8,128)(2,1)S(1)} %bitcast.142, bf16[768,16,128]{0,2,1:T(8,128)(2,1)S(1)} %bitcast.133), kind=kOutput, calls=%fused_computation.26 | convolution fusion | flops 412090368 | bytes 19398656 | tf_op jit(solution)/shard_map/tic,icj->tij/dot_general | solution.py:62
  82.9 4.9 %fusion.12 = bf16[768,16,128]{0,2,1:T(8,128)(2,1)S(1)} fusion(f32[768,16,128]{0,2,1:T(8,128)S(1)} %bitcast.139, f32[16,768,128]{1,2,0:T(8,128)} %get-tuple-element.36, bf16[16,128,128]{1,2,0:T(8,128)(2,1)S(1)} %bitcast.153, bf16[768,16,128]{0,2,1:T(8,128)(2,1)S(1)} %bitcast.134), kind=kOutput, calls=%fused_computation.18 | convolution fusion | flops 418381824 | bytes 19398656 | tf_op jit(solution)/shard_map/tic,icj->tij/dot_general | solution.py:61
  94.0 3.8 %add_bitcast_fusion = f32[768,16,128]{2,0,1:T(8,128)} fusion(f32[16,768,128]{2,1,0:T(8,128)S(1)} %fusion.34, bf16[768,16,128]{0,2,1:T(8,128)(2,1)S(1)} %fusion.12, bf16[16,128,128]{1,2,0:T(8,128)(2,1)S(1)} %bitcast.143), kind=kOutput, calls=%fused_computation.34 | convolution fusion | flops 404226048 | bytes 16252928 | tf_op jit(solution)/shard_map/tij,icj->tic/dot_general | solution.py:76
  97.8 11.8 %all-to-all-done = bf16[768,64,32]{0,2,1:T(8,128)(2,1)} async-done(((bf16[768,64,32]{0,2,1:T(8,128)(2,1)}), bf16[768,64,32]{0,2,1:T(8,128)(2,1)}, u32[]{:S(2)}, u32[]{:S(2)}) %all-to-all-start) | async-done | bytes 3145760 | tf_op jit(solution)/shard_map/all_to_all | solution.py:60
  109.6 3.8 %copy.96 = bf16[768,16,4,32]{0,3,2,1:T(8,128)(2,1)} copy(bf16[768,16,4,32]{0,3,1,2:T(8,128)(2,1)} %bitcast.13) | data formatting | bytes 6291456 | tf_op jit(solution)/shard_map/all_to_all | solution.py:60
  113.5 2.5 %copy.135 = f32[16,128,128]{2,1,0:T(8,128)} copy(f32[16,128,128]{1,0,2:T(8,128)} %bitcast.147) | data formatting | bytes 2097152 | tf_op jit(solution)/shard_map/reshape | solution.py:13
  118.6 4.0 %fusion.24 = f32[16,128,128]{2,1,0:T(8,128)S(1)} fusion(bf16[768,16,128]{0,2,1:T(8,128)(2,1)} %bitcast.150, bf16[768,2048]{1,0:T(8,128)(2,1)} %param.11), kind=kOutput, calls=%fused_computation.36 | convolution fusion | flops 402653184 | bytes 7340032 | tf_op jit(solution)/shard_map/tkc,tkm->kcm/dot_general | solution.py:82
  124.5 9.6 %all-to-all-start.2 = ((f32[32,192,128]{2,1,0:T(8,128)}), f32[32,192,128]{2,1,0:T(8,128)}, u32[]{:S(2)}, u32[]{:S(2)}) async-start(f32[32,192,128]{2,1,0:T(8,128)} %bitcast.137), calls=%async_computation.2 | async-start | bytes 6291456 | tf_op jit(solution)/shard_map/all_to_all | solution.py:14
  134.1 4.6 %copy.117 = bf16[768,2048]{0,1:T(8,128)(2,1)} copy(bf16[768,2048]{1,0:T(8,128)(2,1)} %param.11) | data formatting | bytes 6291456 | tf_op args[5]
  138.7 6.6 %copy.118 = f32[768,16,128]{0,2,1:T(8,128)} copy(f32[768,16,128]{2,0,1:T(8,128)} %add_bitcast_fusion) | data formatting | bytes 12582912 | tf_op jit(solution)/shard_map/optimization_barrier | solution.py:79
  145.3 3.7 %fusion.9 = f32[768]{0:T(1024)S(1)} fusion(bf16[768,2048]{0,1:T(8,128)(2,1)S(1)} %copy.88, f32[768,16,128]{0,2,1:T(8,128)} %copy.118, f32[2048]{0:T(1024)S(1)} %copy-done.10), kind=kLoop, calls=%fused_computation.12 | loop fusion | flops 6290688 | bytes 9448448 | tf_op jit(solution)/shard_map/reduce_sum | solution.py:88
  149.0 24.7 %psum.15 = f32[768]{0:T(1024)S(1)} all-reduce(f32[768]{0:T(1024)S(1)} %fusion.9), channel_id=1, replica_groups=mesh['dp'=32,'mp'=4] {'mp'}, use_global_device_ids=true, to_apply=%region_4.5 | all-reduce | flops 768 | bytes 6144 | tf_op jit(solution)/shard_map/psum | solution.py:88
  173.7 5.9 %fusion.7 = bf16[768,2048]{0,1:T(8,128)(2,1)} fusion(bf16[768,2048]{0,1:T(8,128)(2,1)S(1)} %copy.88, bf16[768,2048]{0,1:T(8,128)(2,1)} %copy.117, f32[768,16,128]{0,2,1:T(8,128)} %copy.118, f32[768]{0:T(1024)S(1)} %broadcast_multiply_fusion, f32[2048]{0:T(1024)S(1)} %copy-done.10, f32[768]{0:T(1024)S(1)} %add_rsqrt_fusion), kind=kLoop, calls=%fused_computation.10 | loop fusion | flops 15728640 | bytes 15742976 | tf_op jit(solution)/shard_map/convert_element_type | solution.py:92
  183.2 8.1 %all-to-all-start.3 = ((bf16[32,192,128]{2,1,0:T(8,128)(2,1)}), bf16[32,192,128]{2,1,0:T(8,128)(2,1)S(1)}, u32[]{:S(2)}, u32[]{:S(2)}) async-start(bf16[32,192,128]{2,1,0:T(8,128)(2,1)} %broadcast_in_dim.2), calls=%async_computation.3 | async-start | bytes 3145728 | tf_op jit(solution)/shard_map/all_to_all | solution.py:21
  191.3 4.7 %copy.119 = bf16[768,2048]{1,0:T(8,128)(2,1)} copy(bf16[768,2048]{0,1:T(8,128)(2,1)} %fusion.7) | data formatting | bytes 6291456
  196.0 17.0 %all-to-all-done.3 = bf16[32,192,128]{2,1,0:T(8,128)(2,1)S(1)} async-done(((bf16[32,192,128]{2,1,0:T(8,128)(2,1)}), bf16[32,192,128]{2,1,0:T(8,128)(2,1)S(1)}, u32[]{:S(2)}, u32[]{:S(2)}) %all-to-all-start.3) | async-done | bytes 1572896 | tf_op jit(solution)/shard_map/all_to_all | solution.py:21
  (45 shorter events, 31.9 us)
Async XLA Ops:
  0.6 1.1 copy-start
  8.0 61.3 %all-to-all-start.1 = ((bf16[768,16,128]{0,1,2:T(8,128)(2,1)}), bf16[768,16,128]{0,1,2:T(8,128)(2,1)}, u32[]{:S(2)}, u32[]{:S(2)}) async-start(bf16[768,16,128]{0,1,2:T(8,128)(2,1)} %copy.98), calls=%async_computation.1 | async-start | bytes 6291456 | tf_op jit(solution)/shard_map/all_to_all | solution.py:58
  17.2 44.2 %copy-start.10 = (f32[2048]{0:T(1024)S(1)}, f32[2048]{0:T(1024)}, u32[]{:S(2)}) copy-start(f32[2048]{0:T(1024)} %param.7) | copy-start | bytes 24580
  61.4 2.2 %copy-start.8 = (bf16[16,128,2,64]{1,3,2,0:T(8,128)(2,1)}, bf16[16,128,2,64]{1,3,2,0:T(8,128)(2,1)S(1)}, u32[]{:S(2)}) copy-start(bf16[16,128,2,64]{1,3,2,0:T(8,128)(2,1)S(1)} %copy.90) | copy-start | bytes 1572868
  61.4 1.2 copy-start.4
  62.2 1.7 copy-start.2
  69.3 40.3 %all-to-all-start = ((bf16[768,64,32]{0,2,1:T(8,128)(2,1)}), bf16[768,64,32]{0,2,1:T(8,128)(2,1)}, u32[]{:S(2)}, u32[]{:S(2)}) async-start(bf16[768,64,32]{0,2,1:T(8,128)(2,1)} %copy.134), calls=%async_computation | async-start | bytes 6291456 | tf_op jit(solution)/shard_map/all_to_all | solution.py:60
  77.0 1.9 copy-start.3
  77.0 2.0 copy-start.5
  79.0 3.9 %copy-start.9 = (bf16[16,128,2,64]{1,3,2,0:T(8,128)(2,1)S(1)}, bf16[16,128,2,64]{1,3,2,0:T(8,128)(2,1)}, u32[]{:S(2)}) copy-start(bf16[16,128,2,64]{1,3,2,0:T(8,128)(2,1)} %copy-done.8) | copy-start | bytes 1572868
  118.6 4.0 %copy-start.6 = (f32[16,128,128]{2,1,0:T(8,128)S(1)}, f32[16,128,128]{2,1,0:T(8,128)}, u32[]{:S(2)}) copy-start(f32[16,128,128]{2,1,0:T(8,128)} %copy.135) | copy-start | bytes 3145732
  118.6 4.0 %copy-start.7 = (f32[16,128,128]{2,1,0:T(8,128)S(1)}, f32[16,128,128]{2,1,0:T(8,128)}, u32[]{:S(2)}) copy-start(f32[16,128,128]{2,1,0:T(8,128)} %copy.136) | copy-start | bytes 3145732
  124.5 55.2 %all-to-all-start.2 = ((f32[32,192,128]{2,1,0:T(8,128)}), f32[32,192,128]{2,1,0:T(8,128)}, u32[]{:S(2)}, u32[]{:S(2)}) async-start(f32[32,192,128]{2,1,0:T(8,128)} %bitcast.137), calls=%async_computation.2 | async-start | bytes 6291456 | tf_op jit(solution)/shard_map/all_to_all | solution.py:14
  183.2 29.8 %all-to-all-start.3 = ((bf16[32,192,128]{2,1,0:T(8,128)(2,1)}), bf16[32,192,128]{2,1,0:T(8,128)(2,1)S(1)}, u32[]{:S(2)}, u32[]{:S(2)}) async-start(bf16[32,192,128]{2,1,0:T(8,128)(2,1)} %broadcast_in_dim.2), calls=%async_computation.3 | async-start | bytes 3145728 | tf_op jit(solution)/shard_map/all_to_all | solution.py:21
  191.3 23.5 %copy-start.1 = (bf16[16,128,128]{2,1,0:T(8,128)(2,1)S(1)}, bf16[16,128,128]{2,1,0:T(8,128)(2,1)}, u32[]{:S(2)}) copy-start(bf16[16,128,128]{2,1,0:T(8,128)(2,1)} %param.10) | copy-start | bytes 1572868

commit v6 on v1

--- a/solution.py
+++ b/solution.py
@@ -58,7 +58,13 @@
     )
     returned = lax.all_to_all(grad_perm, "mp", split_axis=2, concat_axis=1, tiled=True)
     outgoing, xn_b = lax.optimization_barrier((outgoing, xn))
-    permuted = lax.all_to_all(outgoing, "mp", split_axis=1, concat_axis=2, tiled=True)
+    me = lax.axis_index("mp")
+    nmp = lax.axis_size("mp")
+    width = outgoing.shape[1] // nmp
+    arrived = [lax.dynamic_slice_in_dim(outgoing, me * width, width, axis=1)]
+    for d in range(1, nmp):
+        chunk = lax.dynamic_slice_in_dim(outgoing, (me ^ d) * width, width, axis=1)
+        arrived.append(lax.ppermute(chunk, "mp", [(i, i ^ d) for i in range(nmp)]))
     act_a = jnp.einsum("tic,icj->tij", xn_b, left_p, preferred_element_type=jnp.float32)
     act_g = jnp.einsum("tic,icj->tij", xn_b, gate_p, preferred_element_type=jnp.float32)
     silu_g = jax.nn.silu(act_g)
@@ -77,14 +83,17 @@
     grad_norm = grad_norm + jnp.einsum(
         "tij,icj->tic", grad_g, gate_p, preferred_element_type=jnp.float32
     )
-    permuted, left_local, gate_local, grad_norm = lax.optimization_barrier(
-        (permuted, left_local, gate_local, grad_norm)
+    lg_mine = dp_reduce_scatter((left_local, gate_local))
+    arrived, grad_norm = lax.optimization_barrier((arrived, grad_norm))
+    permuted = jnp.stack(arrived, axis=2).reshape(rows, nlocal, BLOCK)
+    by_partner = jnp.einsum(
+        "tkc,tkm->kcm", permuted, cot_blocks, preferred_element_type=jnp.float32
+    ).reshape(nlocal, nmp, BLOCK // nmp, BLOCK)
+    right_local = jnp.concatenate(
+        [lax.dynamic_index_in_dim(by_partner, me ^ b, axis=1, keepdims=False) for b in range(nmp)], axis=1
     )
-    right_local = jnp.einsum(
-        "tkc,tkm->kcm", permuted, cot_blocks, preferred_element_type=jnp.float32
-    )
-    partials = (left_local, gate_local, right_local)
-    mine = dp_reduce_scatter(partials)
+    right_mine = dp_reduce_scatter((right_local,))
+    mine = jnp.concatenate([lg_mine, right_mine])
     scaled = grad_norm.reshape(rows, width_local) * gain
     inner = lax.psum(jnp.sum(scaled * xf, axis=1), "mp")
     mean_inner = (inner / W)[:, None]
@@ -92,7 +101,14 @@
         cotangent.astype(jnp.float32) + rstd * (scaled - xf * rstd * rstd * mean_inner)
     ).astype(jnp.bfloat16)
     mine, grad_input = lax.optimization_barrier((mine, grad_input))
-    left_total, gate_total, right_total = dp_all_gather(mine, [p.shape for p in partials])
+    ndp = lax.axis_size("dp")
+    whole = lax.all_to_all(
+        jnp.broadcast_to(mine.astype(jnp.bfloat16)[None], (ndp,) + mine.shape), "dp", 0, 0, tiled=True
+    )
+    nlg = lg_mine.shape[0]
+    lg = whole[:, :nlg].reshape(2, nlocal, BLOCK, BLOCK).astype(jnp.float32)
+    left_total, gate_total = lg[0], lg[1]
+    right_total = whole[:, nlg:].reshape(nlocal, BLOCK, BLOCK).astype(jnp.float32)
     return (grad_input, left_total, gate_total, right_total)
 
 

time: 212 us -> 207 us (0.976)
  blocking collectives: 32 us -> 19.7 us
  waiting for transfers between devices: 55.6 us -> 58.7 us
    all_to_all x2 -> x1, waiting for transfers between devices: 31.3 us -> 16.9 us  [body(): lax.all_to_all(jnp.broadcast_to(mine.astype(jnp.bfloat16)[None], (ndp,) +...]
    ppermute x0 -> x3, waiting for transfers between devices: none -> 14.3 us  [body(): arrived.append(lax.ppermute(chunk, 'mp', [(i, i ^ d) for i in range(nmp)]))]
    psum x1, blocking collectives: 23.7 us -> 11.4 us  [body(): inner = lax.psum(jnp.sum(scaled * xf, axis=1), 'mp')]
    all_to_all x1 -> x2, waiting for transfers between devices: 0.01 us -> 9.71 us  [dp_reduce_scatter(): got = lax.all_to_all(flat, 'dp', 0, 0, tiled=True)]
    all_to_all x2 -> x1, starting transfers between devices: 15.9 us -> 8.5 us  [body(): lax.all_to_all(jnp.broadcast_to(mine.astype(jnp.bfloat16)[None], (ndp,) +...]
    all_to_all x1, waiting for transfers between devices: 24.3 us -> 17.8 us  [body(): lax.all_to_all(grad_perm, 'mp', split_axis=2, concat_axis=1, tiled=True)]
    reshape x3 -> x0, local copies, waits for them, and re-layouts: 5.2 us -> none  [the longest x1 3.38 us: body(): gated.reshape(rows, nlocal, 2, NBLK).transpose(0, 3, 1, 2)]
    all_to_all x1 -> x2, starting transfers between devices: 9.62 us -> 14.6 us  [dp_reduce_scatter(): got = lax.all_to_all(flat, 'dp', 0, 0, tiled=True)]
  transfers between devices with their start and end apart: 4 -> 7, of which waited for: 3 -> 4; matrix products, arithmetic and copies ran while one was open for 28% -> 33% of each run, Pallas kernels for 0% -> 0%
where the time goes in v6:
time: 207 us; the launch traced here: 206 us
  waiting for transfers between devices  58.7 us (28%)
  local copies, waits for them, and re-layouts  46.3 us (22%)
  starting transfers between devices  33.4 us (16%)
  other arithmetic  24.6 us (12%)
  matrix products  22.2 us (11%)
  blocking collectives  19.7 us (10%)
    all_to_all x1, waiting for transfers between devices, body(): lax.all_to_all(grad_perm, 'mp', split_axis=2, concat_axis=1, tiled=True)  17.8 us
    unnamed x27, local copies, waits for them, and re-layouts  17.3 us
    all_to_all x1, waiting for transfers between devices, body(): lax.all_to_all(jnp.broadcast_to(mine.astype(jnp.bfloat16)[None], (ndp,) +...  16.9 us
    all_to_all x2, starting transfers between devices, dp_reduce_scatter(): got = lax.all_to_all(flat, 'dp', 0, 0, tiled=True)  14.6 us
    ppermute x3, waiting for transfers between devices, body(): arrived.append(lax.ppermute(chunk, 'mp', [(i, i ^ d) for i in range(nmp)]))  14.3 us
    psum x1, blocking collectives, body(): inner = lax.psum(jnp.sum(scaled * xf, axis=1), 'mp')  11.4 us
    all_to_all x2, waiting for transfers between devices, dp_reduce_scatter(): got = lax.all_to_all(flat, 'dp', 0, 0, tiled=True)  9.71 us
    all_to_all x1, starting transfers between devices, body(): lax.all_to_all(jnp.broadcast_to(mine.astype(jnp.bfloat16)[None], (ndp,) +...  8.5 us
  transfers between devices with their start and end apart: 7, of which 4 were waited for; matrix products, arithmetic and copies ran while one was open for 33% of the time, Pallas kernels for 0%

profile of v6, /device:TPU:6, one launch (start us, length us, event | category | flops | bytes accessed | tf_op | source)
XLA Modules:
  0.0 205.8 jit_solution(13543565072001696499)
XLA Ops:
  0.6 4.7 %copy.131 = bf16[768,2048]{0,1:T(8,128)(2,1)} copy(bf16[768,2048]{1,0:T(8,128)(2,1)} %param.6) | data formatting | bytes 6291456 | tf_op args[0]
  7.9 8.3 %psum.14 = f32[768]{0:T(1024)S(1)} all-reduce(f32[768]{0:T(1024)S(1)} %fusion.8), channel_id=1, replica_groups=mesh['dp'=32,'mp'=4] {'mp'}, use_global_device_ids=true, to_apply=%region_1.0 | all-reduce | flops 768 | bytes 6144 | tf_op jit(solution)/shard_map/psum | solution.py:47
  19.1 3.4 %copy.139 = bf16[768,16,128]{0,1,2:T(8,128)(2,1)} copy(bf16[768,16,128]{0,2,1:T(8,128)(2,1)S(1)} %convert_bitcast_fusion.1) | data formatting | bytes 6291456 | tf_op jit(solution)/shard_map/optimization_barrier | solution.py:48
  22.6 6.9 %all-to-all-start = ((bf16[768,16,128]{0,1,2:T(8,128)(2,1)}), bf16[768,16,128]{0,1,2:T(8,128)(2,1)}, u32[]{:S(2)}, u32[]{:S(2)}) async-start(bf16[768,16,128]{0,1,2:T(8,128)(2,1)} %copy.139), calls=%async_computation | async-start | bytes 6291456 | tf_op jit(solution)/shard_map/all_to_all | solution.py:59
  37.2 3.4 %copy.154 = bf16[768,64,32]{0,2,1:T(8,128)(2,1)} copy(bf16[768,64,32]{0,1,2:T(8,128)(2,1)S(1)} %bitcast.171) | data formatting | bytes 6291456 | tf_op jit(solution)/shard_map/optimization_barrier | solution.py:60
  40.6 3.3 %constant_dynamic-slice_fusion = (bf16[768,16,32]{0,2,1:T(8,128)(2,1)}, bf16[768,16,32]{0,2,1:T(8,128)(2,1)}, bf16[768,16,32]{0,2,1:T(8,128)(2,1)}, bf16[768,16,32]{0,2,1:T(8,128)(2,1)S(1)}) fusion(bf16[768,64,32]{0,2,1:T(8,128)(2,1)} %copy.154, s32[]{:T(128)S(6)} %select_n.28, s32[]{:T(128)S(6)} %select_n.27, s32[]{:T(128)S(6)} %select_n.26, s32[]{:T(128)S(6)} %select_n.25), kind=kLoop, calls=%fused_computation.57 | loop fusion | bytes 6291472 | tf_op jit(solution)/shard_map/dynamic_slice | solution.py:66
  47.2 17.8 %all-to-all-done = bf16[768,16,128]{0,1,2:T(8,128)(2,1)} async-done(((bf16[768,16,128]{0,1,2:T(8,128)(2,1)}), bf16[768,16,128]{0,1,2:T(8,128)(2,1)}, u32[]{:S(2)}, u32[]{:S(2)}) %all-to-all-start) | async-done | bytes 3145760 | tf_op jit(solution)/shard_map/all_to_all | solution.py:59
  65.0 2.9 %copy.140 = bf16[768,16,128]{0,2,1:T(8,128)(2,1)S(1)} copy(bf16[768,16,128]{0,1,2:T(8,128)(2,1)} %all-to-all-done) | data formatting | bytes 6291456 | tf_op jit(solution)/shard_map/all_to_all | solution.py:59
  68.8 3.6 %copy.141 = f32[768,4,16,32]{0,2,1,3:T(8,128)S(1)} copy(f32[768,4,16,32]{0,3,1,2:T(8,128)S(1)} %convert_bitcast_fusion) | data formatting | bytes 12582912 | tf_op jit(solution)/shard_map/convert_element_type | solution.py:75
  75.1 3.0 %fusion.12 = bf16[768,16,128]{0,2,1:T(8,128)(2,1)S(1)} fusion(f32[768,16,128]{0,2,1:T(8,128)S(1)} %bitcast.162, f32[16,768,128]{1,2,0:T(8,128)S(1)} %get-tuple-element.53, bf16[16,128,128]{1,2,0:T(8,128)(2,1)S(1)} %bitcast.174, bf16[768,16,128]{0,2,1:T(8,128)(2,1)S(1)} %bitcast.158), kind=kOutput, calls=%fused_computation.18 | convolution fusion | flops 418381824 | bytes 19398656 | tf_op jit(solution)/shard_map/tic,icj->tij/dot_general | solution.py:68
  80.1 3.8 %add_bitcast_fusion = f32[768,16,128]{2,0,1:T(8,128)} fusion(f32[16,768,128]{2,1,0:T(8,128)S(1)} %fusion.35, bf16[768,16,128]{0,2,1:T(8,128)(2,1)S(1)} %fusion.12, bf16[16,128,128]{1,2,0:T(8,128)(2,1)S(1)} %bitcast.165), kind=kOutput, calls=%fused_computation.34 | convolution fusion | flops 404226048 | bytes 16252928 | tf_op jit(solution)/shard_map/tij,icj->tic/dot_general | solution.py:83
  84.0 14.3 %collective-permute-done.2 = bf16[768,16,32]{0,2,1:T(8,128)(2,1)} collective-permute-done((bf16[768,16,32]{0,2,1:T(8,128)(2,1)}, bf16[768,16,32]{0,2,1:T(8,128)(2,1)}, u32[]{:S(2)}, u32[]{:S(2)}) %collective-permute-start.2) | collective-permute-done | bytes 786464 | tf_op jit(solution)/shard_map/ppermute | solution.py:67
  103.4 9.6 %all-to-all-start.2 = ((f32[32,64,128]{2,1,0:T(8,128)}), f32[32,64,128]{2,1,0:T(8,128)S(1)}, u32[]{:S(2)}, u32[]{:S(2)}) async-start(f32[32,64,128]{2,1,0:T(8,128)} %bitcast.37), calls=%async_computation.2 | async-start | bytes 2097152 | tf_op jit(solution)/shard_map/all_to_all | solution.py:14
  113.0 3.8 %fusion.33 = f32[16,128,128]{1,2,0:T(8,128)S(1)} fusion(bf16[768,16,128]{0,2,1:T(8,128)(2,1)} %bitcast.156, bf16[768,16,128]{0,2,1:T(8,128)(2,1)} %copy-done.4), kind=kOutput, calls=%fused_computation.63 | convolution fusion | flops 402653184 | bytes 7340032 | tf_op jit(solution)/shard_map/tic,tij->icj/dot_general | solution.py:80
  119.9 9.7 %all-to-all-done.2 = f32[32,64,128]{2,1,0:T(8,128)S(1)} async-done(((f32[32,64,128]{2,1,0:T(8,128)}), f32[32,64,128]{2,1,0:T(8,128)S(1)}, u32[]{:S(2)}, u32[]{:S(2)}) %all-to-all-start.2) | async-done | bytes 1048608 | tf_op jit(solution)/shard_map/all_to_all | solution.py:14
  130.5 5.1 %all-to-all-start.1 = ((f32[32,128,128]{1,2,0:T(8,128)}), f32[32,128,128]{1,2,0:T(8,128)S(1)}, u32[]{:S(2)}, u32[]{:S(2)}) async-start(f32[32,128,128]{1,2,0:T(8,128)} %copy_bitcast_fusion), calls=%async_computation.1 | async-start | bytes 4194304 | tf_op jit(solution)/shard_map/all_to_all | solution.py:14
  135.6 4.7 %copy.164 = bf16[768,2048]{0,1:T(8,128)(2,1)} copy(bf16[768,2048]{1,0:T(8,128)(2,1)} %param.11) | data formatting | bytes 6291456 | tf_op args[5]
  140.3 6.6 %copy.165 = f32[768,16,128]{0,2,1:T(8,128)} copy(f32[768,16,128]{2,0,1:T(8,128)} %add_bitcast_fusion) | data formatting | bytes 12582912 | tf_op jit(solution)/shard_map/optimization_barrier | solution.py:87
  146.9 4.6 %fusion.9 = f32[768]{0:T(1024)S(1)} fusion(bf16[768,2048]{0,1:T(8,128)(2,1)} %copy.131, f32[768,16,128]{0,2,1:T(8,128)} %copy.165, f32[2048]{0:T(1024)S(1)} %copy-done.10), kind=kLoop, calls=%fused_computation.12 | loop fusion | flops 6290688 | bytes 9448448 | tf_op jit(solution)/shard_map/reduce_sum | solution.py:98
  151.5 11.4 %psum.15 = f32[768]{0:T(1024)S(1)} all-reduce(f32[768]{0:T(1024)S(1)} %fusion.9), channel_id=1, replica_groups=mesh['dp'=32,'mp'=4] {'mp'}, use_global_device_ids=true, to_apply=%region_5.6 | all-reduce | flops 768 | bytes 6144 | tf_op jit(solution)/shard_map/psum | solution.py:98
  162.9 6.8 %fusion.7 = bf16[768,2048]{0,1:T(8,128)(2,1)} fusion(bf16[768,2048]{0,1:T(8,128)(2,1)} %copy.131, bf16[768,2048]{0,1:T(8,128)(2,1)} %copy.164, f32[768,16,128]{0,2,1:T(8,128)} %copy.165, f32[768]{0:T(1024)S(1)} %broadcast_multiply_fusion, f32[2048]{0:T(1024)S(1)} %copy-done.10, f32[768]{0:T(1024)S(1)} %add_rsqrt_fusion), kind=kLoop, calls=%fused_computation.10 | loop fusion | flops 15728640 | bytes 15742976 | tf_op jit(solution)/shard_map/convert_element_type | solution.py:102
  172.9 8.5 %all-to-all-start.3 = ((bf16[32,192,128]{2,1,0:T(8,128)(2,1)}), bf16[32,192,128]{2,1,0:T(8,128)(2,1)S(1)}, u32[]{:S(2)}, u32[]{:S(2)}) async-start(bf16[32,192,128]{2,1,0:T(8,128)(2,1)} %broadcast_in_dim.2), calls=%async_computation.3 | async-start | bytes 3145728 | tf_op jit(solution)/shard_map/all_to_all | solution.py:105
  181.4 4.6 %copy.167 = bf16[768,2048]{1,0:T(8,128)(2,1)} copy(bf16[768,2048]{0,1:T(8,128)(2,1)} %fusion.7) | data formatting | bytes 6291456
  186.1 16.9 %all-to-all-done.3 = bf16[32,192,128]{2,1,0:T(8,128)(2,1)S(1)} async-done(((bf16[32,192,128]{2,1,0:T(8,128)(2,1)}), bf16[32,192,128]{2,1,0:T(8,128)(2,1)S(1)}, u32[]{:S(2)}, u32[]{:S(2)}) %all-to-all-start.3) | async-done | bytes 1572896 | tf_op jit(solution)/shard_map/all_to_all | solution.py:105
  (61 shorter events, 37.1 us)
Async XLA Ops:
  0.6 15.6 %copy-start = (bf16[16,128,128]{2,1,0:T(8,128)(2,1)S(1)}, bf16[16,128,128]{2,1,0:T(8,128)(2,1)}, u32[]{:S(2)}) copy-start(bf16[16,128,128]{2,1,0:T(8,128)(2,1)} %param.10) | copy-start | bytes 1572868
  22.5 6.9 %copy-start.8 = (bf16[16,128,128]{2,1,0:T(8,128)(2,1)S(1)}, bf16[16,128,128]{2,1,0:T(8,128)(2,1)}, u32[]{:S(2)}) copy-start(bf16[16,128,128]{2,1,0:T(8,128)(2,1)} %param.9) | copy-start | bytes 1572868
  22.5 7.5 %copy-start.9 = (bf16[16,128,128]{2,1,0:T(8,128)(2,1)S(1)}, bf16[16,128,128]{2,1,0:T(8,128)(2,1)}, u32[]{:S(2)}) copy-start(bf16[16,128,128]{2,1,0:T(8,128)(2,1)} %param.8) | copy-start | bytes 1572868
  22.6 42.4 %all-to-all-start = ((bf16[768,16,128]{0,1,2:T(8,128)(2,1)}), bf16[768,16,128]{0,1,2:T(8,128)(2,1)}, u32[]{:S(2)}, u32[]{:S(2)}) async-start(bf16[768,16,128]{0,1,2:T(8,128)(2,1)} %copy.139), calls=%async_computation | async-start | bytes 6291456 | tf_op jit(solution)/shard_map/all_to_all | solution.py:59
  29.4 1.3 copy-start.10
  33.4 1.7 copy-start.2
  43.9 40.1 %collective-permute-start = (bf16[768,16,32]{0,2,1:T(8,128)(2,1)}, bf16[768,16,32]{0,2,1:T(8,128)(2,1)S(1)}, u32[]{:S(2)}, u32[]{:S(2)}) collective-permute-start(bf16[768,16,32]{0,2,1:T(8,128)(2,1)} %get-tuple-element.44), channel_id=1, source_target_pairs={{0,1},{1,0},{2,3},{3,2},{4,5},{5,4},{6,7},{7,6},{8,9},{9,8},{10,11... | collective-permute-start | bytes 2359304 | tf_op jit(solution)/shard_map/ppermute | solution.py:67
  44.0 40.0 %collective-permute-start.1 = (bf16[768,16,32]{0,2,1:T(8,128)(2,1)}, bf16[768,16,32]{0,2,1:T(8,128)(2,1)S(1)}, u32[]{:S(2)}, u32[]{:S(2)}) collective-permute-start(bf16[768,16,32]{0,2,1:T(8,128)(2,1)} %get-tuple-element.43), channel_id=1, source_target_pairs={{0,2},{1,3},{2,0},{3,1},{4,6},{5,7},{6,4},{7,5},{8,10},{9,11},{10,... | collective-permute-start | bytes 2359304 | tf_op jit(solution)/shard_map/ppermute | solution.py:67
  44.4 53.9 %collective-permute-start.2 = (bf16[768,16,32]{0,2,1:T(8,128)(2,1)}, bf16[768,16,32]{0,2,1:T(8,128)(2,1)}, u32[]{:S(2)}, u32[]{:S(2)}) collective-permute-start(bf16[768,16,32]{0,2,1:T(8,128)(2,1)} %get-tuple-element.42), channel_id=1, source_target_pairs={{0,3},{1,2},{2,1},{3,0},{4,7},{5,6},{6,5},{7,4},{8,11},{9,10},{10,... | collective-permute-start | bytes 2359304 | tf_op jit(solution)/shard_map/ppermute | solution.py:67
  68.8 3.7 %copy-start.3 = (bf16[768,2048]{0,1:T(8,128)(2,1)S(1)}, bf16[768,2048]{0,1:T(8,128)(2,1)}, u32[]{:S(2)}) copy-start(bf16[768,2048]{0,1:T(8,128)(2,1)} %copy-done.2) | copy-start | bytes 9437188
  75.1 3.0 %copy-start.4 = (bf16[768,16,128]{0,2,1:T(8,128)(2,1)}, bf16[768,16,128]{0,2,1:T(8,128)(2,1)S(1)}, u32[]{:S(2)}) copy-start(bf16[768,16,128]{0,2,1:T(8,128)(2,1)S(1)} %get-tuple-element.52) | copy-start | bytes 9437188
  84.0 14.3 %copy-start.7 = (bf16[768,16,32]{0,2,1:T(8,128)(2,1)}, bf16[768,16,32]{0,2,1:T(8,128)(2,1)S(1)}, u32[]{:S(2)}) copy-start(bf16[768,16,32]{0,2,1:T(8,128)(2,1)S(1)} %collective-permute-done.1) | copy-start | bytes 2359300
  98.9 2.4 %copy-start.5 = (bf16[768,2048]{1,0:T(8,128)(2,1)S(1)}, bf16[768,2048]{1,0:T(8,128)(2,1)}, u32[]{:S(2)}) copy-start(bf16[768,2048]{1,0:T(8,128)(2,1)} %param.11) | copy-start | bytes 9437188
  103.4 26.2 %all-to-all-start.2 = ((f32[32,64,128]{2,1,0:T(8,128)}), f32[32,64,128]{2,1,0:T(8,128)S(1)}, u32[]{:S(2)}, u32[]{:S(2)}) async-start(f32[32,64,128]{2,1,0:T(8,128)} %bitcast.37), calls=%async_computation.2 | async-start | bytes 2097152 | tf_op jit(solution)/shard_map/all_to_all | solution.py:14
  129.6 1.0 copy-start.6
  130.5 40.6 %all-to-all-start.1 = ((f32[32,128,128]{1,2,0:T(8,128)}), f32[32,128,128]{1,2,0:T(8,128)S(1)}, u32[]{:S(2)}, u32[]{:S(2)}) async-start(f32[32,128,128]{1,2,0:T(8,128)} %copy_bitcast_fusion), calls=%async_computation.1 | async-start | bytes 4194304 | tf_op jit(solution)/shard_map/all_to_all | solution.py:14
  172.9 30.0 %all-to-all-start.3 = ((bf16[32,192,128]{2,1,0:T(8,128)(2,1)}), bf16[32,192,128]{2,1,0:T(8,128)(2,1)S(1)}, u32[]{:S(2)}, u32[]{:S(2)}) async-start(bf16[32,192,128]{2,1,0:T(8,128)(2,1)} %broadcast_in_dim.2), calls=%async_computation.3 | async-start | bytes 3145728 | tf_op jit(solution)/shard_map/all_to_all | solution.py:105
  202.9 2.8 %copy-start.1 = (bf16[16,128,128]{2,1,0:T(8,128)(2,1)S(1)}, bf16[16,128,128]{2,1,0:T(8,128)(2,1)}, u32[]{:S(2)}) copy-start(bf16[16,128,128]{2,1,0:T(8,128)(2,1)} %param.10) | copy-start | bytes 1572868

commit v7 on v6

--- a/solution.py
+++ b/solution.py
@@ -83,8 +83,9 @@
     grad_norm = grad_norm + jnp.einsum(
         "tij,icj->tic", grad_g, gate_p, preferred_element_type=jnp.float32
     )
-    lg_mine = dp_reduce_scatter((left_local, gate_local))
-    arrived, grad_norm = lax.optimization_barrier((arrived, grad_norm))
+    arrived, left_local, gate_local, grad_norm = lax.optimization_barrier(
+        (arrived, left_local, gate_local, grad_norm)
+    )
     permuted = jnp.stack(arrived, axis=2).reshape(rows, nlocal, BLOCK)
     by_partner = jnp.einsum(
         "tkc,tkm->kcm", permuted, cot_blocks, preferred_element_type=jnp.float32
@@ -92,8 +93,8 @@
     right_local = jnp.concatenate(
         [lax.dynamic_index_in_dim(by_partner, me ^ b, axis=1, keepdims=False) for b in range(nmp)], axis=1
     )
-    right_mine = dp_reduce_scatter((right_local,))
-    mine = jnp.concatenate([lg_mine, right_mine])
+    partials = (left_local, gate_local, right_local)
+    mine = dp_reduce_scatter(partials)
     scaled = grad_norm.reshape(rows, width_local) * gain
     inner = lax.psum(jnp.sum(scaled * xf, axis=1), "mp")
     mean_inner = (inner / W)[:, None]
@@ -101,14 +102,7 @@
         cotangent.astype(jnp.float32) + rstd * (scaled - xf * rstd * rstd * mean_inner)
     ).astype(jnp.bfloat16)
     mine, grad_input = lax.optimization_barrier((mine, grad_input))
-    ndp = lax.axis_size("dp")
-    whole = lax.all_to_all(
-        jnp.broadcast_to(mine.astype(jnp.bfloat16)[None], (ndp,) + mine.shape), "dp", 0, 0, tiled=True
-    )
-    nlg = lg_mine.shape[0]
-    lg = whole[:, :nlg].reshape(2, nlocal, BLOCK, BLOCK).astype(jnp.float32)
-    left_total, gate_total = lg[0], lg[1]
-    right_total = whole[:, nlg:].reshape(nlocal, BLOCK, BLOCK).astype(jnp.float32)
+    left_total, gate_total, right_total = dp_all_gather(mine, [p.shape for p in partials])
     return (grad_input, left_total, gate_total, right_total)
 
 

time: 207 us -> 203 us (0.981)
  waiting for transfers between devices: 58.7 us -> 44.6 us
  blocking collectives: 19.7 us -> 33.2 us
  starting transfers between devices: 33.4 us -> 27.5 us
    psum x1, blocking collectives: 11.4 us -> 24.9 us  [body(): inner = lax.psum(jnp.sum(scaled * xf, axis=1), 'mp')]
    all_to_all x2 -> x1, waiting for transfers between devices: 9.71 us -> 0.01 us  [dp_reduce_scatter(): got = lax.all_to_all(flat, 'dp', 0, 0, tiled=True)]
    ppermute x3, waiting for transfers between devices: 14.3 us -> 8.8 us  [body(): arrived.append(lax.ppermute(chunk, 'mp', [(i, i ^ d) for i in range(nmp)]))]
    all_to_all x2 -> x1, starting transfers between devices: 14.6 us -> 9.62 us  [dp_reduce_scatter(): got = lax.all_to_all(flat, 'dp', 0, 0, tiled=True)]
    dot_general x1, matrix products: 3.82 us -> 0.98 us  [body(): jnp.einsum('tic,tij->icj', xn_b, grad_a, preferred_element_type=jnp.float32)]
    reshape x0 -> x2, local copies, waits for them, and re-layouts: none -> 2.79 us  [dp_reduce_scatter(): p.reshape(-1, BLOCK)]
    unnamed x27 -> x25, local copies, waits for them, and re-layouts: 17.3 us -> 16.3 us
  transfers between devices with their start and end apart: 7 -> 6, of which waited for: 4 -> 3; matrix products, arithmetic and copies ran while one was open for 33% -> 32% of each run, Pallas kernels for 0% -> 0%
where the time goes in v7:
time: 203 us; the launch traced here: 202 us
  local copies, waits for them, and re-layouts  46.9 us (23%)
  waiting for transfers between devices  44.6 us (22%)
  blocking collectives  33.2 us (16%)
  starting transfers between devices  27.5 us (14%)
  other arithmetic  25.2 us (12%)
  matrix products  23.6 us (12%)
    psum x1, blocking collectives, body(): inner = lax.psum(jnp.sum(scaled * xf, axis=1), 'mp')  24.9 us
    all_to_all x1, waiting for transfers between devices, dp_all_gather(): lax.all_to_all(copies, 'dp', 0, 0, tiled=True).reshape(-1, BLOCK, BLOCK)  18 us
    all_to_all x1, waiting for transfers between devices, body(): lax.all_to_all(grad_perm, 'mp', split_axis=2, concat_axis=1, tiled=True)  17.8 us
    unnamed x25, local copies, waits for them, and re-layouts  16.3 us
    all_to_all x1, starting transfers between devices, dp_reduce_scatter(): got = lax.all_to_all(flat, 'dp', 0, 0, tiled=True)  9.62 us
    ppermute x3, waiting for transfers between devices, body(): arrived.append(lax.ppermute(chunk, 'mp', [(i, i ^ d) for i in range(nmp)]))  8.8 us
    psum x1, blocking collectives, body(): squares = lax.psum(jnp.sum(xf * xf, axis=1), 'mp')  8.3 us
    all_to_all x1, starting transfers between devices, dp_all_gather(): lax.all_to_all(copies, 'dp', 0, 0, tiled=True).reshape(-1, BLOCK, BLOCK)  7.66 us
  transfers between devices with their start and end apart: 6, of which 3 were waited for; matrix products, arithmetic and copies ran while one was open for 32% of the time, Pallas kernels for 0%

profile of v7, /device:TPU:6, one launch (start us, length us, event | category | flops | bytes accessed | tf_op | source)
XLA Modules:
  0.0 201.9 jit_solution(17586748330814962046)
XLA Ops:
  0.6 4.7 %copy.135 = bf16[768,2048]{0,1:T(8,128)(2,1)} copy(bf16[768,2048]{1,0:T(8,128)(2,1)} %param.6) | data formatting | bytes 6291456 | tf_op args[0]
  7.9 8.3 %psum.14 = f32[768]{0:T(1024)S(1)} all-reduce(f32[768]{0:T(1024)S(1)} %fusion.8), channel_id=1, replica_groups=mesh['dp'=32,'mp'=4] {'mp'}, use_global_device_ids=true, to_apply=%region_1.0 | all-reduce | flops 768 | bytes 6144 | tf_op jit(solution)/shard_map/psum | solution.py:47
  16.2 2.9 %convert_bitcast_fusion.1 = bf16[768,16,128]{0,2,1:T(8,128)(2,1)S(1)} fusion(bf16[16,128,128]{2,1,0:T(8,128)(2,1)S(1)} %copy-done, bf16[768,2048]{1,0:T(8,128)(2,1)} %param.11), kind=kOutput, calls=%fused_computation.42 | convolution fusion | flops 404226048 | bytes 6815744 | tf_op jit(solution)/shard_map/tkm,kcm->tkc/dot_general | solution.py:44
  19.1 3.4 %copy.147 = bf16[768,16,128]{0,1,2:T(8,128)(2,1)} copy(bf16[768,16,128]{0,2,1:T(8,128)(2,1)S(1)} %convert_bitcast_fusion.1) | data formatting | bytes 6291456 | tf_op jit(solution)/shard_map/optimization_barrier | solution.py:48
  22.6 6.9 %all-to-all-start = ((bf16[768,16,128]{0,1,2:T(8,128)(2,1)}), bf16[768,16,128]{0,1,2:T(8,128)(2,1)}, u32[]{:S(2)}, u32[]{:S(2)}) async-start(bf16[768,16,128]{0,1,2:T(8,128)(2,1)} %copy.147), calls=%async_computation | async-start | bytes 6291456 | tf_op jit(solution)/shard_map/all_to_all | solution.py:59
  37.2 3.4 %copy.143 = bf16[768,64,32]{0,2,1:T(8,128)(2,1)} copy(bf16[768,64,32]{0,1,2:T(8,128)(2,1)S(1)} %bitcast.171) | data formatting | bytes 6291456 | tf_op jit(solution)/shard_map/optimization_barrier | solution.py:60
  40.6 3.3 %constant_dynamic-slice_fusion = (bf16[768,16,32]{0,2,1:T(8,128)(2,1)}, bf16[768,16,32]{0,2,1:T(8,128)(2,1)}, bf16[768,16,32]{0,2,1:T(8,128)(2,1)}, bf16[768,16,32]{0,2,1:T(8,128)(2,1)S(1)}) fusion(bf16[768,64,32]{0,2,1:T(8,128)(2,1)} %copy.143, s32[]{:T(128)S(6)} %select_n.28, s32[]{:T(128)S(6)} %select_n.27, s32[]{:T(128)S(6)} %select_n.26, s32[]{:T(128)S(6)} %select_n.25), kind=kLoop, calls=%fused_computation.54 | loop fusion | bytes 6291472 | tf_op jit(solution)/shard_map/dynamic_slice | solution.py:66
  44.4 2.9 %collective-permute-start.2 = (bf16[768,16,32]{0,2,1:T(8,128)(2,1)}, bf16[768,16,32]{0,2,1:T(8,128)(2,1)}, u32[]{:S(2)}, u32[]{:S(2)}) collective-permute-start(bf16[768,16,32]{0,2,1:T(8,128)(2,1)} %get-tuple-element.46), channel_id=1, source_target_pairs={{0,3},{1,2},{2,1},{3,0},{4,7},{5,6},{6,5},{7,4},{8,11},{9,10},{10,... | collective-permute-start | bytes 2359304 | tf_op jit(solution)/shard_map/ppermute | solution.py:67
  47.2 17.8 %all-to-all-done = bf16[768,16,128]{0,1,2:T(8,128)(2,1)} async-done(((bf16[768,16,128]{0,1,2:T(8,128)(2,1)}), bf16[768,16,128]{0,1,2:T(8,128)(2,1)}, u32[]{:S(2)}, u32[]{:S(2)}) %all-to-all-start) | async-done | bytes 3145760 | tf_op jit(solution)/shard_map/all_to_all | solution.py:59
  65.0 2.9 %copy.148 = bf16[768,16,128]{0,2,1:T(8,128)(2,1)S(1)} copy(bf16[768,16,128]{0,1,2:T(8,128)(2,1)} %all-to-all-done) | data formatting | bytes 6291456 | tf_op jit(solution)/shard_map/all_to_all | solution.py:59
  68.8 3.6 %copy.149 = f32[768,4,16,32]{0,2,1,3:T(8,128)S(1)} copy(f32[768,4,16,32]{0,3,1,2:T(8,128)S(1)} %convert_bitcast_fusion) | data formatting | bytes 12582912 | tf_op jit(solution)/shard_map/convert_element_type | solution.py:75
  72.4 4.0 %fusion.17 = (bf16[768,16,128]{0,2,1:T(8,128)(2,1)S(1)}, f32[16,768,128]{1,2,0:T(8,128)}) fusion(f32[768,16,128]{0,2,1:T(8,128)S(1)} %bitcast.157, bf16[16,128,128]{1,2,0:T(8,128)(2,1)S(1)} %bitcast.161, bf16[768,16,128]{0,2,1:T(8,128)(2,1)S(1)} %bitcast.151), kind=kOutput, calls=%fused_computation.26 | convolution fusion | flops 412090368 | bytes 19398656 | tf_op jit(solution)/shard_map/tic,icj->tij/dot_general | solution.py:69
  78.5 4.9 %fusion.12 = bf16[768,16,128]{0,2,1:T(8,128)(2,1)S(1)} fusion(f32[768,16,128]{0,2,1:T(8,128)S(1)} %bitcast.158, f32[16,768,128]{1,2,0:T(8,128)} %get-tuple-element.58, bf16[16,128,128]{1,2,0:T(8,128)(2,1)S(1)} %bitcast.175, bf16[768,16,128]{0,2,1:T(8,128)(2,1)S(1)} %bitcast.153), kind=kOutput, calls=%fused_computation.18 | convolution fusion | flops 418381824 | bytes 19398656 | tf_op jit(solution)/shard_map/tic,icj->tij/dot_general | solution.py:68
  85.7 3.8 %add_bitcast_fusion = f32[768,16,128]{2,0,1:T(8,128)} fusion(f32[16,768,128]{2,1,0:T(8,128)S(1)} %fusion.34, bf16[768,16,128]{0,2,1:T(8,128)(2,1)S(1)} %fusion.12, bf16[16,128,128]{1,2,0:T(8,128)(2,1)S(1)} %bitcast.162), kind=kOutput, calls=%fused_computation.34 | convolution fusion | flops 404226048 | bytes 16252928 | tf_op jit(solution)/shard_map/tij,icj->tic/dot_general | solution.py:83
  89.5 8.8 %collective-permute-done.2 = bf16[768,16,32]{0,2,1:T(8,128)(2,1)} collective-permute-done((bf16[768,16,32]{0,2,1:T(8,128)(2,1)}, bf16[768,16,32]{0,2,1:T(8,128)(2,1)}, u32[]{:S(2)}, u32[]{:S(2)}) %collective-permute-start.2) | collective-permute-done | bytes 786464 | tf_op jit(solution)/shard_map/ppermute | solution.py:67
  109.1 9.6 %all-to-all-start.1 = ((f32[32,192,128]{2,1,0:T(8,128)}), f32[32,192,128]{2,1,0:T(8,128)}, u32[]{:S(2)}, u32[]{:S(2)}) async-start(f32[32,192,128]{2,1,0:T(8,128)} %bitcast.155), calls=%async_computation.1 | async-start | bytes 6291456 | tf_op jit(solution)/shard_map/all_to_all | solution.py:14
  118.7 4.6 %copy.171 = bf16[768,2048]{0,1:T(8,128)(2,1)} copy(bf16[768,2048]{1,0:T(8,128)(2,1)} %param.11) | data formatting | bytes 6291456 | tf_op args[5]
  123.3 6.5 %copy.172 = f32[768,16,128]{0,2,1:T(8,128)} copy(f32[768,16,128]{2,0,1:T(8,128)} %add_bitcast_fusion) | data formatting | bytes 12582912 | tf_op jit(solution)/shard_map/optimization_barrier | solution.py:86
  129.9 4.6 %fusion.9 = f32[768]{0:T(1024)S(1)} fusion(bf16[768,2048]{0,1:T(8,128)(2,1)} %copy.135, f32[768,16,128]{0,2,1:T(8,128)} %copy.172, f32[2048]{0:T(1024)S(1)} %copy-done.9), kind=kLoop, calls=%fused_computation.12 | loop fusion | flops 6290688 | bytes 9448448 | tf_op jit(solution)/shard_map/reduce_sum | solution.py:99
  134.5 24.9 %psum.15 = f32[768]{0:T(1024)S(1)} all-reduce(f32[768]{0:T(1024)S(1)} %fusion.9), channel_id=1, replica_groups=mesh['dp'=32,'mp'=4] {'mp'}, use_global_device_ids=true, to_apply=%region_4.5 | all-reduce | flops 768 | bytes 6144 | tf_op jit(solution)/shard_map/psum | solution.py:99
  159.4 6.8 %fusion.7 = bf16[768,2048]{0,1:T(8,128)(2,1)} fusion(bf16[768,2048]{0,1:T(8,128)(2,1)} %copy.135, bf16[768,2048]{0,1:T(8,128)(2,1)} %copy.171, f32[768,16,128]{0,2,1:T(8,128)} %copy.172, f32[768]{0:T(1024)S(1)} %broadcast_multiply_fusion, f32[2048]{0:T(1024)S(1)} %copy-done.9, f32[768]{0:T(1024)S(1)} %add_rsqrt_fusion), kind=kLoop, calls=%fused_computation.10 | loop fusion | flops 15728640 | bytes 15742976 | tf_op jit(solution)/shard_map/convert_element_type | solution.py:103
  169.7 7.7 %all-to-all-start.2 = ((bf16[32,192,128]{2,1,0:T(8,128)(2,1)}), bf16[32,192,128]{2,1,0:T(8,128)(2,1)S(1)}, u32[]{:S(2)}, u32[]{:S(2)}) async-start(bf16[32,192,128]{2,1,0:T(8,128)(2,1)} %broadcast_in_dim.2), calls=%async_computation.2 | async-start | bytes 3145728 | tf_op jit(solution)/shard_map/all_to_all | solution.py:21
  177.4 4.7 %copy.173 = bf16[768,2048]{1,0:T(8,128)(2,1)} copy(bf16[768,2048]{0,1:T(8,128)(2,1)} %fusion.7) | data formatting | bytes 6291456
  182.1 18.0 %all-to-all-done.2 = bf16[32,192,128]{2,1,0:T(8,128)(2,1)S(1)} async-done(((bf16[32,192,128]{2,1,0:T(8,128)(2,1)}), bf16[32,192,128]{2,1,0:T(8,128)(2,1)S(1)}, u32[]{:S(2)}, u32[]{:S(2)}) %all-to-all-start.2) | async-done | bytes 1572896 | tf_op jit(solution)/shard_map/all_to_all | solution.py:21
  (51 shorter events, 31.9 us)
Async XLA Ops:
  0.6 15.6 %copy-start = (bf16[16,128,128]{2,1,0:T(8,128)(2,1)S(1)}, bf16[16,128,128]{2,1,0:T(8,128)(2,1)}, u32[]{:S(2)}) copy-start(bf16[16,128,128]{2,1,0:T(8,128)(2,1)} %param.10) | copy-start | bytes 1572868
  22.6 6.9 %copy-start.7 = (bf16[16,128,128]{2,1,0:T(8,128)(2,1)S(1)}, bf16[16,128,128]{2,1,0:T(8,128)(2,1)}, u32[]{:S(2)}) copy-start(bf16[16,128,128]{2,1,0:T(8,128)(2,1)} %param.9) | copy-start | bytes 1572868
  22.6 7.5 %copy-start.8 = (bf16[16,128,128]{2,1,0:T(8,128)(2,1)S(1)}, bf16[16,128,128]{2,1,0:T(8,128)(2,1)}, u32[]{:S(2)}) copy-start(bf16[16,128,128]{2,1,0:T(8,128)(2,1)} %param.8) | copy-start | bytes 1572868
  22.6 42.5 %all-to-all-start = ((bf16[768,16,128]{0,1,2:T(8,128)(2,1)}), bf16[768,16,128]{0,1,2:T(8,128)(2,1)}, u32[]{:S(2)}, u32[]{:S(2)}) async-start(bf16[768,16,128]{0,1,2:T(8,128)(2,1)} %copy.147), calls=%async_computation | async-start | bytes 6291456 | tf_op jit(solution)/shard_map/all_to_all | solution.py:59
  29.4 1.3 copy-start.9
  33.4 1.7 copy-start.2
  43.9 45.6 %collective-permute-start = (bf16[768,16,32]{0,2,1:T(8,128)(2,1)}, bf16[768,16,32]{0,2,1:T(8,128)(2,1)}, u32[]{:S(2)}, u32[]{:S(2)}) collective-permute-start(bf16[768,16,32]{0,2,1:T(8,128)(2,1)} %get-tuple-element.48), channel_id=1, source_target_pairs={{0,1},{1,0},{2,3},{3,2},{4,5},{5,4},{6,7},{7,6},{8,9},{9,8},{10,11... | collective-permute-start | bytes 2359304 | tf_op jit(solution)/shard_map/ppermute | solution.py:67
  44.0 45.5 %collective-permute-start.1 = (bf16[768,16,32]{0,2,1:T(8,128)(2,1)}, bf16[768,16,32]{0,2,1:T(8,128)(2,1)}, u32[]{:S(2)}, u32[]{:S(2)}) collective-permute-start(bf16[768,16,32]{0,2,1:T(8,128)(2,1)} %get-tuple-element.47), channel_id=1, source_target_pairs={{0,2},{1,3},{2,0},{3,1},{4,6},{5,7},{6,4},{7,5},{8,10},{9,11},{10,... | collective-permute-start | bytes 2359304 | tf_op jit(solution)/shard_map/ppermute | solution.py:67
  44.4 53.9 %collective-permute-start.2 = (bf16[768,16,32]{0,2,1:T(8,128)(2,1)}, bf16[768,16,32]{0,2,1:T(8,128)(2,1)}, u32[]{:S(2)}, u32[]{:S(2)}) collective-permute-start(bf16[768,16,32]{0,2,1:T(8,128)(2,1)} %get-tuple-element.46), channel_id=1, source_target_pairs={{0,3},{1,2},{2,1},{3,0},{4,7},{5,6},{6,5},{7,4},{8,11},{9,10},{10,... | collective-permute-start | bytes 2359304 | tf_op jit(solution)/shard_map/ppermute | solution.py:67
  68.8 3.7 %copy-start.3 = (bf16[768,2048]{0,1:T(8,128)(2,1)S(1)}, bf16[768,2048]{0,1:T(8,128)(2,1)}, u32[]{:S(2)}) copy-start(bf16[768,2048]{0,1:T(8,128)(2,1)} %copy-done.2) | copy-start | bytes 9437188
  98.3 2.6 %copy-start.4 = (bf16[768,2048]{1,0:T(8,128)(2,1)S(1)}, bf16[768,2048]{1,0:T(8,128)(2,1)}, u32[]{:S(2)}) copy-start(bf16[768,2048]{1,0:T(8,128)(2,1)} %param.11) | copy-start | bytes 9437188
  104.3 2.9 %copy-start.5 = (f32[16,128,128]{2,1,0:T(8,128)S(1)}, f32[16,128,128]{2,1,0:T(8,128)}, u32[]{:S(2)}) copy-start(f32[16,128,128]{2,1,0:T(8,128)} %copy.188) | copy-start | bytes 3145732
  105.7 1.5 copy-start.6
  109.1 57.1 %all-to-all-start.1 = ((f32[32,192,128]{2,1,0:T(8,128)}), f32[32,192,128]{2,1,0:T(8,128)}, u32[]{:S(2)}, u32[]{:S(2)}) async-start(f32[32,192,128]{2,1,0:T(8,128)} %bitcast.155), calls=%async_computation.1 | async-start | bytes 6291456 | tf_op jit(solution)/shard_map/all_to_all | solution.py:14
  169.7 30.4 %all-to-all-start.2 = ((bf16[32,192,128]{2,1,0:T(8,128)(2,1)}), bf16[32,192,128]{2,1,0:T(8,128)(2,1)S(1)}, u32[]{:S(2)}, u32[]{:S(2)}) async-start(bf16[32,192,128]{2,1,0:T(8,128)(2,1)} %broadcast_in_dim.2), calls=%async_computation.2 | async-start | bytes 3145728 | tf_op jit(solution)/shard_map/all_to_all | solution.py:21
  177.4 24.5 %copy-start.1 = (bf16[16,128,128]{2,1,0:T(8,128)(2,1)S(1)}, bf16[16,128,128]{2,1,0:T(8,128)(2,1)}, u32[]{:S(2)}) copy-start(bf16[16,128,128]{2,1,0:T(8,128)(2,1)} %param.10) | copy-start | bytes 1572868

commit v8 on v7

--- a/solution.py
+++ b/solution.py
@@ -83,8 +83,10 @@
     grad_norm = grad_norm + jnp.einsum(
         "tij,icj->tic", grad_g, gate_p, preferred_element_type=jnp.float32
     )
-    arrived, left_local, gate_local, grad_norm = lax.optimization_barrier(
-        (arrived, left_local, gate_local, grad_norm)
+    scaled = grad_norm.reshape(rows, width_local) * gain
+    inner = lax.psum(jnp.sum(scaled * xf, axis=1), "mp")
+    arrived, left_local, gate_local, scaled, inner = lax.optimization_barrier(
+        (arrived, left_local, gate_local, scaled, inner)
     )
     permuted = jnp.stack(arrived, axis=2).reshape(rows, nlocal, BLOCK)
     by_partner = jnp.einsum(
@@ -95,8 +97,6 @@
     )
     partials = (left_local, gate_local, right_local)
     mine = dp_reduce_scatter(partials)
-    scaled = grad_norm.reshape(rows, width_local) * gain
-    inner = lax.psum(jnp.sum(scaled * xf, axis=1), "mp")
     mean_inner = (inner / W)[:, None]
     grad_input = (
         cotangent.astype(jnp.float32) + rstd * (scaled - xf * rstd * rstd * mean_inner)

time: 203 us -> 208 us (1.025); the launches traced: 202 us -> 205 us
  blocking collectives: 33.2 us -> 46.3 us
  starting transfers between devices: 27.5 us -> 19.7 us
  waiting for transfers between devices: 44.6 us -> 41.8 us
  matrix products: 23.6 us -> 26.4 us
    all_to_all x1, waiting for transfers between devices: 0.01 us -> 31.5 us  [dp_reduce_scatter(): got = lax.all_to_all(flat, 'dp', 0, 0, tiled=True)]
    all_to_all x0 -> x1, blocking collectives: none -> 28.7 us  [dp_all_gather(): lax.all_to_all(copies, 'dp', 0, 0, tiled=True).reshape(-1, BLOCK, BLOCK)]
    all_to_all x1 -> x0, waiting for transfers between devices: 18 us -> none  [dp_all_gather(): lax.all_to_all(copies, 'dp', 0, 0, tiled=True).reshape(-1, BLOCK, BLOCK)]
    psum x1, blocking collectives: 24.9 us -> 9.33 us  [body(): inner = lax.psum(jnp.sum(scaled * xf, axis=1), 'mp')]
    ppermute x3, waiting for transfers between devices: 8.8 us -> 0.01 us  [body(): arrived.append(lax.ppermute(chunk, 'mp', [(i, i ^ d) for i in range(nmp)]))]
    all_to_all x1 -> x0, starting transfers between devices: 7.66 us -> none  [dp_all_gather(): lax.all_to_all(copies, 'dp', 0, 0, tiled=True).reshape(-1, BLOCK, BLOCK)]
    all_to_all x1, waiting for transfers between devices: 17.8 us -> 10.3 us  [body(): lax.all_to_all(grad_perm, 'mp', split_axis=2, concat_axis=1, tiled=True)]
    unnamed x25 -> x27, local copies, waits for them, and re-layouts: 16.3 us -> 9.39 us
  transfers between devices with their start and end apart: 6 -> 5, of which waited for: 3 -> 2; matrix products, arithmetic and copies ran while one was open for 32% -> 34% of each run, Pallas kernels for 0% -> 0%
where the time goes in v8:
time: 208 us; the launch traced here: 205 us
  blocking collectives  46.3 us (22%)
  local copies, waits for them, and re-layouts  45 us (22%)
  waiting for transfers between devices  41.8 us (20%)
  matrix products  26.4 us (13%)
  other arithmetic  24.5 us (12%)
  starting transfers between devices  19.7 us (9%)
    all_to_all x1, waiting for transfers between devices, dp_reduce_scatter(): got = lax.all_to_all(flat, 'dp', 0, 0, tiled=True)  31.5 us
    all_to_all x1, blocking collectives, dp_all_gather(): lax.all_to_all(copies, 'dp', 0, 0, tiled=True).reshape(-1, BLOCK, BLOCK)  28.7 us
    all_to_all x1, waiting for transfers between devices, body(): lax.all_to_all(grad_perm, 'mp', split_axis=2, concat_axis=1, tiled=True)  10.3 us
    all_to_all x1, starting transfers between devices, dp_reduce_scatter(): got = lax.all_to_all(flat, 'dp', 0, 0, tiled=True)  9.61 us
    unnamed x27, local copies, waits for them, and re-layouts  9.39 us
    psum x1, blocking collectives, body(): inner = lax.psum(jnp.sum(scaled * xf, axis=1), 'mp')  9.33 us
    psum x1, blocking collectives, body(): squares = lax.psum(jnp.sum(xf * xf, axis=1), 'mp')  8.31 us
    all_to_all x1, starting transfers between devices, body(): lax.all_to_all(grad_perm, 'mp', split_axis=2, concat_axis=1, tiled=True)  6.73 us
  transfers between devices with their start and end apart: 5, of which 2 were waited for; matrix products, arithmetic and copies ran while one was open for 34% of the time, Pallas kernels for 0%

profile of v8, /device:TPU:6, one launch (start us, length us, event | category | flops | bytes accessed | tf_op | source)
XLA Modules:
  0.0 204.7 jit_solution(5682136107336759467)
XLA Ops:
  0.6 2.6 %fusion.8 = f32[768]{0:T(1024)S(1)} fusion(bf16[768,2048]{1,0:T(8,128)(2,1)} %param.6), kind=kLoop, calls=%fused_computation.11 | loop fusion | flops 4717824 | bytes 3148800 | tf_op jit(solution)/shard_map/reduce_sum | solution.py:47
  3.3 8.3 %psum.14 = f32[768]{0:T(1024)S(1)} all-reduce(f32[768]{0:T(1024)S(1)} %fusion.8), channel_id=1, replica_groups=mesh['dp'=32,'mp'=4] {'mp'}, use_global_device_ids=true, to_apply=%region_1.0 | all-reduce | flops 768 | bytes 6144 | tf_op jit(solution)/shard_map/psum | solution.py:47
  11.6 2.9 %convert_bitcast_fusion.1 = bf16[768,16,128]{0,2,1:T(8,128)(2,1)S(1)} fusion(bf16[16,128,128]{2,1,0:T(8,128)(2,1)S(1)} %copy-done, bf16[768,2048]{1,0:T(8,128)(2,1)} %param.11), kind=kOutput, calls=%fused_computation.45 | convolution fusion | flops 404226048 | bytes 6815744 | tf_op jit(solution)/shard_map/tkm,kcm->tkc/dot_general | solution.py:44
  14.5 3.4 %copy.138 = bf16[768,16,128]{0,1,2:T(8,128)(2,1)} copy(bf16[768,16,128]{0,2,1:T(8,128)(2,1)S(1)} %convert_bitcast_fusion.1) | data formatting | bytes 6291456 | tf_op jit(solution)/shard_map/optimization_barrier | solution.py:48
  17.9 6.7 %all-to-all-start = ((bf16[768,16,128]{0,1,2:T(8,128)(2,1)}), bf16[768,16,128]{0,1,2:T(8,128)(2,1)}, u32[]{:S(2)}, u32[]{:S(2)}) async-start(bf16[768,16,128]{0,1,2:T(8,128)(2,1)} %copy.138), calls=%async_computation | async-start | bytes 6291456 | tf_op jit(solution)/shard_map/all_to_all | solution.py:59
  33.5 2.7 %copy.179 = bf16[96,8,16,128]{3,2,1,0:T(8,128)(2,1)} copy(bf16[96,8,16,128]{3,1,2,0:T(8,128)(2,1)S(1)} %get-tuple-element.34) | data formatting | bytes 6291456
  39.5 3.5 %copy.134 = bf16[768,64,32]{0,2,1:T(8,128)(2,1)} copy(bf16[768,64,32]{0,1,2:T(8,128)(2,1)S(1)} %bitcast.168) | data formatting | bytes 6291456 | tf_op jit(solution)/shard_map/optimization_barrier | solution.py:60
  42.9 3.6 %constant_dynamic-slice_fusion = (bf16[768,16,32]{0,2,1:T(8,128)(2,1)}, bf16[768,16,32]{0,2,1:T(8,128)(2,1)}, bf16[768,16,32]{0,2,1:T(8,128)(2,1)}, bf16[768,16,32]{0,2,1:T(8,128)(2,1)}) fusion(bf16[768,64,32]{0,2,1:T(8,128)(2,1)} %copy.134, s32[]{:T(128)S(6)} %select_n.28, s32[]{:T(128)S(6)} %select_n.27, s32[]{:T(128)S(6)} %select_n.26, s32[]{:T(128)S(6)} %select_n.25), kind=kLoop, calls=%fused_computation.69 | loop fusion | bytes 6291472 | tf_op jit(solution)/shard_map/dynamic_slice | solution.py:66
  46.6 3.2 %collective-permute-start.1 = (bf16[768,16,32]{0,2,1:T(8,128)(2,1)}, bf16[768,16,32]{0,2,1:T(8,128)(2,1)}, u32[]{:S(2)}, u32[]{:S(2)}) collective-permute-start(bf16[768,16,32]{0,2,1:T(8,128)(2,1)} %get-tuple-element.37), channel_id=1, source_target_pairs={{0,2},{1,3},{2,0},{3,1},{4,6},{5,7},{6,4},{7,5},{8,10},{9,11},{10,... | collective-permute-start | bytes 2359304 | tf_op jit(solution)/shard_map/ppermute | solution.py:67
  49.9 10.3 %all-to-all-done = bf16[768,16,128]{0,1,2:T(8,128)(2,1)} async-done(((bf16[768,16,128]{0,1,2:T(8,128)(2,1)}), bf16[768,16,128]{0,1,2:T(8,128)(2,1)}, u32[]{:S(2)}, u32[]{:S(2)}) %all-to-all-start) | async-done | bytes 3145760 | tf_op jit(solution)/shard_map/all_to_all | solution.py:59
  60.2 2.9 %copy.139 = bf16[768,16,128]{0,2,1:T(8,128)(2,1)S(1)} copy(bf16[768,16,128]{0,1,2:T(8,128)(2,1)} %all-to-all-done) | data formatting | bytes 6291456 | tf_op jit(solution)/shard_map/all_to_all | solution.py:59
  64.0 3.6 %copy.140 = f32[768,4,16,32]{0,2,1,3:T(8,128)S(1)} copy(f32[768,4,16,32]{0,3,1,2:T(8,128)S(1)} %convert_bitcast_fusion) | data formatting | bytes 12582912 | tf_op jit(solution)/shard_map/convert_element_type | solution.py:75
  67.7 4.9 %fusion.17 = (bf16[768,16,128]{0,2,1:T(8,128)(2,1)S(1)}, f32[16,768,128]{1,2,0:T(8,128)}) fusion(f32[768,16,128]{0,2,1:T(8,128)S(1)} %bitcast.152, bf16[16,128,128]{1,2,0:T(8,128)(2,1)S(1)} %bitcast.156, bf16[768,16,128]{2,1,0:T(8,128)(2,1)S(1)} %bitcast.163), kind=kOutput, calls=%fused_computation.25 | convolution fusion | flops 412090368 | bytes 19398656 | tf_op jit(solution)/shard_map/tic,icj->tij/dot_general | solution.py:69
  72.6 5.8 %fusion.12 = bf16[768,16,128]{0,2,1:T(8,128)(2,1)S(1)} fusion(f32[768,16,128]{0,2,1:T(8,128)S(1)} %bitcast.153, f32[16,768,128]{1,2,0:T(8,128)} %get-tuple-element.48, bf16[16,128,128]{1,2,0:T(8,128)(2,1)S(1)} %bitcast.171, bf16[768,16,128]{2,1,0:T(8,128)(2,1)S(1)} %bitcast.164), kind=kOutput, calls=%fused_computation.17 | convolution fusion | flops 418381824 | bytes 19398656 | tf_op jit(solution)/shard_map/tic,icj->tij/dot_general | solution.py:68
  81.4 3.8 %convolution_add_fusion = f32[16,768,128]{1,2,0:T(8,128)} fusion(f32[16,768,128]{1,2,0:T(8,128)S(1)} %fusion.49, bf16[768,16,128]{0,2,1:T(8,128)(2,1)S(1)} %fusion.12, bf16[16,128,128]{1,2,0:T(8,128)(2,1)S(1)} %bitcast.157), kind=kOutput, calls=%fused_computation.50 | convolution fusion | flops 404226048 | bytes 16252928 | tf_op jit(solution)/shard_map/tij,icj->tic/dot_general | solution.py:83
  90.2 6.7 %copy.155 = f32[768,2048]{1,0:T(8,128)} copy(f32[768,2048]{0,1:T(8,128)} %bitcast.149) | data formatting | bytes 12582912 | tf_op jit(solution)/shard_map/reshape | solution.py:86
  96.9 6.3 %fusion.9 = (f32[768]{0:T(1024)S(1)}, f32[768,2048]{1,0:T(8,128)}) fusion(bf16[768,2048]{1,0:T(8,128)(2,1)S(1)} %copy-done.2, f32[768,2048]{1,0:T(8,128)} %copy.155, f32[2048]{0:T(1024)S(1)} %copy-done.11), kind=kLoop, calls=%fused_computation.12 | loop fusion | flops 6290688 | bytes 15739904 | tf_op jit(solution)/shard_map/reduce_sum | solution.py:87
  103.1 9.3 %psum.15 = f32[768]{0:T(1024)S(1)} all-reduce(f32[768]{0:T(1024)S(1)} %get-tuple-element.32), channel_id=1, replica_groups=mesh['dp'=32,'mp'=4] {'mp'}, use_global_device_ids=true, to_apply=%region_3.4 | all-reduce | flops 768 | bytes 6144 | tf_op jit(solution)/shard_map/psum | solution.py:87
  112.5 2.6 %copy.171 = f32[16,128,128]{2,1,0:T(8,128)} copy(f32[16,128,128]{1,0,2:T(8,128)} %bitcast.158) | data formatting | bytes 2097152 | tf_op jit(solution)/shard_map/reshape | solution.py:13
  115.0 2.5 %copy.172 = f32[16,128,128]{2,1,0:T(8,128)} copy(f32[16,128,128]{1,0,2:T(8,128)} %bitcast.159) | data formatting | bytes 2097152 | tf_op jit(solution)/shard_map/reshape | solution.py:13
  124.9 9.6 %all-to-all-start.1 = ((f32[32,192,128]{2,1,0:T(8,128)}), f32[32,192,128]{2,1,0:T(8,128)}, u32[]{:S(2)}, u32[]{:S(2)}) async-start(f32[32,192,128]{2,1,0:T(8,128)} %bitcast.150), calls=%async_computation.1 | async-start | bytes 6291456 | tf_op jit(solution)/shard_map/all_to_all | solution.py:14
  134.5 5.9 %fusion.7 = bf16[768,2048]{1,0:T(8,128)(2,1)} fusion(f32[768,2048]{1,0:T(8,128)} %get-tuple-element.28, bf16[768,2048]{1,0:T(8,128)(2,1)S(1)} %copy-done.2, bf16[768,2048]{1,0:T(8,128)(2,1)} %param.11, f32[768]{0:T(1024)S(1)} %broadcast_multiply_fusion.1, f32[768]{0:T(1024)S(1)} %add_rsqrt_fusion), kind=kLoop, calls=%fused_computation.10 | loop fusion | flops 14155776 | bytes 15734784 | tf_op jit(solution)/shard_map/convert_element_type | solution.py:103
  140.4 31.5 %all-to-all-done.1 = f32[32,192,128]{2,1,0:T(8,128)} async-done(((f32[32,192,128]{2,1,0:T(8,128)}), f32[32,192,128]{2,1,0:T(8,128)}, u32[]{:S(2)}, u32[]{:S(2)}) %all-to-all-start.1) | async-done | bytes 3145760 | tf_op jit(solution)/shard_map/all_to_all | solution.py:14
  174.3 28.7 %all_to_all.22 = bf16[32,192,128]{2,1,0:T(8,128)(2,1)S(1)} all-to-all(bf16[32,192,128]{2,1,0:T(8,128)(2,1)S(1)} %broadcast_in_dim.2), channel_id=1, replica_groups=mesh['dp'=32,'mp'=4] {'dp'}, dimensions={0} | all-to-all | bytes 3145728 | tf_op jit(solution)/shard_map/all_to_all | solution.py:21
  (52 shorter events, 32.6 us)
Async XLA Ops:
  0.6 11.0 %copy-start = (bf16[16,128,128]{2,1,0:T(8,128)(2,1)S(1)}, bf16[16,128,128]{2,1,0:T(8,128)(2,1)}, u32[]{:S(2)}) copy-start(bf16[16,128,128]{2,1,0:T(8,128)(2,1)} %param.10) | copy-start | bytes 1572868
  17.9 42.3 %all-to-all-start = ((bf16[768,16,128]{0,1,2:T(8,128)(2,1)}), bf16[768,16,128]{0,1,2:T(8,128)(2,1)}, u32[]{:S(2)}, u32[]{:S(2)}) async-start(bf16[768,16,128]{0,1,2:T(8,128)(2,1)} %copy.138), calls=%async_computation | async-start | bytes 6291456 | tf_op jit(solution)/shard_map/all_to_all | solution.py:59
  24.6 7.9 %copy-start.2 = (bf16[768,2048]{1,0:T(8,128)(2,1)S(1)}, bf16[768,2048]{1,0:T(8,128)(2,1)}, u32[]{:S(2)}) copy-start(bf16[768,2048]{1,0:T(8,128)(2,1)} %param.6) | copy-start | bytes 9437188
  24.6 7.9 %copy-start.11 = (f32[2048]{0:T(1024)S(1)}, f32[2048]{0:T(1024)}, u32[]{:S(2)}) copy-start(f32[2048]{0:T(1024)} %param.7) | copy-start | bytes 24580
  32.6 3.7 %copy-start.4 = (bf16[16,128,2,64]{1,3,2,0:T(8,128)(2,1)}, bf16[16,128,2,64]{1,3,2,0:T(8,128)(2,1)S(1)}, u32[]{:S(2)}) copy-start(bf16[16,128,2,64]{1,3,2,0:T(8,128)(2,1)S(1)} %copy.132) | copy-start | bytes 1572868
  36.2 1.0 copy-start.9
  46.5 66.0 %collective-permute-start.2 = (bf16[768,16,32]{0,2,1:T(8,128)(2,1)}, bf16[768,16,32]{0,2,1:T(8,128)(2,1)}, u32[]{:S(2)}, u32[]{:S(2)}) collective-permute-start(bf16[768,16,32]{0,2,1:T(8,128)(2,1)} %get-tuple-element.36), channel_id=1, source_target_pairs={{0,3},{1,2},{2,1},{3,0},{4,7},{5,6},{6,5},{7,4},{8,11},{9,10},{10,... | collective-permute-start | bytes 2359304 | tf_op jit(solution)/shard_map/ppermute | solution.py:67
  46.6 65.9 %collective-permute-start.1 = (bf16[768,16,32]{0,2,1:T(8,128)(2,1)}, bf16[768,16,32]{0,2,1:T(8,128)(2,1)}, u32[]{:S(2)}, u32[]{:S(2)}) collective-permute-start(bf16[768,16,32]{0,2,1:T(8,128)(2,1)} %get-tuple-element.37), channel_id=1, source_target_pairs={{0,2},{1,3},{2,0},{3,1},{4,6},{5,7},{6,4},{7,5},{8,10},{9,11},{10,... | collective-permute-start | bytes 2359304 | tf_op jit(solution)/shard_map/ppermute | solution.py:67
  49.8 62.7 %collective-permute-start = (bf16[768,16,32]{0,2,1:T(8,128)(2,1)}, bf16[768,16,32]{0,2,1:T(8,128)(2,1)}, u32[]{:S(2)}, u32[]{:S(2)}) collective-permute-start(bf16[768,16,32]{0,2,1:T(8,128)(2,1)} %get-tuple-element.38), channel_id=1, source_target_pairs={{0,1},{1,0},{2,3},{3,2},{4,5},{5,4},{6,7},{7,6},{8,9},{9,8},{10,11... | collective-permute-start | bytes 2359304 | tf_op jit(solution)/shard_map/ppermute | solution.py:67
  64.0 3.7 %copy-start.5 = (bf16[16,128,2,64]{1,3,2,0:T(8,128)(2,1)S(1)}, bf16[16,128,2,64]{1,3,2,0:T(8,128)(2,1)}, u32[]{:S(2)}) copy-start(bf16[16,128,2,64]{1,3,2,0:T(8,128)(2,1)} %copy-done.4) | copy-start | bytes 1572868
  64.0 3.7 %copy-start.8 = (bf16[96,8,16,128]{3,2,1,0:T(8,128)(2,1)S(1)}, bf16[96,8,16,128]{3,2,1,0:T(8,128)(2,1)}, u32[]{:S(2)}) copy-start(bf16[96,8,16,128]{3,2,1,0:T(8,128)(2,1)} %copy.179) | copy-start | bytes 9437188
  67.6 4.9 %copy-start.10 = (bf16[16,128,2,64]{1,3,2,0:T(8,128)(2,1)S(1)}, bf16[16,128,2,64]{1,3,2,0:T(8,128)(2,1)}, u32[]{:S(2)}) copy-start(bf16[16,128,2,64]{1,3,2,0:T(8,128)(2,1)} %copy.129) | copy-start | bytes 1572868
  117.6 2.8 %copy-start.3 = (bf16[768,2048]{1,0:T(8,128)(2,1)S(1)}, bf16[768,2048]{1,0:T(8,128)(2,1)}, u32[]{:S(2)}) copy-start(bf16[768,2048]{1,0:T(8,128)(2,1)} %param.11) | copy-start | bytes 9437188
  121.4 1.2 copy-start.6
  121.4 1.5 copy-start.7
  124.9 47.0 %all-to-all-start.1 = ((f32[32,192,128]{2,1,0:T(8,128)}), f32[32,192,128]{2,1,0:T(8,128)}, u32[]{:S(2)}, u32[]{:S(2)}) async-start(f32[32,192,128]{2,1,0:T(8,128)} %bitcast.150), calls=%async_computation.1 | async-start | bytes 6291456 | tf_op jit(solution)/shard_map/all_to_all | solution.py:14
  174.3 30.4 %copy-start.1 = (bf16[16,128,128]{2,1,0:T(8,128)(2,1)S(1)}, bf16[16,128,128]{2,1,0:T(8,128)(2,1)}, u32[]{:S(2)}) copy-start(bf16[16,128,128]{2,1,0:T(8,128)(2,1)} %param.10) | copy-start | bytes 1572868

commit v9 on v7

--- a/solution.py
+++ b/solution.py
@@ -26,6 +26,12 @@
     return tuple(out)
 
 
+def mp_sum(v):
+    n = lax.axis_size("mp")
+    v = v + lax.ppermute(v, "mp", [(i, i ^ 1) for i in range(n)])
+    return v + lax.ppermute(v, "mp", [(i, i ^ 2) for i in range(n)])
+
+
 def pair_major(blocks):
     n, c, _ = blocks.shape
     return blocks.reshape(n, c, NBLK, 2).transpose(0, 1, 3, 2).reshape(n, c, 2 * NBLK)
@@ -44,7 +50,7 @@
     grad_perm = jnp.einsum(
         "tkm,kcm->tkc", cot_blocks, right_blocks, preferred_element_type=jnp.float32
     ).astype(jnp.bfloat16)
-    squares = lax.psum(jnp.sum(xf * xf, axis=1), "mp")
+    squares = mp_sum(jnp.sum(xf * xf, axis=1))
     grad_perm, squares = lax.optimization_barrier((grad_perm, squares))
     rstd = lax.rsqrt(squares / W + 1e-05)[:, None]
     xn = (xf * rstd * gain).astype(jnp.bfloat16).reshape(rows, nlocal, BLOCK)

time: 203 us -> 200 us (0.985)
  blocking collectives: 33.2 us -> 24.8 us
  waiting for transfers between devices: 44.6 us -> 50.6 us
    psum x1 -> x0, blocking collectives: 8.3 us -> none  [body(): squares = lax.psum(jnp.sum(xf * xf, axis=1), 'mp')]
    all_to_all x1, waiting for transfers between devices: 17.8 us -> 22.6 us  [body(): lax.all_to_all(grad_perm, 'mp', split_axis=2, concat_axis=1, tiled=True)]
    unnamed x25 -> x27, local copies, waits for them, and re-layouts: 16.3 us -> 16.4 us
  transfers between devices with their start and end apart: 6 -> 8, of which waited for: 3 -> 4; matrix products, arithmetic and copies ran while one was open for 32% -> 32% of each run, Pallas kernels for 0% -> 0%
where the time goes in v9:
time: 200 us; the launch traced here: 199 us
  waiting for transfers between devices  50.6 us (25%)
  local copies, waits for them, and re-layouts  45.3 us (23%)
  starting transfers between devices  29.1 us (15%)
  other arithmetic  25.4 us (13%)
  blocking collectives  24.8 us (12%)
  matrix products  23.4 us (12%)
    psum x1, blocking collectives, body(): inner = lax.psum(jnp.sum(scaled * xf, axis=1), 'mp')  24.8 us
    all_to_all x1, waiting for transfers between devices, body(): lax.all_to_all(grad_perm, 'mp', split_axis=2, concat_axis=1, tiled=True)  22.6 us
    all_to_all x1, waiting for transfers between devices, dp_all_gather(): lax.all_to_all(copies, 'dp', 0, 0, tiled=True).reshape(-1, BLOCK, BLOCK)  18 us
    unnamed x27, local copies, waits for them, and re-layouts  16.4 us
    all_to_all x1, starting transfers between devices, dp_reduce_scatter(): got = lax.all_to_all(flat, 'dp', 0, 0, tiled=True)  9.62 us
    ppermute x3, waiting for transfers between devices, body(): arrived.append(lax.ppermute(chunk, 'mp', [(i, i ^ d) for i in range(nmp)]))  8.83 us
    all_to_all x1, starting transfers between devices, dp_all_gather(): lax.all_to_all(copies, 'dp', 0, 0, tiled=True).reshape(-1, BLOCK, BLOCK)  7.66 us
    all_to_all x1, starting transfers between devices, body(): lax.all_to_all(grad_perm, 'mp', split_axis=2, concat_axis=1, tiled=True)  6.87 us
  transfers between devices with their start and end apart: 8, of which 4 were waited for; matrix products, arithmetic and copies ran while one was open for 32% of the time, Pallas kernels for 0%

profile of v9, /device:TPU:6, one launch (start us, length us, event | category | flops | bytes accessed | tf_op | source)
XLA Modules:
  0.0 199.4 jit_solution(11691683566525453677)
XLA Ops:
  0.6 4.7 %copy.135 = bf16[768,2048]{0,1:T(8,128)(2,1)} copy(bf16[768,2048]{1,0:T(8,128)(2,1)} %param.6) | data formatting | bytes 6291456 | tf_op args[0]
  5.3 2.7 %fusion.8 = f32[768]{0:T(1024)S(1)} fusion(bf16[768,2048]{0,1:T(8,128)(2,1)} %copy.135), kind=kLoop, calls=%fused_computation.11 | loop fusion | flops 4717824 | bytes 3148800 | tf_op jit(solution)/shard_map/reduce_sum | solution.py:53
  10.8 2.7 %convert_bitcast_fusion.1 = bf16[768,16,128]{0,2,1:T(8,128)(2,1)} fusion(bf16[16,128,128]{2,1,0:T(8,128)(2,1)S(1)} %copy-done, bf16[768,2048]{1,0:T(8,128)(2,1)S(1)} %copy-done.4), kind=kOutput, calls=%fused_computation.42 | convolution fusion | flops 404226048 | bytes 6815744 | tf_op jit(solution)/shard_map/tkm,kcm->tkc/dot_general | solution.py:50
  14.9 5.3 %copy.147 = bf16[768,16,128]{0,1,2:T(8,128)(2,1)} copy(bf16[768,16,128]{0,2,1:T(8,128)(2,1)} %convert_bitcast_fusion.1) | data formatting | bytes 6291456 | tf_op jit(solution)/shard_map/optimization_barrier | solution.py:54
  20.1 6.9 %all-to-all-start = ((bf16[768,16,128]{0,1,2:T(8,128)(2,1)}), bf16[768,16,128]{0,1,2:T(8,128)(2,1)}, u32[]{:S(2)}, u32[]{:S(2)}) async-start(bf16[768,16,128]{0,1,2:T(8,128)(2,1)} %copy.147), calls=%async_computation | async-start | bytes 6291456 | tf_op jit(solution)/shard_map/all_to_all | solution.py:65
  27.0 2.7 %fusion.2 = bf16[768,2048]{0,1:T(8,128)(2,1)S(1)} fusion(bf16[768,2048]{0,1:T(8,128)(2,1)} %copy.135, f32[2048]{0:T(1024)S(1)} %copy-done.10, f32[768]{0:T(1024)S(1)} %add_rsqrt_fusion), kind=kLoop, calls=%fused_computation.5 | loop fusion | flops 6291456 | bytes 6302720 | tf_op jit(solution)/shard_map/convert_element_type | solution.py:56
  37.1 2.9 %collective-permute-start.4 = (bf16[768,16,32]{0,2,1:T(8,128)(2,1)}, bf16[768,16,32]{0,2,1:T(8,128)(2,1)}, u32[]{:S(2)}, u32[]{:S(2)}) collective-permute-start(bf16[768,16,32]{0,2,1:T(8,128)(2,1)} %get-tuple-element.46), channel_id=1, source_target_pairs={{0,3},{1,2},{2,1},{3,0},{4,7},{5,6},{6,5},{7,4},{8,11},{9,10},{10,... | collective-permute-start | bytes 2359304 | tf_op jit(solution)/shard_map/ppermute | solution.py:73
  40.0 22.6 %all-to-all-done = bf16[768,16,128]{0,1,2:T(8,128)(2,1)} async-done(((bf16[768,16,128]{0,1,2:T(8,128)(2,1)}), bf16[768,16,128]{0,1,2:T(8,128)(2,1)}, u32[]{:S(2)}, u32[]{:S(2)}) %all-to-all-start) | async-done | bytes 3145760 | tf_op jit(solution)/shard_map/all_to_all | solution.py:65
  62.6 2.9 %copy.148 = bf16[768,16,128]{0,2,1:T(8,128)(2,1)S(1)} copy(bf16[768,16,128]{0,1,2:T(8,128)(2,1)} %all-to-all-done) | data formatting | bytes 6291456 | tf_op jit(solution)/shard_map/all_to_all | solution.py:65
  66.3 3.6 %copy.149 = f32[768,4,16,32]{0,2,1,3:T(8,128)S(1)} copy(f32[768,4,16,32]{0,3,1,2:T(8,128)S(1)} %convert_bitcast_fusion) | data formatting | bytes 12582912 | tf_op jit(solution)/shard_map/convert_element_type | solution.py:81
  70.0 4.0 %fusion.17 = (bf16[768,16,128]{0,2,1:T(8,128)(2,1)S(1)}, f32[16,768,128]{1,2,0:T(8,128)}) fusion(f32[768,16,128]{0,2,1:T(8,128)S(1)} %bitcast.157, bf16[16,128,128]{1,2,0:T(8,128)(2,1)S(1)} %bitcast.161, bf16[768,16,128]{0,2,1:T(8,128)(2,1)S(1)} %bitcast.151), kind=kOutput, calls=%fused_computation.26 | convolution fusion | flops 412090368 | bytes 19398656 | tf_op jit(solution)/shard_map/tic,icj->tij/dot_general | solution.py:75
  76.1 4.9 %fusion.12 = bf16[768,16,128]{0,2,1:T(8,128)(2,1)S(1)} fusion(f32[768,16,128]{0,2,1:T(8,128)S(1)} %bitcast.158, f32[16,768,128]{1,2,0:T(8,128)} %get-tuple-element.58, bf16[16,128,128]{1,2,0:T(8,128)(2,1)S(1)} %bitcast.175, bf16[768,16,128]{0,2,1:T(8,128)(2,1)S(1)} %bitcast.153), kind=kOutput, calls=%fused_computation.18 | convolution fusion | flops 418381824 | bytes 19398656 | tf_op jit(solution)/shard_map/tic,icj->tij/dot_general | solution.py:74
  83.2 3.8 %add_bitcast_fusion = f32[768,16,128]{2,0,1:T(8,128)} fusion(f32[16,768,128]{2,1,0:T(8,128)S(1)} %fusion.34, bf16[768,16,128]{0,2,1:T(8,128)(2,1)S(1)} %fusion.12, bf16[16,128,128]{1,2,0:T(8,128)(2,1)S(1)} %bitcast.162), kind=kOutput, calls=%fused_computation.34 | convolution fusion | flops 404226048 | bytes 16252928 | tf_op jit(solution)/shard_map/tij,icj->tic/dot_general | solution.py:89
  87.0 8.8 %collective-permute-done.4 = bf16[768,16,32]{0,2,1:T(8,128)(2,1)} collective-permute-done((bf16[768,16,32]{0,2,1:T(8,128)(2,1)}, bf16[768,16,32]{0,2,1:T(8,128)(2,1)}, u32[]{:S(2)}, u32[]{:S(2)}) %collective-permute-start.4) | collective-permute-done | bytes 786464 | tf_op jit(solution)/shard_map/ppermute | solution.py:73
  106.6 9.6 %all-to-all-start.1 = ((f32[32,192,128]{2,1,0:T(8,128)}), f32[32,192,128]{2,1,0:T(8,128)}, u32[]{:S(2)}, u32[]{:S(2)}) async-start(f32[32,192,128]{2,1,0:T(8,128)} %bitcast.155), calls=%async_computation.1 | async-start | bytes 6291456 | tf_op jit(solution)/shard_map/all_to_all | solution.py:14
  116.2 4.7 %copy.171 = bf16[768,2048]{0,1:T(8,128)(2,1)} copy(bf16[768,2048]{1,0:T(8,128)(2,1)} %param.11) | data formatting | bytes 6291456 | tf_op args[5]
  120.9 6.6 %copy.172 = f32[768,16,128]{0,2,1:T(8,128)} copy(f32[768,16,128]{2,0,1:T(8,128)} %add_bitcast_fusion) | data formatting | bytes 12582912 | tf_op jit(solution)/shard_map/optimization_barrier | solution.py:92
  127.5 4.6 %fusion.9 = f32[768]{0:T(1024)S(1)} fusion(bf16[768,2048]{0,1:T(8,128)(2,1)} %copy.135, f32[768,16,128]{0,2,1:T(8,128)} %copy.172, f32[2048]{0:T(1024)S(1)} %copy-done.10), kind=kLoop, calls=%fused_computation.12 | loop fusion | flops 6290688 | bytes 9448448 | tf_op jit(solution)/shard_map/reduce_sum | solution.py:105
  132.1 24.8 %psum.7 = f32[768]{0:T(1024)S(1)} all-reduce(f32[768]{0:T(1024)S(1)} %fusion.9), channel_id=1, replica_groups=mesh['dp'=32,'mp'=4] {'mp'}, use_global_device_ids=true, to_apply=%region_3.4 | all-reduce | flops 768 | bytes 6144 | tf_op jit(solution)/shard_map/psum | solution.py:105
  156.9 6.8 %fusion.7 = bf16[768,2048]{0,1:T(8,128)(2,1)} fusion(bf16[768,2048]{0,1:T(8,128)(2,1)} %copy.135, bf16[768,2048]{0,1:T(8,128)(2,1)} %copy.171, f32[768,16,128]{0,2,1:T(8,128)} %copy.172, f32[768]{0:T(1024)S(1)} %broadcast_multiply_fusion, f32[2048]{0:T(1024)S(1)} %copy-done.10, f32[768]{0:T(1024)S(1)} %add_rsqrt_fusion), kind=kLoop, calls=%fused_computation.10 | loop fusion | flops 15728640 | bytes 15742976 | tf_op jit(solution)/shard_map/convert_element_type | solution.py:109
  163.8 2.0 %reduce_sum.28 = bf16[192,128]{1,0:T(8,128)(2,1)S(1)} reduce(f32[32,192,128]{2,1,0:T(8,128)} %all-to-all-done.1, f32[]{:T(128)} %constant.14.clone.1), dimensions={0}, to_apply=%region_1.2 | reduce | flops 761856 | bytes 3194884 | tf_op jit(solution)/shard_map/reduce_sum | solution.py:15
  167.3 7.7 %all-to-all-start.2 = ((bf16[32,192,128]{2,1,0:T(8,128)(2,1)}), bf16[32,192,128]{2,1,0:T(8,128)(2,1)S(1)}, u32[]{:S(2)}, u32[]{:S(2)}) async-start(bf16[32,192,128]{2,1,0:T(8,128)(2,1)} %broadcast_in_dim.2), calls=%async_computation.2 | async-start | bytes 3145728 | tf_op jit(solution)/shard_map/all_to_all | solution.py:21
  175.0 4.7 %copy.173 = bf16[768,2048]{1,0:T(8,128)(2,1)} copy(bf16[768,2048]{0,1:T(8,128)(2,1)} %fusion.7) | data formatting | bytes 6291456
  179.7 18.0 %all-to-all-done.2 = bf16[32,192,128]{2,1,0:T(8,128)(2,1)S(1)} async-done(((bf16[32,192,128]{2,1,0:T(8,128)(2,1)}), bf16[32,192,128]{2,1,0:T(8,128)(2,1)S(1)}, u32[]{:S(2)}, u32[]{:S(2)}) %all-to-all-start.2) | async-done | bytes 1572896 | tf_op jit(solution)/shard_map/all_to_all | solution.py:21
  (58 shorter events, 30.6 us)
Async XLA Ops:
  0.6 10.2 %copy-start = (bf16[16,128,128]{2,1,0:T(8,128)(2,1)S(1)}, bf16[16,128,128]{2,1,0:T(8,128)(2,1)}, u32[]{:S(2)}) copy-start(bf16[16,128,128]{2,1,0:T(8,128)(2,1)} %param.10) | copy-start | bytes 1572868
  5.3 5.5 %copy-start.4 = (bf16[768,2048]{1,0:T(8,128)(2,1)S(1)}, bf16[768,2048]{1,0:T(8,128)(2,1)}, u32[]{:S(2)}) copy-start(bf16[768,2048]{1,0:T(8,128)(2,1)} %param.11) | copy-start | bytes 9437188
  8.1 1.2 collective-permute-start
  9.3 4.2 %copy-start.8 = (bf16[16,128,128]{2,1,0:T(8,128)(2,1)S(1)}, bf16[16,128,128]{2,1,0:T(8,128)(2,1)}, u32[]{:S(2)}) copy-start(bf16[16,128,128]{2,1,0:T(8,128)(2,1)} %param.9) | copy-start | bytes 1572868
  9.3 4.8 %copy-start.9 = (bf16[16,128,128]{2,1,0:T(8,128)(2,1)S(1)}, bf16[16,128,128]{2,1,0:T(8,128)(2,1)}, u32[]{:S(2)}) copy-start(bf16[16,128,128]{2,1,0:T(8,128)(2,1)} %param.8) | copy-start | bytes 1572868
  9.3 5.5 %collective-permute-start.1 = (f32[768]{0:T(1024)S(1)}, f32[768]{0:T(1024)S(1)}, u32[]{:S(2)}, u32[]{:S(2)}) collective-permute-start(f32[768]{0:T(1024)S(1)} %add.59), channel_id=1, source_target_pairs={{0,2},{1,3},{2,0},{3,1},{4,6},{5,7},{6,4},{7,5},{8,10},{9,11},{10,... | collective-permute-start | bytes 9224 | tf_op jit(solution)/shard_map/ppermute | solution.py:32
  20.1 6.9 %copy-start.10 = (f32[2048]{0:T(1024)S(1)}, f32[2048]{0:T(1024)}, u32[]{:S(2)}) copy-start(f32[2048]{0:T(1024)} %param.7) | copy-start | bytes 24580
  20.1 42.5 %all-to-all-start = ((bf16[768,16,128]{0,1,2:T(8,128)(2,1)}), bf16[768,16,128]{0,1,2:T(8,128)(2,1)}, u32[]{:S(2)}, u32[]{:S(2)}) async-start(bf16[768,16,128]{0,1,2:T(8,128)(2,1)} %copy.147), calls=%async_computation | async-start | bytes 6291456 | tf_op jit(solution)/shard_map/all_to_all | solution.py:65
  29.7 1.7 copy-start.2
  36.6 50.4 %collective-permute-start.2 = (bf16[768,16,32]{0,2,1:T(8,128)(2,1)}, bf16[768,16,32]{0,2,1:T(8,128)(2,1)}, u32[]{:S(2)}, u32[]{:S(2)}) collective-permute-start(bf16[768,16,32]{0,2,1:T(8,128)(2,1)} %get-tuple-element.48), channel_id=1, source_target_pairs={{0,1},{1,0},{2,3},{3,2},{4,5},{5,4},{6,7},{7,6},{8,9},{9,8},{10,11... | collective-permute-start | bytes 2359304 | tf_op jit(solution)/shard_map/ppermute | solution.py:73
  36.8 50.3 %collective-permute-start.3 = (bf16[768,16,32]{0,2,1:T(8,128)(2,1)}, bf16[768,16,32]{0,2,1:T(8,128)(2,1)}, u32[]{:S(2)}, u32[]{:S(2)}) collective-permute-start(bf16[768,16,32]{0,2,1:T(8,128)(2,1)} %get-tuple-element.47), channel_id=1, source_target_pairs={{0,2},{1,3},{2,0},{3,1},{4,6},{5,7},{6,4},{7,5},{8,10},{9,11},{10,... | collective-permute-start | bytes 2359304 | tf_op jit(solution)/shard_map/ppermute | solution.py:73
  37.1 58.7 %collective-permute-start.4 = (bf16[768,16,32]{0,2,1:T(8,128)(2,1)}, bf16[768,16,32]{0,2,1:T(8,128)(2,1)}, u32[]{:S(2)}, u32[]{:S(2)}) collective-permute-start(bf16[768,16,32]{0,2,1:T(8,128)(2,1)} %get-tuple-element.46), channel_id=1, source_target_pairs={{0,3},{1,2},{2,1},{3,0},{4,7},{5,6},{6,5},{7,4},{8,11},{9,10},{10,... | collective-permute-start | bytes 2359304 | tf_op jit(solution)/shard_map/ppermute | solution.py:73
  66.3 3.7 %copy-start.3 = (bf16[768,2048]{0,1:T(8,128)(2,1)S(1)}, bf16[768,2048]{0,1:T(8,128)(2,1)}, u32[]{:S(2)}) copy-start(bf16[768,2048]{0,1:T(8,128)(2,1)} %copy-done.2) | copy-start | bytes 9437188
  95.9 2.6 %copy-start.5 = (bf16[768,2048]{1,0:T(8,128)(2,1)S(1)}, bf16[768,2048]{1,0:T(8,128)(2,1)}, u32[]{:S(2)}) copy-start(bf16[768,2048]{1,0:T(8,128)(2,1)} %param.11) | copy-start | bytes 9437188
  101.8 2.9 %copy-start.6 = (f32[16,128,128]{2,1,0:T(8,128)S(1)}, f32[16,128,128]{2,1,0:T(8,128)}, u32[]{:S(2)}) copy-start(f32[16,128,128]{2,1,0:T(8,128)} %copy.188) | copy-start | bytes 3145732
  103.2 1.5 copy-start.7
  106.6 57.1 %all-to-all-start.1 = ((f32[32,192,128]{2,1,0:T(8,128)}), f32[32,192,128]{2,1,0:T(8,128)}, u32[]{:S(2)}, u32[]{:S(2)}) async-start(f32[32,192,128]{2,1,0:T(8,128)} %bitcast.155), calls=%async_computation.1 | async-start | bytes 6291456 | tf_op jit(solution)/shard_map/all_to_all | solution.py:14
  167.3 30.4 %all-to-all-start.2 = ((bf16[32,192,128]{2,1,0:T(8,128)(2,1)}), bf16[32,192,128]{2,1,0:T(8,128)(2,1)S(1)}, u32[]{:S(2)}, u32[]{:S(2)}) async-start(bf16[32,192,128]{2,1,0:T(8,128)(2,1)} %broadcast_in_dim.2), calls=%async_computation.2 | async-start | bytes 3145728 | tf_op jit(solution)/shard_map/all_to_all | solution.py:21
  175.0 24.4 %copy-start.1 = (bf16[16,128,128]{2,1,0:T(8,128)(2,1)S(1)}, bf16[16,128,128]{2,1,0:T(8,128)(2,1)}, u32[]{:S(2)}) copy-start(bf16[16,128,128]{2,1,0:T(8,128)(2,1)} %param.10) | copy-start | bytes 1572868

commit v10 on v9

--- a/solution.py
+++ b/solution.py
@@ -102,7 +102,7 @@
     partials = (left_local, gate_local, right_local)
     mine = dp_reduce_scatter(partials)
     scaled = grad_norm.reshape(rows, width_local) * gain
-    inner = lax.psum(jnp.sum(scaled * xf, axis=1), "mp")
+    inner = mp_sum(jnp.sum(scaled * xf, axis=1))
     mean_inner = (inner / W)[:, None]
     grad_input = (
         cotangent.astype(jnp.float32) + rstd * (scaled - xf * rstd * rstd * mean_inner)

time: 200 us -> 199 us (level)
  blocking collectives: 24.8 us -> 0 us
  waiting for transfers between devices: 50.6 us -> 69.8 us
  starting transfers between devices: 29.1 us -> 32.8 us
    psum x1 -> x0, blocking collectives: 24.8 us -> none  [body(): inner = lax.psum(jnp.sum(scaled * xf, axis=1), 'mp')]
    ppermute x1 -> x2, waiting for transfers between devices: 0.01 us -> 19.6 us  [mp_sum(): return v + lax.ppermute(v, 'mp', [(i, i ^ 2) for i in range(n)])]
    ppermute x1 -> x2, starting transfers between devices: 1.48 us -> 4.39 us  [mp_sum(): return v + lax.ppermute(v, 'mp', [(i, i ^ 2) for i in range(n)])]
  transfers between devices with their start and end apart: 8 -> 10, of which waited for: 4 -> 6; matrix products, arithmetic and copies ran while one was open for 32% -> 33% of each run, Pallas kernels for 0% -> 0%
where the time goes in v10:
time: 199 us; the launch traced here: 198 us
  waiting for transfers between devices  69.8 us (35%)
  local copies, waits for them, and re-layouts  45.3 us (23%)
  starting transfers between devices  32.8 us (16%)
  other arithmetic  25.4 us (13%)
  matrix products  23.6 us (12%)
    all_to_all x1, waiting for transfers between devices, body(): lax.all_to_all(grad_perm, 'mp', split_axis=2, concat_axis=1, tiled=True)  22.6 us
    ppermute x2, waiting for transfers between devices, mp_sum(): return v + lax.ppermute(v, 'mp', [(i, i ^ 2) for i in range(n)])  19.6 us
    all_to_all x1, waiting for transfers between devices, dp_all_gather(): lax.all_to_all(copies, 'dp', 0, 0, tiled=True).reshape(-1, BLOCK, BLOCK)  16.6 us
    unnamed x27, local copies, waits for them, and re-layouts  16.4 us
    all_to_all x1, starting transfers between devices, dp_reduce_scatter(): got = lax.all_to_all(flat, 'dp', 0, 0, tiled=True)  9.62 us
    ppermute x3, waiting for transfers between devices, body(): arrived.append(lax.ppermute(chunk, 'mp', [(i, i ^ d) for i in range(nmp)]))  8.68 us
    all_to_all x1, starting transfers between devices, dp_all_gather(): lax.all_to_all(copies, 'dp', 0, 0, tiled=True).reshape(-1, BLOCK, BLOCK)  8.43 us
    all_to_all x1, starting transfers between devices, body(): lax.all_to_all(grad_perm, 'mp', split_axis=2, concat_axis=1, tiled=True)  6.88 us
  transfers between devices with their start and end apart: 10, of which 6 were waited for; matrix products, arithmetic and copies ran while one was open for 33% of the time, Pallas kernels for 0%

profile of v10, /device:TPU:6, one launch (start us, length us, event | category | flops | bytes accessed | tf_op | source)
XLA Modules:
  0.0 197.7 jit_solution(10861009130970120360)
XLA Ops:
  0.6 4.7 %copy.135 = bf16[768,2048]{0,1:T(8,128)(2,1)} copy(bf16[768,2048]{1,0:T(8,128)(2,1)} %param.6) | data formatting | bytes 6291456 | tf_op args[0]
  5.3 2.7 %fusion.8 = f32[768]{0:T(1024)S(1)} fusion(bf16[768,2048]{0,1:T(8,128)(2,1)} %copy.135), kind=kLoop, calls=%fused_computation.11 | loop fusion | flops 4717824 | bytes 3148800 | tf_op jit(solution)/shard_map/reduce_sum | solution.py:53
  10.8 2.7 %convert_bitcast_fusion.1 = bf16[768,16,128]{0,2,1:T(8,128)(2,1)} fusion(bf16[16,128,128]{2,1,0:T(8,128)(2,1)S(1)} %copy-done, bf16[768,2048]{1,0:T(8,128)(2,1)S(1)} %copy-done.4), kind=kOutput, calls=%fused_computation.42 | convolution fusion | flops 404226048 | bytes 6815744 | tf_op jit(solution)/shard_map/tkm,kcm->tkc/dot_general | solution.py:50
  14.9 5.3 %copy.147 = bf16[768,16,128]{0,1,2:T(8,128)(2,1)} copy(bf16[768,16,128]{0,2,1:T(8,128)(2,1)} %convert_bitcast_fusion.1) | data formatting | bytes 6291456 | tf_op jit(solution)/shard_map/optimization_barrier | solution.py:54
  20.2 6.9 %all-to-all-start = ((bf16[768,16,128]{0,1,2:T(8,128)(2,1)}), bf16[768,16,128]{0,1,2:T(8,128)(2,1)}, u32[]{:S(2)}, u32[]{:S(2)}) async-start(bf16[768,16,128]{0,1,2:T(8,128)(2,1)} %copy.147), calls=%async_computation | async-start | bytes 6291456 | tf_op jit(solution)/shard_map/all_to_all | solution.py:65
  27.0 2.7 %fusion.2 = bf16[768,2048]{0,1:T(8,128)(2,1)S(1)} fusion(bf16[768,2048]{0,1:T(8,128)(2,1)} %copy.135, f32[2048]{0:T(1024)S(1)} %copy-done.10, f32[768]{0:T(1024)S(1)} %add_rsqrt_fusion), kind=kLoop, calls=%fused_computation.5 | loop fusion | flops 6291456 | bytes 6302720 | tf_op jit(solution)/shard_map/convert_element_type | solution.py:56
  37.2 2.9 %collective-permute-start.4 = (bf16[768,16,32]{0,2,1:T(8,128)(2,1)}, bf16[768,16,32]{0,2,1:T(8,128)(2,1)}, u32[]{:S(2)}, u32[]{:S(2)}) collective-permute-start(bf16[768,16,32]{0,2,1:T(8,128)(2,1)} %get-tuple-element.46), channel_id=1, source_target_pairs={{0,3},{1,2},{2,1},{3,0},{4,7},{5,6},{6,5},{7,4},{8,11},{9,10},{10,... | collective-permute-start | bytes 2359304 | tf_op jit(solution)/shard_map/ppermute | solution.py:73
  40.0 22.6 %all-to-all-done = bf16[768,16,128]{0,1,2:T(8,128)(2,1)} async-done(((bf16[768,16,128]{0,1,2:T(8,128)(2,1)}), bf16[768,16,128]{0,1,2:T(8,128)(2,1)}, u32[]{:S(2)}, u32[]{:S(2)}) %all-to-all-start) | async-done | bytes 3145760 | tf_op jit(solution)/shard_map/all_to_all | solution.py:65
  62.6 2.9 %copy.148 = bf16[768,16,128]{0,2,1:T(8,128)(2,1)S(1)} copy(bf16[768,16,128]{0,1,2:T(8,128)(2,1)} %all-to-all-done) | data formatting | bytes 6291456 | tf_op jit(solution)/shard_map/all_to_all | solution.py:65
  66.4 3.6 %copy.149 = f32[768,4,16,32]{0,2,1,3:T(8,128)S(1)} copy(f32[768,4,16,32]{0,3,1,2:T(8,128)S(1)} %convert_bitcast_fusion) | data formatting | bytes 12582912 | tf_op jit(solution)/shard_map/convert_element_type | solution.py:81
  70.0 4.1 %fusion.17 = (bf16[768,16,128]{0,2,1:T(8,128)(2,1)S(1)}, f32[16,768,128]{1,2,0:T(8,128)}) fusion(f32[768,16,128]{0,2,1:T(8,128)S(1)} %bitcast.157, bf16[16,128,128]{1,2,0:T(8,128)(2,1)S(1)} %bitcast.161, bf16[768,16,128]{0,2,1:T(8,128)(2,1)S(1)} %bitcast.151), kind=kOutput, calls=%fused_computation.26 | convolution fusion | flops 412090368 | bytes 19398656 | tf_op jit(solution)/shard_map/tic,icj->tij/dot_general | solution.py:75
  76.2 4.9 %fusion.12 = bf16[768,16,128]{0,2,1:T(8,128)(2,1)S(1)} fusion(f32[768,16,128]{0,2,1:T(8,128)S(1)} %bitcast.158, f32[16,768,128]{1,2,0:T(8,128)} %get-tuple-element.58, bf16[16,128,128]{1,2,0:T(8,128)(2,1)S(1)} %bitcast.175, bf16[768,16,128]{0,2,1:T(8,128)(2,1)S(1)} %bitcast.153), kind=kOutput, calls=%fused_computation.18 | convolution fusion | flops 418381824 | bytes 19398656 | tf_op jit(solution)/shard_map/tic,icj->tij/dot_general | solution.py:74
  83.4 3.8 %add_bitcast_fusion = f32[768,16,128]{2,0,1:T(8,128)} fusion(f32[16,768,128]{2,1,0:T(8,128)S(1)} %fusion.34, bf16[768,16,128]{0,2,1:T(8,128)(2,1)S(1)} %fusion.12, bf16[16,128,128]{1,2,0:T(8,128)(2,1)S(1)} %bitcast.162), kind=kOutput, calls=%fused_computation.34 | convolution fusion | flops 404226048 | bytes 16252928 | tf_op jit(solution)/shard_map/tij,icj->tic/dot_general | solution.py:89
  87.2 8.7 %collective-permute-done.4 = bf16[768,16,32]{0,2,1:T(8,128)(2,1)} collective-permute-done((bf16[768,16,32]{0,2,1:T(8,128)(2,1)}, bf16[768,16,32]{0,2,1:T(8,128)(2,1)}, u32[]{:S(2)}, u32[]{:S(2)}) %collective-permute-start.4) | collective-permute-done | bytes 786464 | tf_op jit(solution)/shard_map/ppermute | solution.py:73
  106.7 9.6 %all-to-all-start.1 = ((f32[32,192,128]{2,1,0:T(8,128)}), f32[32,192,128]{2,1,0:T(8,128)}, u32[]{:S(2)}, u32[]{:S(2)}) async-start(f32[32,192,128]{2,1,0:T(8,128)} %bitcast.155), calls=%async_computation.1 | async-start | bytes 6291456 | tf_op jit(solution)/shard_map/all_to_all | solution.py:14
  116.3 6.6 %copy.172 = f32[768,16,128]{0,2,1:T(8,128)} copy(f32[768,16,128]{2,0,1:T(8,128)} %add_bitcast_fusion) | data formatting | bytes 12582912 | tf_op jit(solution)/shard_map/optimization_barrier | solution.py:92
  122.9 4.6 %fusion.9 = f32[768]{0:T(1024)S(1)} fusion(bf16[768,2048]{0,1:T(8,128)(2,1)} %copy.135, f32[768,16,128]{0,2,1:T(8,128)} %copy.172, f32[2048]{0:T(1024)S(1)} %copy-done.10), kind=kLoop, calls=%fused_computation.12 | loop fusion | flops 6290688 | bytes 9448448 | tf_op jit(solution)/shard_map/reduce_sum | solution.py:105
  128.8 2.9 %collective-permute-start.6 = (f32[768]{0:T(1024)S(1)}, f32[768]{0:T(1024)S(1)}, u32[]{:S(2)}, u32[]{:S(2)}) collective-permute-start(f32[768]{0:T(1024)S(1)} %add.80), channel_id=1, source_target_pairs={{0,2},{1,3},{2,0},{3,1},{4,6},{5,7},{6,4},{7,5},{8,10},{9,11},{10,... | collective-permute-start | bytes 9224 | tf_op jit(solution)/shard_map/ppermute | solution.py:32
  131.7 4.6 %copy.171 = bf16[768,2048]{0,1:T(8,128)(2,1)} copy(bf16[768,2048]{1,0:T(8,128)(2,1)} %param.11) | data formatting | bytes 6291456 | tf_op args[5]
  136.3 19.6 %collective-permute-done.6 = f32[768]{0:T(1024)S(1)} collective-permute-done((f32[768]{0:T(1024)S(1)}, f32[768]{0:T(1024)S(1)}, u32[]{:S(2)}, u32[]{:S(2)}) %collective-permute-start.6) | collective-permute-done | bytes 3104 | tf_op jit(solution)/shard_map/ppermute | solution.py:32
  155.9 6.8 %fusion.7 = bf16[768,2048]{0,1:T(8,128)(2,1)} fusion(bf16[768,2048]{0,1:T(8,128)(2,1)} %copy.135, bf16[768,2048]{0,1:T(8,128)(2,1)} %copy.171, f32[768,16,128]{0,2,1:T(8,128)} %copy.172, f32[768]{0:T(1024)S(1)} %add_multiply_fusion, f32[2048]{0:T(1024)S(1)} %copy-done.10, f32[768]{0:T(1024)S(1)} %add_rsqrt_fusion), kind=kLoop, calls=%fused_computation.10 | loop fusion | flops 15728640 | bytes 15742976 | tf_op jit(solution)/shard_map/convert_element_type | solution.py:109
  166.2 8.4 %all-to-all-start.2 = ((bf16[32,192,128]{2,1,0:T(8,128)(2,1)}), bf16[32,192,128]{2,1,0:T(8,128)(2,1)S(1)}, u32[]{:S(2)}, u32[]{:S(2)}) async-start(bf16[32,192,128]{2,1,0:T(8,128)(2,1)} %broadcast_in_dim.2), calls=%async_computation.2 | async-start | bytes 3145728 | tf_op jit(solution)/shard_map/all_to_all | solution.py:21
  174.7 4.7 %copy.173 = bf16[768,2048]{1,0:T(8,128)(2,1)} copy(bf16[768,2048]{0,1:T(8,128)(2,1)} %fusion.7) | data formatting | bytes 6291456
  179.4 16.6 %all-to-all-done.2 = bf16[32,192,128]{2,1,0:T(8,128)(2,1)S(1)} async-done(((bf16[32,192,128]{2,1,0:T(8,128)(2,1)}), bf16[32,192,128]{2,1,0:T(8,128)(2,1)S(1)}, u32[]{:S(2)}, u32[]{:S(2)}) %all-to-all-start.2) | async-done | bytes 1572896 | tf_op jit(solution)/shard_map/all_to_all | solution.py:21
  (62 shorter events, 33.9 us)
Async XLA Ops:
  0.6 10.2 %copy-start = (bf16[16,128,128]{2,1,0:T(8,128)(2,1)S(1)}, bf16[16,128,128]{2,1,0:T(8,128)(2,1)}, u32[]{:S(2)}) copy-start(bf16[16,128,128]{2,1,0:T(8,128)(2,1)} %param.10) | copy-start | bytes 1572868
  5.3 5.5 %copy-start.4 = (bf16[768,2048]{1,0:T(8,128)(2,1)S(1)}, bf16[768,2048]{1,0:T(8,128)(2,1)}, u32[]{:S(2)}) copy-start(bf16[768,2048]{1,0:T(8,128)(2,1)} %param.11) | copy-start | bytes 9437188
  8.1 1.2 collective-permute-start
  9.3 4.2 %copy-start.8 = (bf16[16,128,128]{2,1,0:T(8,128)(2,1)S(1)}, bf16[16,128,128]{2,1,0:T(8,128)(2,1)}, u32[]{:S(2)}) copy-start(bf16[16,128,128]{2,1,0:T(8,128)(2,1)} %param.9) | copy-start | bytes 1572868
  9.3 4.8 %copy-start.9 = (bf16[16,128,128]{2,1,0:T(8,128)(2,1)S(1)}, bf16[16,128,128]{2,1,0:T(8,128)(2,1)}, u32[]{:S(2)}) copy-start(bf16[16,128,128]{2,1,0:T(8,128)(2,1)} %param.8) | copy-start | bytes 1572868
  9.3 5.5 %collective-permute-start.1 = (f32[768]{0:T(1024)S(1)}, f32[768]{0:T(1024)S(1)}, u32[]{:S(2)}, u32[]{:S(2)}) collective-permute-start(f32[768]{0:T(1024)S(1)} %add.63), channel_id=1, source_target_pairs={{0,2},{1,3},{2,0},{3,1},{4,6},{5,7},{6,4},{7,5},{8,10},{9,11},{10,... | collective-permute-start | bytes 9224 | tf_op jit(solution)/shard_map/ppermute | solution.py:32
  20.2 6.9 %copy-start.10 = (f32[2048]{0:T(1024)S(1)}, f32[2048]{0:T(1024)}, u32[]{:S(2)}) copy-start(f32[2048]{0:T(1024)} %param.7) | copy-start | bytes 24580
  20.2 42.5 %all-to-all-start = ((bf16[768,16,128]{0,1,2:T(8,128)(2,1)}), bf16[768,16,128]{0,1,2:T(8,128)(2,1)}, u32[]{:S(2)}, u32[]{:S(2)}) async-start(bf16[768,16,128]{0,1,2:T(8,128)(2,1)} %copy.147), calls=%async_computation | async-start | bytes 6291456 | tf_op jit(solution)/shard_map/all_to_all | solution.py:65
  29.7 1.7 copy-start.2
  36.7 50.6 %collective-permute-start.2 = (bf16[768,16,32]{0,2,1:T(8,128)(2,1)}, bf16[768,16,32]{0,2,1:T(8,128)(2,1)}, u32[]{:S(2)}, u32[]{:S(2)}) collective-permute-start(bf16[768,16,32]{0,2,1:T(8,128)(2,1)} %get-tuple-element.48), channel_id=1, source_target_pairs={{0,1},{1,0},{2,3},{3,2},{4,5},{5,4},{6,7},{7,6},{8,9},{9,8},{10,11... | collective-permute-start | bytes 2359304 | tf_op jit(solution)/shard_map/ppermute | solution.py:73
  36.8 50.4 %collective-permute-start.3 = (bf16[768,16,32]{0,2,1:T(8,128)(2,1)}, bf16[768,16,32]{0,2,1:T(8,128)(2,1)}, u32[]{:S(2)}, u32[]{:S(2)}) collective-permute-start(bf16[768,16,32]{0,2,1:T(8,128)(2,1)} %get-tuple-element.47), channel_id=1, source_target_pairs={{0,2},{1,3},{2,0},{3,1},{4,6},{5,7},{6,4},{7,5},{8,10},{9,11},{10,... | collective-permute-start | bytes 2359304 | tf_op jit(solution)/shard_map/ppermute | solution.py:73
  37.2 58.7 %collective-permute-start.4 = (bf16[768,16,32]{0,2,1:T(8,128)(2,1)}, bf16[768,16,32]{0,2,1:T(8,128)(2,1)}, u32[]{:S(2)}, u32[]{:S(2)}) collective-permute-start(bf16[768,16,32]{0,2,1:T(8,128)(2,1)} %get-tuple-element.46), channel_id=1, source_target_pairs={{0,3},{1,2},{2,1},{3,0},{4,7},{5,6},{6,5},{7,4},{8,11},{9,10},{10,... | collective-permute-start | bytes 2359304 | tf_op jit(solution)/shard_map/ppermute | solution.py:73
  66.4 3.7 %copy-start.3 = (bf16[768,2048]{0,1:T(8,128)(2,1)S(1)}, bf16[768,2048]{0,1:T(8,128)(2,1)}, u32[]{:S(2)}) copy-start(bf16[768,2048]{0,1:T(8,128)(2,1)} %copy-done.2) | copy-start | bytes 9437188
  95.9 2.6 %copy-start.5 = (bf16[768,2048]{1,0:T(8,128)(2,1)S(1)}, bf16[768,2048]{1,0:T(8,128)(2,1)}, u32[]{:S(2)}) copy-start(bf16[768,2048]{1,0:T(8,128)(2,1)} %param.11) | copy-start | bytes 9437188
  101.9 2.9 %copy-start.6 = (f32[16,128,128]{2,1,0:T(8,128)S(1)}, f32[16,128,128]{2,1,0:T(8,128)}, u32[]{:S(2)}) copy-start(f32[16,128,128]{2,1,0:T(8,128)} %copy.188) | copy-start | bytes 3145732
  103.3 1.5 copy-start.7
  106.7 56.0 %all-to-all-start.1 = ((f32[32,192,128]{2,1,0:T(8,128)}), f32[32,192,128]{2,1,0:T(8,128)}, u32[]{:S(2)}, u32[]{:S(2)}) async-start(f32[32,192,128]{2,1,0:T(8,128)} %bitcast.155), calls=%async_computation.1 | async-start | bytes 6291456 | tf_op jit(solution)/shard_map/all_to_all | solution.py:14
  127.5 1.2 collective-permute-start.5
  128.8 27.1 %collective-permute-start.6 = (f32[768]{0:T(1024)S(1)}, f32[768]{0:T(1024)S(1)}, u32[]{:S(2)}, u32[]{:S(2)}) collective-permute-start(f32[768]{0:T(1024)S(1)} %add.80), channel_id=1, source_target_pairs={{0,2},{1,3},{2,0},{3,1},{4,6},{5,7},{6,4},{7,5},{8,10},{9,11},{10,... | collective-permute-start | bytes 9224 | tf_op jit(solution)/shard_map/ppermute | solution.py:32
  166.2 29.8 %all-to-all-start.2 = ((bf16[32,192,128]{2,1,0:T(8,128)(2,1)}), bf16[32,192,128]{2,1,0:T(8,128)(2,1)S(1)}, u32[]{:S(2)}, u32[]{:S(2)}) async-start(bf16[32,192,128]{2,1,0:T(8,128)(2,1)} %broadcast_in_dim.2), calls=%async_computation.2 | async-start | bytes 3145728 | tf_op jit(solution)/shard_map/all_to_all | solution.py:21
  174.6 23.1 %copy-start.1 = (bf16[16,128,128]{2,1,0:T(8,128)(2,1)S(1)}, bf16[16,128,128]{2,1,0:T(8,128)(2,1)}, u32[]{:S(2)}) copy-start(bf16[16,128,128]{2,1,0:T(8,128)(2,1)} %param.10) | copy-start | bytes 1572868

commit v11 on v10

--- a/solution.py
+++ b/solution.py
@@ -48,7 +48,7 @@
     xf = samples.astype(jnp.float32)
     cot_blocks = cotangent.reshape(rows, nlocal, BLOCK)
     grad_perm = jnp.einsum(
-        "tkm,kcm->tkc", cot_blocks, right_blocks, preferred_element_type=jnp.float32
+        "tkm,kcm->ckt", cot_blocks, right_blocks, preferred_element_type=jnp.float32
     ).astype(jnp.bfloat16)
     squares = mp_sum(jnp.sum(xf * xf, axis=1))
     grad_perm, squares = lax.optimization_barrier((grad_perm, squares))
@@ -62,7 +62,7 @@
     outgoing = (
         gated.reshape(rows, nlocal, 2, NBLK).transpose(0, 3, 1, 2).reshape(rows, NBLK, 2 * nlocal)
     )
-    returned = lax.all_to_all(grad_perm, "mp", split_axis=2, concat_axis=1, tiled=True)
+    returned = lax.all_to_all(grad_perm, "mp", split_axis=0, concat_axis=1, tiled=True).transpose(2, 1, 0)
     outgoing, xn_b = lax.optimization_barrier((outgoing, xn))
     me = lax.axis_index("mp")
     nmp = lax.axis_size("mp")

time: 199 us -> 199 us (level)
  local copies, waits for them, and re-layouts: 45.3 us -> 40.6 us
  waiting for transfers between devices: 69.8 us -> 72.7 us
    convert_element_type x1, local copies, waits for them, and re-layouts: 3.64 us -> 0.52 us  [body(): grad_gated = returned.reshape(rows, NBLK, nlocal, 2).transpose(0, 2, 3, 1...]
    ppermute x3, waiting for transfers between devices: 8.68 us -> 11.7 us  [body(): arrived.append(lax.ppermute(chunk, 'mp', [(i, i ^ d) for i in range(nmp)]))]
    all_to_all x1 -> x0, local copies, waits for them, and re-layouts: 2.89 us -> none  [body(): lax.all_to_all(grad_perm, 'mp', split_axis=2, concat_axis=1, tiled=True)]
  transfers between devices with their start and end apart: 10 -> 10, of which waited for: 6 -> 6; matrix products, arithmetic and copies ran while one was open for 33% -> 31% of each run, Pallas kernels for 0% -> 0%
where the time goes in v11:
time: 199 us; the launch traced here: 198 us
  waiting for transfers between devices  72.7 us (37%)
  local copies, waits for them, and re-layouts  40.6 us (20%)
  starting transfers between devices  32.9 us (17%)
  other arithmetic  27.3 us (14%)
  matrix products  23.3 us (12%)
    all_to_all x1, waiting for transfers between devices, body(): lax.all_to_all(grad_perm, 'mp', split_axis=0, concat_axis=1, tiled=True)  22.6 us
    ppermute x2, waiting for transfers between devices, mp_sum(): return v + lax.ppermute(v, 'mp', [(i, i ^ 2) for i in range(n)])  19.5 us
    unnamed x27, local copies, waits for them, and re-layouts  17.7 us
    all_to_all x1, waiting for transfers between devices, dp_all_gather(): lax.all_to_all(copies, 'dp', 0, 0, tiled=True).reshape(-1, BLOCK, BLOCK)  16.6 us
    ppermute x3, waiting for transfers between devices, body(): arrived.append(lax.ppermute(chunk, 'mp', [(i, i ^ d) for i in range(nmp)]))  11.7 us
    all_to_all x1, starting transfers between devices, dp_reduce_scatter(): got = lax.all_to_all(flat, 'dp', 0, 0, tiled=True)  9.62 us
    all_to_all x1, starting transfers between devices, dp_all_gather(): lax.all_to_all(copies, 'dp', 0, 0, tiled=True).reshape(-1, BLOCK, BLOCK)  8.47 us
    all_to_all x1, starting transfers between devices, body(): lax.all_to_all(grad_perm, 'mp', split_axis=0, concat_axis=1, tiled=True)  6.88 us
  transfers between devices with their start and end apart: 10, of which 6 were waited for; matrix products, arithmetic and copies ran while one was open for 31% of the time, Pallas kernels for 0%

profile of v11, /device:TPU:6, one launch (start us, length us, event | category | flops | bytes accessed | tf_op | source)
XLA Modules:
  0.0 197.7 jit_solution(6831470254080139028)
XLA Ops:
  0.6 4.7 %copy.135 = bf16[768,2048]{0,1:T(8,128)(2,1)} copy(bf16[768,2048]{1,0:T(8,128)(2,1)} %param.6) | data formatting | bytes 6291456 | tf_op args[0]
  5.3 2.7 %fusion.8 = f32[768]{0:T(1024)S(1)} fusion(bf16[768,2048]{0,1:T(8,128)(2,1)} %copy.135), kind=kLoop, calls=%fused_computation.11 | loop fusion | flops 4717824 | bytes 3148800 | tf_op jit(solution)/shard_map/reduce_sum | solution.py:53
  10.8 2.7 %convert_bitcast_fusion.1 = bf16[128,16,768]{2,0,1:T(8,128)(2,1)} fusion(bf16[16,128,128]{2,1,0:T(8,128)(2,1)S(1)} %copy-done, bf16[768,2048]{1,0:T(8,128)(2,1)S(1)} %copy-done.4), kind=kOutput, calls=%fused_computation.42 | convolution fusion | flops 404226048 | bytes 6815744 | tf_op jit(solution)/shard_map/tkm,kcm->ckt/dot_general | solution.py:50
  14.9 5.3 %copy.147 = bf16[128,16,768]{2,1,0:T(8,128)(2,1)} copy(bf16[128,16,768]{2,0,1:T(8,128)(2,1)} %convert_bitcast_fusion.1) | data formatting | bytes 6291456 | tf_op jit(solution)/shard_map/optimization_barrier | solution.py:54
  20.2 6.9 %all-to-all-start = ((bf16[128,16,768]{2,1,0:T(8,128)(2,1)}), bf16[128,16,768]{2,1,0:T(8,128)(2,1)}, u32[]{:S(2)}, u32[]{:S(2)}) async-start(bf16[128,16,768]{2,1,0:T(8,128)(2,1)} %copy.147), calls=%async_computation | async-start | bytes 6291456 | tf_op jit(solution)/shard_map/all_to_all | solution.py:65
  27.0 2.7 %fusion.2 = bf16[768,2048]{0,1:T(8,128)(2,1)S(1)} fusion(bf16[768,2048]{0,1:T(8,128)(2,1)} %copy.135, f32[2048]{0:T(1024)S(1)} %copy-done.10, f32[768]{0:T(1024)S(1)} %add_rsqrt_fusion), kind=kLoop, calls=%fused_computation.5 | loop fusion | flops 6291456 | bytes 6302720 | tf_op jit(solution)/shard_map/convert_element_type | solution.py:56
  37.2 2.9 %collective-permute-start.4 = (bf16[768,16,32]{0,2,1:T(8,128)(2,1)}, bf16[768,16,32]{0,2,1:T(8,128)(2,1)}, u32[]{:S(2)}, u32[]{:S(2)}) collective-permute-start(bf16[768,16,32]{0,2,1:T(8,128)(2,1)} %get-tuple-element.46), channel_id=1, source_target_pairs={{0,3},{1,2},{2,1},{3,0},{4,7},{5,6},{6,5},{7,4},{8,11},{9,10},{10,... | collective-permute-start | bytes 2359304 | tf_op jit(solution)/shard_map/ppermute | solution.py:73
  40.0 22.6 %all-to-all-done = bf16[128,16,768]{2,1,0:T(8,128)(2,1)} async-done(((bf16[128,16,768]{2,1,0:T(8,128)(2,1)}), bf16[128,16,768]{2,1,0:T(8,128)(2,1)}, u32[]{:S(2)}, u32[]{:S(2)}) %all-to-all-start) | async-done | bytes 3145760 | tf_op jit(solution)/shard_map/all_to_all | solution.py:65
  62.6 2.8 %convert_bitcast_fusion = f32[32,4,16,768]{3,2,0,1:T(8,128)S(1)} fusion(bf16[4,32,16,768]{3,2,1,0:T(8,128)(2,1)} %bitcast.53), kind=kLoop, calls=%fused_computation.13 | loop fusion | flops 1572864 | bytes 9437184 | tf_op jit(solution)/shard_map/convert_element_type | solution.py:81
  67.3 3.9 %fusion.17 = (bf16[768,16,128]{0,2,1:T(8,128)(2,1)S(1)}, f32[16,768,128]{1,2,0:T(8,128)}) fusion(f32[768,16,128]{0,2,1:T(8,128)S(1)} %bitcast.160, bf16[16,128,128]{1,2,0:T(8,128)(2,1)S(1)} %bitcast.164, bf16[768,16,128]{0,2,1:T(8,128)(2,1)S(1)} %bitcast.155), kind=kOutput, calls=%fused_computation.26 | convolution fusion | flops 412090368 | bytes 19398656 | tf_op jit(solution)/shard_map/tic,icj->tij/dot_general | solution.py:75
  73.2 4.9 %fusion.12 = bf16[768,16,128]{0,2,1:T(8,128)(2,1)S(1)} fusion(f32[768,16,128]{0,2,1:T(8,128)S(1)} %bitcast.161, f32[16,768,128]{1,2,0:T(8,128)} %get-tuple-element.58, bf16[16,128,128]{1,2,0:T(8,128)(2,1)S(1)} %bitcast.178, bf16[768,16,128]{0,2,1:T(8,128)(2,1)S(1)} %bitcast.157), kind=kOutput, calls=%fused_computation.18 | convolution fusion | flops 418381824 | bytes 19398656 | tf_op jit(solution)/shard_map/tic,icj->tij/dot_general | solution.py:74
  80.4 3.8 %add_bitcast_fusion = f32[768,16,128]{2,0,1:T(8,128)} fusion(f32[16,768,128]{2,1,0:T(8,128)S(1)} %fusion.34, bf16[768,16,128]{0,2,1:T(8,128)(2,1)S(1)} %fusion.12, bf16[16,128,128]{1,2,0:T(8,128)(2,1)S(1)} %bitcast.165), kind=kOutput, calls=%fused_computation.34 | convolution fusion | flops 404226048 | bytes 16252928 | tf_op jit(solution)/shard_map/tij,icj->tic/dot_general | solution.py:89
  84.2 11.7 %collective-permute-done.4 = bf16[768,16,32]{0,2,1:T(8,128)(2,1)} collective-permute-done((bf16[768,16,32]{0,2,1:T(8,128)(2,1)}, bf16[768,16,32]{0,2,1:T(8,128)(2,1)}, u32[]{:S(2)}, u32[]{:S(2)}) %collective-permute-start.4) | collective-permute-done | bytes 786464 | tf_op jit(solution)/shard_map/ppermute | solution.py:73
  106.7 9.6 %all-to-all-start.1 = ((f32[32,192,128]{2,1,0:T(8,128)}), f32[32,192,128]{2,1,0:T(8,128)}, u32[]{:S(2)}, u32[]{:S(2)}) async-start(f32[32,192,128]{2,1,0:T(8,128)} %bitcast.159), calls=%async_computation.1 | async-start | bytes 6291456 | tf_op jit(solution)/shard_map/all_to_all | solution.py:14
  116.3 6.6 %copy.171 = f32[768,16,128]{0,2,1:T(8,128)} copy(f32[768,16,128]{2,0,1:T(8,128)} %add_bitcast_fusion) | data formatting | bytes 12582912 | tf_op jit(solution)/shard_map/optimization_barrier | solution.py:92
  122.9 4.6 %fusion.9 = f32[768]{0:T(1024)S(1)} fusion(bf16[768,2048]{0,1:T(8,128)(2,1)} %copy.135, f32[768,16,128]{0,2,1:T(8,128)} %copy.171, f32[2048]{0:T(1024)S(1)} %copy-done.10), kind=kLoop, calls=%fused_computation.12 | loop fusion | flops 6290688 | bytes 9448448 | tf_op jit(solution)/shard_map/reduce_sum | solution.py:105
  128.8 2.9 %collective-permute-start.6 = (f32[768]{0:T(1024)S(1)}, f32[768]{0:T(1024)S(1)}, u32[]{:S(2)}, u32[]{:S(2)}) collective-permute-start(f32[768]{0:T(1024)S(1)} %add.80), channel_id=1, source_target_pairs={{0,2},{1,3},{2,0},{3,1},{4,6},{5,7},{6,4},{7,5},{8,10},{9,11},{10,... | collective-permute-start | bytes 9224 | tf_op jit(solution)/shard_map/ppermute | solution.py:32
  131.7 4.6 %copy.170 = bf16[768,2048]{0,1:T(8,128)(2,1)} copy(bf16[768,2048]{1,0:T(8,128)(2,1)} %param.11) | data formatting | bytes 6291456 | tf_op args[5]
  136.3 19.5 %collective-permute-done.6 = f32[768]{0:T(1024)S(1)} collective-permute-done((f32[768]{0:T(1024)S(1)}, f32[768]{0:T(1024)S(1)}, u32[]{:S(2)}, u32[]{:S(2)}) %collective-permute-start.6) | collective-permute-done | bytes 3104 | tf_op jit(solution)/shard_map/ppermute | solution.py:32
  155.8 6.8 %fusion.7 = bf16[768,2048]{0,1:T(8,128)(2,1)} fusion(bf16[768,2048]{0,1:T(8,128)(2,1)} %copy.135, bf16[768,2048]{0,1:T(8,128)(2,1)} %copy.170, f32[768,16,128]{0,2,1:T(8,128)} %copy.171, f32[768]{0:T(1024)S(1)} %add_multiply_fusion, f32[2048]{0:T(1024)S(1)} %copy-done.10, f32[768]{0:T(1024)S(1)} %add_rsqrt_fusion), kind=kLoop, calls=%fused_computation.10 | loop fusion | flops 15728640 | bytes 15742976 | tf_op jit(solution)/shard_map/convert_element_type | solution.py:109
  162.6 2.0 %reduce_sum.28 = bf16[192,128]{1,0:T(8,128)(2,1)S(1)} reduce(f32[32,192,128]{2,1,0:T(8,128)} %all-to-all-done.1, f32[]{:T(128)} %constant.14.clone.1), dimensions={0}, to_apply=%region_1.2 | reduce | flops 761856 | bytes 3194884 | tf_op jit(solution)/shard_map/reduce_sum | solution.py:15
  166.2 8.5 %all-to-all-start.2 = ((bf16[32,192,128]{2,1,0:T(8,128)(2,1)}), bf16[32,192,128]{2,1,0:T(8,128)(2,1)S(1)}, u32[]{:S(2)}, u32[]{:S(2)}) async-start(bf16[32,192,128]{2,1,0:T(8,128)(2,1)} %broadcast_in_dim.2), calls=%async_computation.2 | async-start | bytes 3145728 | tf_op jit(solution)/shard_map/all_to_all | solution.py:21
  174.7 4.7 %copy.172 = bf16[768,2048]{1,0:T(8,128)(2,1)} copy(bf16[768,2048]{0,1:T(8,128)(2,1)} %fusion.7) | data formatting | bytes 6291456
  179.4 16.6 %all-to-all-done.2 = bf16[32,192,128]{2,1,0:T(8,128)(2,1)S(1)} async-done(((bf16[32,192,128]{2,1,0:T(8,128)(2,1)}), bf16[32,192,128]{2,1,0:T(8,128)(2,1)S(1)}, u32[]{:S(2)}, u32[]{:S(2)}) %all-to-all-start.2) | async-done | bytes 1572896 | tf_op jit(solution)/shard_map/all_to_all | solution.py:21
  (61 shorter events, 32.9 us)
Async XLA Ops:
  0.6 10.2 %copy-start = (bf16[16,128,128]{2,1,0:T(8,128)(2,1)S(1)}, bf16[16,128,128]{2,1,0:T(8,128)(2,1)}, u32[]{:S(2)}) copy-start(bf16[16,128,128]{2,1,0:T(8,128)(2,1)} %param.10) | copy-start | bytes 1572868
  5.3 5.5 %copy-start.4 = (bf16[768,2048]{1,0:T(8,128)(2,1)S(1)}, bf16[768,2048]{1,0:T(8,128)(2,1)}, u32[]{:S(2)}) copy-start(bf16[768,2048]{1,0:T(8,128)(2,1)} %param.11) | copy-start | bytes 9437188
  8.1 1.2 collective-permute-start
  9.3 4.2 %copy-start.8 = (bf16[16,128,128]{2,1,0:T(8,128)(2,1)S(1)}, bf16[16,128,128]{2,1,0:T(8,128)(2,1)}, u32[]{:S(2)}) copy-start(bf16[16,128,128]{2,1,0:T(8,128)(2,1)} %param.9) | copy-start | bytes 1572868
  9.3 4.8 %copy-start.9 = (bf16[16,128,128]{2,1,0:T(8,128)(2,1)S(1)}, bf16[16,128,128]{2,1,0:T(8,128)(2,1)}, u32[]{:S(2)}) copy-start(bf16[16,128,128]{2,1,0:T(8,128)(2,1)} %param.8) | copy-start | bytes 1572868
  9.3 5.5 %collective-permute-start.1 = (f32[768]{0:T(1024)S(1)}, f32[768]{0:T(1024)S(1)}, u32[]{:S(2)}, u32[]{:S(2)}) collective-permute-start(f32[768]{0:T(1024)S(1)} %add.63), channel_id=1, source_target_pairs={{0,2},{1,3},{2,0},{3,1},{4,6},{5,7},{6,4},{7,5},{8,10},{9,11},{10,... | collective-permute-start | bytes 9224 | tf_op jit(solution)/shard_map/ppermute | solution.py:32
  20.2 6.9 %copy-start.10 = (f32[2048]{0:T(1024)S(1)}, f32[2048]{0:T(1024)}, u32[]{:S(2)}) copy-start(f32[2048]{0:T(1024)} %param.7) | copy-start | bytes 24580
  20.2 42.5 %all-to-all-start = ((bf16[128,16,768]{2,1,0:T(8,128)(2,1)}), bf16[128,16,768]{2,1,0:T(8,128)(2,1)}, u32[]{:S(2)}, u32[]{:S(2)}) async-start(bf16[128,16,768]{2,1,0:T(8,128)(2,1)} %copy.147), calls=%async_computation | async-start | bytes 6291456 | tf_op jit(solution)/shard_map/all_to_all | solution.py:65
  29.7 1.7 copy-start.2
  36.7 47.5 %collective-permute-start.2 = (bf16[768,16,32]{0,2,1:T(8,128)(2,1)}, bf16[768,16,32]{0,2,1:T(8,128)(2,1)}, u32[]{:S(2)}, u32[]{:S(2)}) collective-permute-start(bf16[768,16,32]{0,2,1:T(8,128)(2,1)} %get-tuple-element.48), channel_id=1, source_target_pairs={{0,1},{1,0},{2,3},{3,2},{4,5},{5,4},{6,7},{7,6},{8,9},{9,8},{10,11... | collective-permute-start | bytes 2359304 | tf_op jit(solution)/shard_map/ppermute | solution.py:73
  36.8 47.4 %collective-permute-start.3 = (bf16[768,16,32]{0,2,1:T(8,128)(2,1)}, bf16[768,16,32]{0,2,1:T(8,128)(2,1)}, u32[]{:S(2)}, u32[]{:S(2)}) collective-permute-start(bf16[768,16,32]{0,2,1:T(8,128)(2,1)} %get-tuple-element.47), channel_id=1, source_target_pairs={{0,2},{1,3},{2,0},{3,1},{4,6},{5,7},{6,4},{7,5},{8,10},{9,11},{10,... | collective-permute-start | bytes 2359304 | tf_op jit(solution)/shard_map/ppermute | solution.py:73
  37.2 58.7 %collective-permute-start.4 = (bf16[768,16,32]{0,2,1:T(8,128)(2,1)}, bf16[768,16,32]{0,2,1:T(8,128)(2,1)}, u32[]{:S(2)}, u32[]{:S(2)}) collective-permute-start(bf16[768,16,32]{0,2,1:T(8,128)(2,1)} %get-tuple-element.46), channel_id=1, source_target_pairs={{0,3},{1,2},{2,1},{3,0},{4,7},{5,6},{6,5},{7,4},{8,11},{9,10},{10,... | collective-permute-start | bytes 2359304 | tf_op jit(solution)/shard_map/ppermute | solution.py:73
  65.4 1.9 copy-start.3
  95.9 2.6 %copy-start.5 = (bf16[768,2048]{1,0:T(8,128)(2,1)S(1)}, bf16[768,2048]{1,0:T(8,128)(2,1)}, u32[]{:S(2)}) copy-start(bf16[768,2048]{1,0:T(8,128)(2,1)} %param.11) | copy-start | bytes 9437188
  101.9 2.9 %copy-start.6 = (f32[16,128,128]{2,1,0:T(8,128)S(1)}, f32[16,128,128]{2,1,0:T(8,128)}, u32[]{:S(2)}) copy-start(f32[16,128,128]{2,1,0:T(8,128)} %copy.187) | copy-start | bytes 3145732
  103.3 1.5 copy-start.7
  106.7 55.9 %all-to-all-start.1 = ((f32[32,192,128]{2,1,0:T(8,128)}), f32[32,192,128]{2,1,0:T(8,128)}, u32[]{:S(2)}, u32[]{:S(2)}) async-start(f32[32,192,128]{2,1,0:T(8,128)} %bitcast.159), calls=%async_computation.1 | async-start | bytes 6291456 | tf_op jit(solution)/shard_map/all_to_all | solution.py:14
  127.5 1.2 collective-permute-start.5
  128.8 27.1 %collective-permute-start.6 = (f32[768]{0:T(1024)S(1)}, f32[768]{0:T(1024)S(1)}, u32[]{:S(2)}, u32[]{:S(2)}) collective-permute-start(f32[768]{0:T(1024)S(1)} %add.80), channel_id=1, source_target_pairs={{0,2},{1,3},{2,0},{3,1},{4,6},{5,7},{6,4},{7,5},{8,10},{9,11},{10,... | collective-permute-start | bytes 9224 | tf_op jit(solution)/shard_map/ppermute | solution.py:32
  166.2 29.8 %all-to-all-start.2 = ((bf16[32,192,128]{2,1,0:T(8,128)(2,1)}), bf16[32,192,128]{2,1,0:T(8,128)(2,1)S(1)}, u32[]{:S(2)}, u32[]{:S(2)}) async-start(bf16[32,192,128]{2,1,0:T(8,128)(2,1)} %broadcast_in_dim.2), calls=%async_computation.2 | async-start | bytes 3145728 | tf_op jit(solution)/shard_map/all_to_all | solution.py:21
  174.6 23.1 %copy-start.1 = (bf16[16,128,128]{2,1,0:T(8,128)(2,1)S(1)}, bf16[16,128,128]{2,1,0:T(8,128)(2,1)}, u32[]{:S(2)}) copy-start(bf16[16,128,128]{2,1,0:T(8,128)(2,1)} %param.10) | copy-start | bytes 1572868
